TPU v7x, 256 devices: a whole 4x4x8 slice. The times are simulated.
256 devices in a mesh: band: 16 (over y, z_lo), bin: 16 (over z_hi, x, core).
Axes of the slice: x: 4, y: 4, z: 8 (z_hi: 2, z_lo: 4; z = z_hi * 4 + z_lo), core: 2. Of those that a mesh axis runs over, the one named last changes fastest.
Arguments:
- spectrum: float32 [131072, 1152], P('band', 'bin'), may hold values from -6 to 6
- velocity: float32 [16384, 128], P(('band', 'bin')), may hold values from -5 to 5
- source_a: bfloat16 [1152, 1152], replicated, may hold values from -0.1875 to 0.1875
- source_b: bfloat16 [1152, 1152], replicated, may hold values from -0.1875 to 0.1875
- stokes_kernel: bfloat16 [1152, 128], replicated, may hold values from -0.1875 to 0.1875
- group_speed: float32 [1152], replicated, may hold values from 0.4 to 0.6
- column_map: int32 [131072], replicated, may hold values from 0 to 16383, as said below
- land_mask: int32 [131072], replicated, may hold values 0 or 1
Outputs:
- spectrum_out: float32 [131072, 1152], P('band', 'bin')
- velocity_out: float32 [16384, 128], P(('band', 'bin'))
Inputs may be any that keep to these rules, and one draw needn't show every extreme that they name: `column_map`: the cells of the k-th aligned block of 512 cells belong to the 64 columns from k * 64 + 64 // 2 onward, counted modulo 16384, in rising order along the block; every column owns from 1 to 16 cells, and in every block some column owns exactly 16.
All inputs are finite; a program needn't handle non-finite values.
Results may differ from a plain program's by a relative error of at most 0.002.
Values may be sent and summed in bfloat16 or wider, within the bound.
No kernel may reach another device: no remote copies, remote signals or barrier semaphores. Data moves between devices by JAX's collectives and lax.ppermute only.
A program may use at most 64 MiB of HBM per device.

v0:
```python
import math

import jax
import jax.numpy as jnp
from jax import lax
from jax.sharding import PartitionSpec as P

NDIR = 36
LEVELS = 64
STEPS = 2


def shifted(block, axis, distance):
    devices = range(lax.axis_size(axis))
    route = [((i - distance) % len(devices), i) for i in devices]
    return lax.ppermute(block, axis, route)


def padded_2(block, sides, width):
    for axis, dim in sides:
        count = lax.axis_size(axis)
        forward = [(i, i + 1) for i in range(count - 1)]
        backward = [(target, source) for source, target in forward]
        low = lax.ppermute(
            lax.slice_in_dim(block, block.shape[dim] - width, None, axis=dim), axis, forward
        )
        high = lax.ppermute(lax.slice_in_dim(block, 0, width, axis=dim), axis, backward)
        block = jnp.concatenate([low, block, high], axis=dim)
    return block


def from_behind(shard, axis, by):
    peers = lax.axis_size(axis)
    pairs = [(i, i + by) for i in range(peers) if 0 <= i + by < peers]
    return lax.ppermute(shard, axis, pairs)


def bin_angles(first, count):
    index = first + jnp.arange(count)
    angle = 2.0 * math.pi / NDIR * (index % NDIR).astype(jnp.float32)
    return (jnp.cos(angle), jnp.sin(angle))


def local_currents(velocity, local_map, device, columns, total):
    surface = jnp.stack([velocity[:, 0], velocity[:, LEVELS]])
    after = shifted(surface, ("band", "bin"), -1)
    table = jnp.concatenate([surface, after], 1)
    where = jnp.mod(local_map - device * columns, total)
    return jnp.take(table, where, axis=1)


def propagate(field, prev, current, speed_bins, cos_b, sin_b, mask_cells):
    speed = speed_bins[None, :] + 0.25 * (
        jnp.tanh(current[0])[:, None] * cos_b[None, :]
        + jnp.tanh(current[1])[:, None] * sin_b[None, :]
    )
    behind = jnp.concatenate([prev, field[:-1]], 0)
    return mask_cells[:, None] * (field - speed * (field - behind))


def sources(rounded, mask_cells, source_a, source_b, stokes_kernel):
    gain = jnp.dot(rounded, source_a, preferred_element_type=jnp.float32)
    other = jnp.dot(rounded, source_b, preferred_element_type=jnp.float32)
    increment = (0.1 * mask_cells[:, None] * (gain + 0.5 * gain * other)).astype(jnp.bfloat16)
    stokes = jnp.dot(rounded, stokes_kernel, preferred_element_type=jnp.float32)
    return (increment, stokes)


def owned_counts(column_map, device, cell_dev, columns):
    extended = jnp.concatenate([column_map[-cell_dev:], column_map])
    window = lax.dynamic_slice_in_dim(extended, device * cell_dev, 2 * cell_dev)
    owned = device * columns + jnp.arange(columns)
    return jnp.sum((window[None, :] == owned[:, None]).astype(jnp.float32), axis=1)


def window_sums(stokes, local_map, base, columns, total):
    relative = jnp.mod(local_map - base, total)
    onehot = (relative[None, :] == jnp.arange(columns)[:, None]).astype(jnp.float32)
    return jnp.dot(onehot, stokes, precision=lax.Precision.HIGHEST)


def column_forcing(stokes, local_map, counts, base, total):
    columns = counts.shape[0]
    partial_sums = window_sums(stokes, local_map, base, columns, total)
    half = columns // 2
    received = shifted(partial_sums[half:], ("band", "bin"), 1)
    summed = jnp.concatenate([received, partial_sums[:half]], 0)
    return summed / counts[:, None]


def ocean_step(velocity, forcing):
    columns = velocity.shape[0]
    padded = padded_2(velocity, ((("band", "bin"), 0),), 1)
    lap_h = padded[2:] + padded[:-2] - 2.0 * velocity
    cube = velocity.reshape(columns, 2, LEVELS)
    edge = jnp.pad(cube, ((0, 0), (0, 0), (1, 1)), mode="edge")
    lap_v = (edge[:, :, 2:] + edge[:, :, :-2] - 2.0 * cube).reshape(columns, 2 * LEVELS)
    return velocity + 0.2 * lap_h + 0.2 * lap_v + 1.5 * forcing - 0.05 * velocity


def per_device(
    spectrum, velocity, source_a, source_b, stokes_kernel, group_speed, column_map, land_mask
):
    bin_count = lax.axis_size("bin")
    device_count = lax.axis_size("band") * bin_count
    band_pos = lax.axis_index("band")
    bin_pos = lax.axis_index("bin")
    device = band_pos * bin_count + bin_pos
    band_rows = spectrum.shape[0]
    cell_dev = band_rows // bin_count
    columns = velocity.shape[0]
    total = columns * device_count
    base = device * columns + columns // 2
    counts = owned_counts(column_map, device, cell_dev, columns)
    mask_all = land_mask.astype(jnp.float32)
    cell_first = device * cell_dev
    local_map = lax.dynamic_slice_in_dim(column_map, cell_first, cell_dev)
    local_mask = lax.dynamic_slice_in_dim(mask_all, cell_first, cell_dev)
    band_first = band_pos * band_rows
    band_mask = lax.dynamic_slice_in_dim(mask_all, band_first, band_rows)
    width = spectrum.shape[1]
    bin_first = bin_pos * width
    cos_part, sin_part = bin_angles(bin_first, width)
    speed_part = lax.dynamic_slice_in_dim(group_speed, bin_first, width)
    field = spectrum
    for step in range(STEPS):
        mine = local_currents(velocity, local_map, device, columns, total)
        current = lax.all_gather(mine, "bin", axis=1, tiled=True)
        prev = from_behind(field[-1:], "band", 1)
        moved = propagate(field, prev, current, speed_part, cos_part, sin_part, band_mask)
        rounded = lax.all_to_all(
            moved.astype(jnp.bfloat16), "bin", split_axis=0, concat_axis=1, tiled=True
        )
        increment, stokes = sources(rounded, local_mask, source_a, source_b, stokes_kernel)
        returned = lax.all_to_all(increment, "bin", split_axis=1, concat_axis=0, tiled=True)
        field = moved + returned.astype(jnp.float32)
        velocity = ocean_step(velocity, column_forcing(stokes, local_map, counts, base, total))
    return (field, velocity)


def solution(mesh):
    in_specs = (P("band", "bin"), P(("band", "bin"), None), P(), P(), P(), P(), P(), P())
    out_specs = (P("band", "bin"), P(("band", "bin"), None))
    return jax.shard_map(
        per_device, mesh=mesh, in_specs=in_specs, out_specs=out_specs, check_vma=False
    )
```

profile of v0, /device:TPU:80, one launch (start us, length us, event | category | flops | bytes accessed | tf_op | source)
XLA Modules:
  0.0 344.1 jit_solution(14762460017091194551)
XLA Ops:
  0.6 1.1 slice_reduce_fusion.3
  1.8 6.6 %collective-permute-start = (f32[2,64]{1,0:T(2,128)S(1)}, f32[2,64]{1,0:T(2,128)S(1)}, u32[]{:S(2)}, u32[]{:S(2)}) collective-permute-start(f32[2,64]{1,0:T(2,128)S(1)} %pad_maximum_fusion.8), channel_id=1, source_target_pairs={{1,0},{2,1},{3,2},{4,3},{5,4},{6,5},{7,6},{8,7},{9,8},{10,9},{11,1... | collective-permute-start | bytes 1544 | tf_op jit(solution)/shard_map/ppermute | solution.py:16
  8.4 1.5 slice.113
  9.9 2.9 collective-permute-start.1
  12.8 0.6 fusion.47
  13.4 0.8 compare_and_fusion
  14.2 1.1 convert_element_type.48
  15.3 1.3 dynamic_slice.16
  16.8 1.0 gather_fusion
  17.9 0.1 select_bitcast_fusion.1
  18.0 54.9 %all_gather.6 = f32[2,8192]{0,1:T(8,128)S(1)} all-gather(f32[2,512]{0,1:T(8,128)S(1)} %select_bitcast_fusion.1), channel_id=1, replica_groups=mesh['band'=16,'bin'=16] {'bin'}, dimensions={1}, use_global_device_ids=true | all-gather | bytes 69632 | tf_op jit(solution)/shard_map/all_gather | solution.py:128
  72.9 3.3 fusion.3
  76.3 3.1 fusion.51
  79.4 1.1 copy.55
  80.5 6.6 %all-to-all-start = ((bf16[16,512,72]{1,2,0:T(8,128)(2,1)}), bf16[16,512,72]{1,2,0:T(8,128)(2,1)}, u32[]{:S(2)}, u32[]{:S(2)}) async-start(bf16[16,512,72]{1,2,0:T(8,128)(2,1)} %bitcast.57), calls=%async_computation | async-start | bytes 2359296 | tf_op jit(solution)/shard_map/all_to_all | solution.py:131
  87.1 0.6 fusion.59
  87.7 9.8 %collective-permute-start.2 = (f32[1,128]{1,0:T(1,128)}, f32[1,128]{1,0:T(1,128)}, u32[]{:S(2)}, u32[]{:S(2)}) collective-permute-start(f32[1,128]{1,0:T(1,128)} %get-tuple-element.29), channel_id=1, source_target_pairs={{1,0},{2,1},{3,2},{4,3},{5,4},{6,5},{7,6},{8,7},{9,8},{10,9},{11,1... | collective-permute-start | bytes 1544 | tf_op jit(solution)/shard_map/ppermute | solution.py:27
  97.5 1.9 collective-permute-start.3
  99.6 0.8 fusion.53
  100.4 0.8 fusion.42
  101.2 8.0 %all-to-all-done = bf16[16,512,72]{1,2,0:T(8,128)(2,1)} async-done(((bf16[16,512,72]{1,2,0:T(8,128)(2,1)}), bf16[16,512,72]{1,2,0:T(8,128)(2,1)}, u32[]{:S(2)}, u32[]{:S(2)}) %all-to-all-start) | async-done | bytes 1179680 | tf_op jit(solution)/shard_map/all_to_all | solution.py:131
  109.3 3.3 fusion.60
  112.6 4.4 %fusion.9 = bf16[512,1152]{1,0:T(8,128)(2,1)} fusion(f32[512,1152]{1,0:T(8,128)S(1)} %fusion.60, bf16[512,1152]{0,1:T(8,128)(2,1)} %bitcast.2, bf16[1152,1152]{1,0:T(8,128)(2,1)S(1)} %copy-done.3, f32[512]{0:T(512)S(1)} %dynamic-slice_multiply_fusion), kind=kOutput, calls=%fused_computation.17 | convolution fusion | flops 1361903616 | bytes 7374848 | tf_op jit(solution)/shard_map/dot_general | solution.py:63
  116.9 2.4 copy.42
  119.4 4.5 %all-to-all-start.1 = ((bf16[512,16,72]{0,2,1:T(8,128)(2,1)}), bf16[512,16,72]{0,2,1:T(8,128)(2,1)}, u32[]{:S(2)}, u32[]{:S(2)}) async-start(bf16[512,16,72]{0,2,1:T(8,128)(2,1)} %bitcast.55), calls=%async_computation.1 | async-start | bytes 2359296 | tf_op jit(solution)/shard_map/all_to_all | solution.py:135
  124.1 0.3 fusion.23
  124.3 1.8 fusion.61
  126.1 0.2 fusion.17
  126.4 0.5 collective-permute-start.4
  126.9 0.2 convert_reduce_fusion
  127.2 41.5 %collective-permute-done.4 = f32[32,128]{1,0:T(8,128)S(1)} collective-permute-done((f32[32,128]{1,0:T(8,128)S(1)}, f32[32,128]{1,0:T(8,128)S(1)}, u32[]{:S(2)}, u32[]{:S(2)}) %collective-permute-start.4) | collective-permute-done | bytes 16416 | tf_op jit(solution)/shard_map/ppermute | solution.py:16
  168.7 0.8 fusion.39
  169.5 0.2 slice_reduce_fusion.1
  169.8 1.3 collective-permute-done.5
  171.2 1.0 gather_fusion.1
  172.4 65.2 %all_gather.7 = f32[2,8192]{0,1:T(8,128)} all-gather(f32[2,512]{0,1:T(8,128)S(1)} %select_bitcast_fusion), channel_id=1, replica_groups=mesh['band'=16,'bin'=16] {'bin'}, dimensions={1}, use_global_device_ids=true | all-gather | bytes 69632 | tf_op jit(solution)/shard_map/all_gather | solution.py:128
  237.6 1.6 convert_bitcast_fusion.1
  239.3 0.2 copy.50
  239.5 1.4 copy-done.6
  240.9 0.2 add.149
  241.2 4.9 %collective-permute-start.6 = (f32[1,72]{0,1:T(8,128)S(1)}, f32[1,72]{0,1:T(8,128)S(1)}, u32[]{:S(2)}, u32[]{:S(2)}) collective-permute-start(f32[1,72]{0,1:T(8,128)S(1)} %slice.156), channel_id=1, source_target_pairs={{0,16},{16,32},{32,48},{48,64},{64,80},{80,96},{96,112},{112,128},... | collective-permute-start | bytes 872 | tf_op jit(solution)/shard_map/ppermute | solution.py:35
  246.2 3.3 fusion.1
  249.5 5.1 %collective-permute-done.6 = f32[1,72]{0,1:T(8,128)S(1)} collective-permute-done((f32[1,72]{0,1:T(8,128)S(1)}, f32[1,72]{0,1:T(8,128)S(1)}, u32[]{:S(2)}, u32[]{:S(2)}) %collective-permute-start.6) | collective-permute-done | bytes 320 | tf_op jit(solution)/shard_map/ppermute | solution.py:35
  254.6 2.3 fusion.49
  257.0 35.4 %all_to_all.64 = bf16[16,512,72]{1,2,0:T(8,128)(2,1)S(1)} all-to-all(bf16[16,512,72]{1,2,0:T(8,128)(2,1)S(1)} %bitcast.58), channel_id=1, replica_groups=mesh['band'=16,'bin'=16] {'bin'}, dimensions={0} | all-to-all | bytes 2359296 | tf_op jit(solution)/shard_map/all_to_all | solution.py:131
  292.5 1.9 fusion.62
  294.4 0.3 copy-done.4
  294.7 3.1 fusion.8
  297.8 2.4 copy.46
  300.2 4.4 %all-to-all-start.3 = ((bf16[512,16,72]{0,2,1:T(8,128)(2,1)}), bf16[512,16,72]{0,2,1:T(8,128)(2,1)}, u32[]{:S(2)}, u32[]{:S(2)}) async-start(bf16[512,16,72]{0,2,1:T(8,128)(2,1)} %bitcast.56), calls=%async_computation.3 | async-start | bytes 2359296 | tf_op jit(solution)/shard_map/all_to_all | solution.py:135
  304.7 7.7 %collective-permute-start.7 = (f32[1,128]{1,0:T(1,128)S(1)}, f32[1,128]{1,0:T(1,128)S(1)}, u32[]{:S(2)}, u32[]{:S(2)}) collective-permute-start(f32[1,128]{1,0:T(1,128)S(1)} %get-tuple-element.25), channel_id=1, source_target_pairs={{1,0},{2,1},{3,2},{4,3},{5,4},{6,5},{7,6},{8,7},{9,8},{10,9},{11,1... | collective-permute-start | bytes 1544 | tf_op jit(solution)/shard_map/ppermute | solution.py:27
  312.4 1.9 collective-permute-start.8
  314.5 1.8 fusion.63
  316.3 0.2 fusion.16
  316.6 0.3 fusion.20
  317.0 13.9 %collective-permute-done.7 = f32[1,128]{1,0:T(1,128)S(1)} collective-permute-done((f32[1,128]{1,0:T(1,128)S(1)}, f32[1,128]{1,0:T(1,128)S(1)}, u32[]{:S(2)}, u32[]{:S(2)}) %collective-permute-start.7) | collective-permute-done | bytes 544 | tf_op jit(solution)/shard_map/ppermute | solution.py:27
  330.9 3.5 %collective-permute-done.8 = f32[1,128]{1,0:T(1,128)S(1)} collective-permute-done((f32[1,128]{1,0:T(1,128)S(1)}, f32[1,128]{1,0:T(1,128)S(1)}, u32[]{:S(2)}, u32[]{:S(2)}) %collective-permute-start.8) | collective-permute-done | bytes 544 | tf_op jit(solution)/shard_map/ppermute | solution.py:24
  334.4 0.3 collective-permute-done.9
  334.6 0.7 fusion.32
  335.3 3.9 %all-to-all-done.3 = bf16[512,16,72]{0,2,1:T(8,128)(2,1)} async-done(((bf16[512,16,72]{0,2,1:T(8,128)(2,1)}), bf16[512,16,72]{0,2,1:T(8,128)(2,1)}, u32[]{:S(2)}, u32[]{:S(2)}) %all-to-all-start.3) | async-done | bytes 1179680 | tf_op jit(solution)/shard_map/all_to_all | solution.py:135
  339.2 1.6 convert_bitcast_fusion
  340.8 0.2 copy.51
  341.0 1.4 copy-done.7
  342.5 1.6 add.163
  (60 shorter events, 1.7 us)
Async XLA Ops:
  0.6 108.6 %copy-start = (bf16[1152,1152]{1,0:T(8,128)(2,1)S(1)}, bf16[1152,1152]{1,0:T(8,128)(2,1)}, u32[]{:S(2)}) copy-start(bf16[1152,1152]{1,0:T(8,128)(2,1)} %param.12) | copy-start | bytes 7962628
  1.8 14.9 %collective-permute-start = (f32[2,64]{1,0:T(2,128)S(1)}, f32[2,64]{1,0:T(2,128)S(1)}, u32[]{:S(2)}, u32[]{:S(2)}) collective-permute-start(f32[2,64]{1,0:T(2,128)S(1)} %pad_maximum_fusion.8), channel_id=1, source_target_pairs={{1,0},{2,1},{3,2},{4,3},{5,4},{6,5},{7,6},{8,7},{9,8},{10,9},{11,1... | collective-permute-start | bytes 1544 | tf_op jit(solution)/shard_map/ppermute | solution.py:16
  9.9 66.4 %collective-permute-start.1 = (f32[1,72]{0,1:T(8,128)}, f32[1,72]{0,1:T(8,128)}, u32[]{:S(2)}, u32[]{:S(2)}) collective-permute-start(f32[1,72]{0,1:T(8,128)} %slice.113), channel_id=1, source_target_pairs={{0,16},{16,32},{32,48},{48,64},{64,80},{80,96},{96,112},{112,128},... | collective-permute-start | bytes 872 | tf_op jit(solution)/shard_map/ppermute | solution.py:35
  16.6 59.6 %copy-start.11 = (f32[8192]{0:T(1024)}, f32[8192]{0:T(1024)S(1)}, u32[]{:S(2)}) copy-start(f32[8192]{0:T(1024)S(1)} %dynamic_slice.15) | copy-start | bytes 98308
  72.9 3.4 copy-start.5
  72.9 3.4 copy-start.13
  72.9 3.4 copy-start.15
  79.4 7.7 %copy-start.9 = (f32[64,128]{1,0:T(8,128)S(1)}, f32[64,128]{1,0:T(8,128)}, u32[]{:S(2)}) copy-start(f32[64,128]{1,0:T(8,128)} %param.11) | copy-start | bytes 98308
  80.5 28.8 %all-to-all-start = ((bf16[16,512,72]{1,2,0:T(8,128)(2,1)}), bf16[16,512,72]{1,2,0:T(8,128)(2,1)}, u32[]{:S(2)}, u32[]{:S(2)}) async-start(bf16[16,512,72]{1,2,0:T(8,128)(2,1)} %bitcast.57), calls=%async_computation | async-start | bytes 2359296 | tf_op jit(solution)/shard_map/all_to_all | solution.py:131
  87.7 39.4 %collective-permute-start.2 = (f32[1,128]{1,0:T(1,128)}, f32[1,128]{1,0:T(1,128)}, u32[]{:S(2)}, u32[]{:S(2)}) collective-permute-start(f32[1,128]{1,0:T(1,128)} %get-tuple-element.29), channel_id=1, source_target_pairs={{1,0},{2,1},{3,2},{4,3},{5,4},{6,5},{7,6},{8,7},{9,8},{10,9},{11,1... | collective-permute-start | bytes 1544 | tf_op jit(solution)/shard_map/ppermute | solution.py:27
  97.5 29.6 %collective-permute-start.3 = (f32[1,128]{1,0:T(1,128)}, f32[1,128]{1,0:T(1,128)}, u32[]{:S(2)}, u32[]{:S(2)}) collective-permute-start(f32[1,128]{1,0:T(1,128)} %get-tuple-element.30), channel_id=1, source_target_pairs={{0,1},{1,2},{2,3},{3,4},{4,5},{5,6},{6,7},{7,8},{8,9},{9,10},{10,1... | collective-permute-start | bytes 1544 | tf_op jit(solution)/shard_map/ppermute | solution.py:24
  109.3 3.3 copy-start.3
  116.9 7.4 %copy-start.8 = (bf16[1152,128]{1,0:T(8,128)(2,1)S(1)}, bf16[1152,128]{1,0:T(8,128)(2,1)}, u32[]{:S(2)}) copy-start(bf16[1152,128]{1,0:T(8,128)(2,1)} %param.14) | copy-start | bytes 884740
  119.4 49.3 %copy-start.10 = (f32[64,128]{1,0:T(8,128)S(1)}, f32[64,128]{1,0:T(8,128)}, u32[]{:S(2)}) copy-start(f32[64,128]{1,0:T(8,128)} %param.11) | copy-start | bytes 98308
  119.4 118.3 %all-to-all-start.1 = ((bf16[512,16,72]{0,2,1:T(8,128)(2,1)}), bf16[512,16,72]{0,2,1:T(8,128)(2,1)}, u32[]{:S(2)}, u32[]{:S(2)}) async-start(bf16[512,16,72]{0,2,1:T(8,128)(2,1)} %bitcast.55), calls=%async_computation.1 | async-start | bytes 2359296 | tf_op jit(solution)/shard_map/all_to_all | solution.py:135
  126.4 42.3 %collective-permute-start.4 = (f32[32,128]{1,0:T(8,128)S(1)}, f32[32,128]{1,0:T(8,128)S(1)}, u32[]{:S(2)}, u32[]{:S(2)}) collective-permute-start(f32[32,128]{1,0:T(8,128)S(1)} %get-tuple-element.27), channel_id=1, source_target_pairs={{255,0},{0,1},{1,2},{2,3},{3,4},{4,5},{5,6},{6,7},{7,8},{8,9},{9,1... | collective-permute-start | bytes 49160 | tf_op jit(solution)/shard_map/ppermute | solution.py:16
  169.7 1.4 collective-permute-start.5
  239.2 1.7 copy-start.6
  240.9 5.3 %copy-start.1 = (f32[2,8192]{0,1:T(8,128)S(1)}, f32[2,8192]{0,1:T(8,128)}, u32[]{:S(2)}) copy-start(f32[2,8192]{0,1:T(8,128)} %all_gather.7) | copy-start | bytes 196612
  241.2 13.4 %copy-start.12 = (f32[8192]{0:T(1024)S(1)}, f32[8192]{0:T(1024)}, u32[]{:S(2)}) copy-start(f32[8192]{0:T(1024)} %copy-done.11) | copy-start | bytes 98308
  241.2 13.4 %copy-start.14 = (f32[72]{0:T(128)S(1)}, f32[72]{0:T(128)}, u32[]{:S(2)}) copy-start(f32[72]{0:T(128)} %get-tuple-element.32) | copy-start | bytes 868
  241.2 13.4 %copy-start.16 = (f32[72]{0:T(128)S(1)}, f32[72]{0:T(128)}, u32[]{:S(2)}) copy-start(f32[72]{0:T(128)} %dynamic_slice.16) | copy-start | bytes 868
  241.2 13.4 %collective-permute-start.6 = (f32[1,72]{0,1:T(8,128)S(1)}, f32[1,72]{0,1:T(8,128)S(1)}, u32[]{:S(2)}, u32[]{:S(2)}) collective-permute-start(f32[1,72]{0,1:T(8,128)S(1)} %slice.156), channel_id=1, source_target_pairs={{0,16},{16,32},{32,48},{48,64},{64,80},{80,96},{96,112},{112,128},... | collective-permute-start | bytes 872 | tf_op jit(solution)/shard_map/ppermute | solution.py:35
  292.5 1.9 copy-start.2
  292.5 2.2 copy-start.4
  300.2 39.0 %all-to-all-start.3 = ((bf16[512,16,72]{0,2,1:T(8,128)(2,1)}), bf16[512,16,72]{0,2,1:T(8,128)(2,1)}, u32[]{:S(2)}, u32[]{:S(2)}) async-start(bf16[512,16,72]{0,2,1:T(8,128)(2,1)} %bitcast.56), calls=%async_computation.3 | async-start | bytes 2359296 | tf_op jit(solution)/shard_map/all_to_all | solution.py:135
  304.7 26.1 %collective-permute-start.7 = (f32[1,128]{1,0:T(1,128)S(1)}, f32[1,128]{1,0:T(1,128)S(1)}, u32[]{:S(2)}, u32[]{:S(2)}) collective-permute-start(f32[1,128]{1,0:T(1,128)S(1)} %get-tuple-element.25), channel_id=1, source_target_pairs={{1,0},{2,1},{3,2},{4,3},{5,4},{6,5},{7,6},{8,7},{9,8},{10,9},{11,1... | collective-permute-start | bytes 1544 | tf_op jit(solution)/shard_map/ppermute | solution.py:27
  312.4 21.9 %collective-permute-start.8 = (f32[1,128]{1,0:T(1,128)S(1)}, f32[1,128]{1,0:T(1,128)S(1)}, u32[]{:S(2)}, u32[]{:S(2)}) collective-permute-start(f32[1,128]{1,0:T(1,128)S(1)} %get-tuple-element.26), channel_id=1, source_target_pairs={{0,1},{1,2},{2,3},{3,4},{4,5},{5,6},{6,7},{7,8},{8,9},{9,10},{10,1... | collective-permute-start | bytes 1544 | tf_op jit(solution)/shard_map/ppermute | solution.py:24
  316.5 18.1 %collective-permute-start.9 = (f32[32,128]{1,0:T(8,128)S(1)}, f32[32,128]{1,0:T(8,128)S(1)}, u32[]{:S(2)}, u32[]{:S(2)}) collective-permute-start(f32[32,128]{1,0:T(8,128)S(1)} %get-tuple-element.23), channel_id=1, source_target_pairs={{255,0},{0,1},{1,2},{2,3},{3,4},{4,5},{5,6},{6,7},{7,8},{8,9},{9,1... | collective-permute-start | bytes 49160 | tf_op jit(solution)/shard_map/ppermute | solution.py:16
  340.8 1.7 copy-start.7
where the time goes:
time: 345 us; the launch traced here: 344 us
  blocking collectives  156 us (45%)
  waiting for transfers between devices  77.5 us (22%)
  starting transfers between devices  52 us (15%)
  local copies, waits for them, and re-layouts  24 us (7%)
  other arithmetic  17.3 us (5%)
  matrix products  16.7 us (5%)
    all_gather x2, blocking collectives, per_device(): current = lax.all_gather(mine, 'bin', axis=1, tiled=True)  120 us
    ppermute x4, waiting for transfers between devices, shifted(): return lax.ppermute(block, axis, route)  43.1 us
    all_to_all x1, blocking collectives, per_device(): lax.all_to_all(moved.astype(jnp.bfloat16), 'bin', split_axis=0, concat_ax...  35.4 us
    ppermute x2, starting transfers between devices, padded_2(): lax.ppermute(lax.slice_in_dim(block, 0, width, axis=dim), axis, backward)  17.5 us
    ppermute x2, waiting for transfers between devices, padded_2(): lax.ppermute(lax.slice_in_dim(block, 0, width, axis=dim), axis, backward)  13.9 us
    all_to_all x2, starting transfers between devices, per_device(): lax.all_to_all(increment, 'bin', split_axis=1, concat_axis=0, tiled=True)  8.89 us
    all_to_all x1, waiting for transfers between devices, per_device(): lax.all_to_all(moved.astype(jnp.bfloat16), 'bin', split_axis=0, concat_ax...  8.04 us
    ppermute x2, starting transfers between devices, from_behind(): return lax.ppermute(shard, axis, pairs)  7.86 us
  transfers between devices with their start and end apart: 13, of which 8 were waited for; matrix products, arithmetic and copies ran while one was open for 10% of the time, Pallas kernels for 0%

commit v1 on v0

v1 whole, which is shorter than its diff:
```python
import math

import jax
import jax.numpy as jnp
from jax import lax
from jax.sharding import PartitionSpec as P

NDIR = 36
LEVELS = 64
STEPS = 2
ALL = ("band", "bin")


def shifted(block, axis, distance):
    devices = range(lax.axis_size(axis))
    route = [((i - distance) % len(devices), i) for i in devices]
    return lax.ppermute(block, axis, route)


def from_behind(shard, axis, by):
    peers = lax.axis_size(axis)
    pairs = [(i, i + by) for i in range(peers) if 0 <= i + by < peers]
    return lax.ppermute(shard, axis, pairs)


def bin_angles(count):
    index = jnp.arange(count)
    angle = 2.0 * math.pi / NDIR * (index % NDIR).astype(jnp.float32)
    return (jnp.cos(angle), jnp.sin(angle))


def propagate(field, prev, current, speed_bins, cos_b, sin_b, mask_cells):
    speed = speed_bins[None, :] + 0.25 * (
        jnp.tanh(current[0])[:, None] * cos_b[None, :]
        + jnp.tanh(current[1])[:, None] * sin_b[None, :]
    )
    behind = jnp.concatenate([prev, field[:-1]], 0)
    return mask_cells[:, None] * (field - speed * (field - behind))


def sources(rounded, mask_cells, source_a, source_b, stokes_kernel):
    gain = jnp.dot(rounded, source_a, preferred_element_type=jnp.float32)
    other = jnp.dot(rounded, source_b, preferred_element_type=jnp.float32)
    increment = (0.1 * mask_cells[:, None] * (gain + 0.5 * gain * other)).astype(jnp.bfloat16)
    stokes = jnp.dot(rounded, stokes_kernel, preferred_element_type=jnp.float32)
    return (increment, stokes)


def ocean_step(window, below, above, forcing, joint):
    columns = window.shape[0]
    padded = jnp.concatenate([below, window, above], 0)
    up = padded[2:]
    down = padded[:-2]
    if joint is not None:
        row = jnp.arange(columns)[:, None]
        up = jnp.where(joint & (row == columns // 2 - 1), 0.0, up)
        down = jnp.where(joint & (row == columns // 2), 0.0, down)
    lap_h = up + down - 2.0 * window
    cube = window.reshape(columns, 2, LEVELS)
    edge = jnp.pad(cube, ((0, 0), (0, 0), (1, 1)), mode="edge")
    lap_v = (edge[:, :, 2:] + edge[:, :, :-2] - 2.0 * cube).reshape(columns, 2 * LEVELS)
    return window + 0.2 * lap_h + 0.2 * lap_v + 1.5 * forcing - 0.05 * window


def per_device(
    spectrum, velocity, source_a, source_b, stokes_kernel, group_speed, column_map, land_mask
):
    bin_count = lax.axis_size("bin")
    device_count = lax.axis_size("band") * bin_count
    device = lax.axis_index("band") * bin_count + lax.axis_index("bin")
    cell_dev = spectrum.shape[0] // bin_count
    columns = velocity.shape[0]
    half = columns // 2
    total = columns * device_count
    bins = spectrum.shape[1] * bin_count

    cell_first = device * cell_dev
    local_map = lax.dynamic_slice_in_dim(column_map, cell_first, cell_dev)
    local_mask = lax.dynamic_slice_in_dim(land_mask, cell_first, cell_dev).astype(jnp.float32)
    cos_b, sin_b = bin_angles(bins)

    first = device * columns + half
    where = jnp.mod(local_map - first, total)
    onehot = (where[None, :] == jnp.arange(columns)[:, None]).astype(jnp.float32)
    counts = jnp.sum(onehot, axis=1)
    joint = (device == device_count - 1) if device_count > 1 else None

    upper = shifted(velocity[: half + 1], ALL, -1)
    window = jnp.concatenate([velocity[half:], upper[:half]], 0)
    below = velocity[half - 1 : half]
    above = upper[half:]

    field = lax.all_to_all(spectrum, "bin", split_axis=0, concat_axis=1, tiled=True)
    for step in range(STEPS):
        current = jnp.stack(
            [jnp.take(window[:, 0], where, axis=0), jnp.take(window[:, LEVELS], where, axis=0)]
        )
        prev = from_behind(field[-1:], ALL, 1)
        moved = propagate(field, prev, current, group_speed, cos_b, sin_b, local_mask)
        increment, stokes = sources(
            moved.astype(jnp.bfloat16), local_mask, source_a, source_b, stokes_kernel
        )
        field = moved + increment.astype(jnp.float32)
        sums = jnp.dot(onehot, stokes, precision=lax.Precision.HIGHEST)
        forcing = sums / counts[:, None]
        if step > 0:
            below = shifted(window[-1:], ALL, 1)
            above = shifted(window[:1], ALL, -1)
        window = ocean_step(window, below, above, forcing, joint)
    velocity_out = jnp.concatenate([shifted(window[half:], ALL, 1), window[:half]], 0)
    spectrum_out = lax.all_to_all(field, "bin", split_axis=1, concat_axis=0, tiled=True)
    return (spectrum_out, velocity_out)


def solution(mesh):
    in_specs = (P("band", "bin"), P(ALL, None), P(), P(), P(), P(), P(), P())
    out_specs = (P("band", "bin"), P(ALL, None))
    return jax.shard_map(
        per_device, mesh=mesh, in_specs=in_specs, out_specs=out_specs, check_vma=False
    )
```

time: 345 us -> 344 us (level)
  the two profiles are of different devices: /device:TPU:80 before, /device:TPU:88 now
where the time goes in v1:
time: 344 us; the launch traced here: 340 us
  other arithmetic  167 us (49%)
  waiting for transfers between devices  92.7 us (27%)
  starting transfers between devices  38 us (11%)
  local copies, waits for them, and re-layouts  29.4 us (9%)
  matrix products  12.1 us (4%)
    ppermute x4, waiting for transfers between devices, shifted(): return lax.ppermute(block, axis, route)  90.3 us
    tanh x2, other arithmetic, propagate(): jnp.tanh(current[0])[:, None] * cos_b[None, :]  80.3 us
    tanh x2, other arithmetic, propagate(): jnp.tanh(current[1])[:, None] * sin_b[None, :]  79.5 us
    ppermute x4, starting transfers between devices, shifted(): return lax.ppermute(block, axis, route)  14.3 us
    all_to_all x1, starting transfers between devices, per_device(): lax.all_to_all(field, 'bin', split_axis=1, concat_axis=0, tiled=True)  10.4 us
    all_to_all x1, starting transfers between devices, per_device(): lax.all_to_all(spectrum, 'bin', split_axis=0, concat_axis=1, tiled=True)  9.41 us
  transfers between devices with their start and end apart: 8, of which 4 were waited for; matrix products, arithmetic and copies ran while one was open for 52% of the time, Pallas kernels for 0%

profile of v1, /device:TPU:88, one launch (start us, length us, event | category | flops | bytes accessed | tf_op | source)
XLA Modules:
  0.0 339.8 jit_solution(9137622475458007790)
XLA Ops:
  0.6 0.0 copy-start
  0.6 3.4 %copy.39 = f32[9,16,8,512]{3,2,0,1:T(8,128)} copy(f32[9,16,8,512]{3,2,1,0:T(8,128)} %bitcast.281) | data formatting | bytes 4718592 | tf_op jit(solution)/shard_map/all_to_all | solution.py:93
  4.1 9.4 %all-to-all-start = ((f32[16,512,72]{1,2,0:T(8,128)}), f32[16,512,72]{1,2,0:T(8,128)}, u32[]{:S(2)}, u32[]{:S(2)}) async-start(f32[16,512,72]{1,2,0:T(8,128)} %bitcast.279), calls=%async_computation | async-start | bytes 4718592 | tf_op jit(solution)/shard_map/all_to_all | solution.py:93
  13.5 7.2 %collective-permute-start = (f32[33,128]{1,0:T(8,128)S(1)}, f32[33,128]{1,0:T(8,128)S(1)}, u32[]{:S(2)}, u32[]{:S(2)}) collective-permute-start(f32[33,128]{1,0:T(8,128)S(1)} %get-tuple-element.84), channel_id=1, source_target_pairs={{1,0},{2,1},{3,2},{4,3},{5,4},{6,5},{7,6},{8,7},{9,8},{10,9},{11,1... | collective-permute-start | bytes 50696 | tf_op jit(solution)/shard_map/ppermute | solution.py:17
  20.8 0.8 broadcast_multiply_fusion
  21.5 0.1 fusion.53
  21.6 44.8 %collective-permute-done = f32[33,128]{1,0:T(8,128)S(1)} collective-permute-done((f32[33,128]{1,0:T(8,128)S(1)}, f32[33,128]{1,0:T(8,128)S(1)}, u32[]{:S(2)}, u32[]{:S(2)}) %collective-permute-start) | collective-permute-done | bytes 16928 | tf_op jit(solution)/shard_map/ppermute | solution.py:17
  66.4 0.1 reshape.68
  66.6 0.2 fusion.38
  66.7 0.7 fusion.83
  67.4 0.7 fusion.84
  68.2 0.7 fusion.85
  68.9 0.7 fusion.86
  69.7 40.4 %select_tanh_fusion.3 = (f32[512]{0:T(512)S(1)}, pred[512]{0:T(512)(128)(4,1)S(1)}, pred[512]{0:T(512)(128)(4,1)S(1)}, pred[512]{0:T(512)(128)(4,1)S(1)}, pred[5...) fusion(f32[]{:T(128)} %bitcast.65, f32[]{:T(128)} %bitcast.64, ...), kind=kLoop, calls=%fused_computation.93 | loop fusion | flops 74240 | bytes 39176 | tf_op jit(solution)/shard_map/tanh | solution.py:34
  110.1 0.7 fusion.80
  110.8 0.7 fusion.81
  111.5 0.7 fusion.82
  112.3 39.5 %select_tanh_fusion.2 = f32[512]{0:T(512)S(1)} fusion(pred[512]{0:T(512)(128)(4,1)S(1)} %get-tuple-element.73, pred[512]{0:T(512)(128)(4,1)S(1)} %get-tuple-element.72, pred[512]{0:T(512)(128)(4,1)S(1)} %get-tuple-element.71, pred[512]{0:T(512)(128)(4,1)S(1)} %get-tuple-element.70, pred[512]{0:T(512)(128)(4,1)S(1)} %get-tuple-element.69, ...), kind=kLoop, calls=%fused_computation.92 | loop fusion | flops 32768 | bytes 35072 | tf_op jit(solution)/shard_map/tanh | solution.py:35
  151.7 0.1 fusion.68
  151.9 0.3 fusion.25
  152.2 1.6 slice_reduce_fusion
  153.8 0.1 slice.107
  153.9 1.9 collective-permute-start.1
  155.8 0.1 convert_reduce_fusion
  155.9 0.1 mul.203
  156.0 3.0 copy.33
  159.1 3.1 copy.31
  162.1 2.3 collective-permute-done.1
  164.5 3.4 fusion.12
  167.9 0.5 fusion.62
  168.4 0.2 fusion.17
  168.6 0.1 fusion.36
  168.7 0.2 slice_reduce_fusion.2
  168.9 0.7 fusion.79
  169.6 0.7 fusion.76
  170.3 0.7 fusion.77
  171.0 0.7 fusion.78
  171.8 0.7 fusion.75
  172.4 0.7 fusion.72
  173.2 0.7 fusion.73
  173.9 0.7 fusion.74
  174.6 1.8 fusion.65
  176.5 1.9 fusion.9
  178.5 2.1 collective-permute-start.2
  180.6 40.0 %select_tanh_fusion = f32[512]{0:T(512)S(1)} fusion(pred[512]{0:T(512)(128)(4,1)S(1)} %get-tuple-element.73, pred[512]{0:T(512)(128)(4,1)S(1)} %get-tuple-element.72, pred[512]{0:T(512)(128)(4,1)S(1)} %get-tuple-element.71, pred[512]{0:T(512)(128)(4,1)S(1)} %get-tuple-element.70, pred[512]{0:T(512)(128)(4,1)S(1)} %get-tuple-element.69, ...), kind=kLoop, calls=%fused_computation.90 | loop fusion | flops 32768 | bytes 35072 | tf_op jit(solution)/shard_map/tanh | solution.py:35
  220.6 39.9 %select_tanh_fusion.1 = f32[512]{0:T(512)S(1)} fusion(pred[512]{0:T(512)(128)(4,1)S(1)} %get-tuple-element.73, pred[512]{0:T(512)(128)(4,1)S(1)} %get-tuple-element.72, pred[512]{0:T(512)(128)(4,1)S(1)} %get-tuple-element.71, pred[512]{0:T(512)(128)(4,1)S(1)} %get-tuple-element.70, pred[512]{0:T(512)(128)(4,1)S(1)} %get-tuple-element.69, ...), kind=kLoop, calls=%fused_computation.91 | loop fusion | flops 32768 | bytes 35072 | tf_op jit(solution)/shard_map/tanh | solution.py:34
  260.5 1.1 fusion.15
  261.6 1.9 fusion.60
  263.5 3.4 fusion.6
  266.9 3.1 copy.34
  269.9 10.4 %all-to-all-start.1 = ((f32[512,16,72]{0,2,1:T(8,128)}), f32[512,16,72]{0,2,1:T(8,128)}, u32[]{:S(2)}, u32[]{:S(2)}) async-start(f32[512,16,72]{0,2,1:T(8,128)} %bitcast.280), calls=%async_computation.1 | async-start | bytes 4718592 | tf_op jit(solution)/shard_map/all_to_all | solution.py:111
  280.3 0.1 reshape.69
  280.4 0.1 fusion.67
  280.5 0.3 fusion.22
  280.8 0.1 mul.220
  280.9 0.4 collective-permute-start.4
  281.3 6.5 %collective-permute-start.3 = (f32[1,128]{1,0:T(1,128)S(1)}, f32[1,128]{1,0:T(1,128)S(1)}, u32[]{:S(2)}, u32[]{:S(2)}) collective-permute-start(f32[1,128]{1,0:T(1,128)S(1)} %get-tuple-element.81), channel_id=1, source_target_pairs={{1,0},{2,1},{3,2},{4,3},{5,4},{6,5},{7,6},{8,7},{9,8},{10,9},{11,1... | collective-permute-start | bytes 1544 | tf_op jit(solution)/shard_map/ppermute | solution.py:17
  287.8 2.1 fusion.57
  290.0 37.2 %collective-permute-done.4 = f32[1,128]{1,0:T(1,128)S(1)} collective-permute-done((f32[1,128]{1,0:T(1,128)S(1)}, f32[1,128]{1,0:T(1,128)S(1)}, u32[]{:S(2)}, u32[]{:S(2)}) %collective-permute-start.4) | collective-permute-done | bytes 544 | tf_op jit(solution)/shard_map/ppermute | solution.py:17
  327.2 0.2 fusion.19
  327.5 0.1 collective-permute-start.5
  327.6 8.3 %collective-permute-done.5 = f32[32,128]{1,0:T(8,128)S(1)} collective-permute-done((f32[32,128]{1,0:T(8,128)S(1)}, f32[32,128]{1,0:T(8,128)S(1)}, u32[]{:S(2)}, u32[]{:S(2)}) %collective-permute-start.5) | collective-permute-done | bytes 16416 | tf_op jit(solution)/shard_map/ppermute | solution.py:17
  335.8 0.6 pad_maximum_fusion.8
  336.5 3.4 copy.37
  (23 shorter events, 0.1 us)
Async XLA Ops:
  0.6 174.0 %copy-start = (bf16[1152,1152]{1,0:T(8,128)(2,1)S(1)}, bf16[1152,1152]{1,0:T(8,128)(2,1)}, u32[]{:S(2)}) copy-start(bf16[1152,1152]{1,0:T(8,128)(2,1)} %param.12) | copy-start | bytes 7962628
  4.1 9.4 %copy-start.3 = (f32[64,128]{1,0:T(8,128)S(1)}, f32[64,128]{1,0:T(8,128)}, u32[]{:S(2)}) copy-start(f32[64,128]{1,0:T(8,128)} %param.11) | copy-start | bytes 98308
  4.1 148.1 %all-to-all-start = ((f32[16,512,72]{1,2,0:T(8,128)}), f32[16,512,72]{1,2,0:T(8,128)}, u32[]{:S(2)}, u32[]{:S(2)}) async-start(f32[16,512,72]{1,2,0:T(8,128)} %bitcast.279), calls=%async_computation | async-start | bytes 4718592 | tf_op jit(solution)/shard_map/all_to_all | solution.py:93
  13.5 52.9 %collective-permute-start = (f32[33,128]{1,0:T(8,128)S(1)}, f32[33,128]{1,0:T(8,128)S(1)}, u32[]{:S(2)}, u32[]{:S(2)}) collective-permute-start(f32[33,128]{1,0:T(8,128)S(1)} %get-tuple-element.84), channel_id=1, source_target_pairs={{1,0},{2,1},{3,2},{4,3},{5,4},{6,5},{7,6},{8,7},{9,8},{10,9},{11,1... | collective-permute-start | bytes 50696 | tf_op jit(solution)/shard_map/ppermute | solution.py:17
  153.9 10.6 %collective-permute-start.1 = (f32[1,1152]{1,0:T(1,128)S(1)}, f32[1,1152]{1,0:T(1,128)S(1)}, u32[]{:S(2)}, u32[]{:S(2)}) collective-permute-start(f32[1,1152]{1,0:T(1,128)S(1)} %slice.107), channel_id=1, source_target_pairs={{0,1},{1,2},{2,3},{3,4},{4,5},{5,6},{6,7},{7,8},{8,9},{9,10},{10,1... | collective-permute-start | bytes 13832 | tf_op jit(solution)/shard_map/ppermute | solution.py:23
  159.1 5.4 %copy-start.4 = (f32[1152]{0:T(1024)S(1)}, f32[1152]{0:T(1024)}, u32[]{:S(2)}) copy-start(f32[1152]{0:T(1024)} %param.15) | copy-start | bytes 13828
  164.5 3.4 copy-start.2
  174.6 1.9 copy-start.5
  178.5 82.1 %collective-permute-start.2 = (f32[1,1152]{1,0:T(1,128)S(1)}, f32[1,1152]{1,0:T(1,128)S(1)}, u32[]{:S(2)}, u32[]{:S(2)}) collective-permute-start(f32[1,1152]{1,0:T(1,128)S(1)} %slice.660), channel_id=1, source_target_pairs={{0,1},{1,2},{2,3},{3,4},{4,5},{5,6},{6,7},{7,8},{8,9},{9,10},{10,1... | collective-permute-start | bytes 13832 | tf_op jit(solution)/shard_map/ppermute | solution.py:23
  261.6 1.9 copy-start.1
  269.9 66.5 %all-to-all-start.1 = ((f32[512,16,72]{0,2,1:T(8,128)}), f32[512,16,72]{0,2,1:T(8,128)}, u32[]{:S(2)}, u32[]{:S(2)}) async-start(f32[512,16,72]{0,2,1:T(8,128)} %bitcast.280), calls=%async_computation.1 | async-start | bytes 4718592 | tf_op jit(solution)/shard_map/all_to_all | solution.py:111
  280.9 46.3 %collective-permute-start.4 = (f32[1,128]{1,0:T(1,128)S(1)}, f32[1,128]{1,0:T(1,128)S(1)}, u32[]{:S(2)}, u32[]{:S(2)}) collective-permute-start(f32[1,128]{1,0:T(1,128)S(1)} %get-tuple-element.82), channel_id=1, source_target_pairs={{255,0},{0,1},{1,2},{2,3},{3,4},{4,5},{5,6},{6,7},{7,8},{8,9},{9,1... | collective-permute-start | bytes 1544 | tf_op jit(solution)/shard_map/ppermute | solution.py:17
  281.3 45.9 %collective-permute-start.3 = (f32[1,128]{1,0:T(1,128)S(1)}, f32[1,128]{1,0:T(1,128)S(1)}, u32[]{:S(2)}, u32[]{:S(2)}) collective-permute-start(f32[1,128]{1,0:T(1,128)S(1)} %get-tuple-element.81), channel_id=1, source_target_pairs={{1,0},{2,1},{3,2},{4,3},{5,4},{6,5},{7,6},{8,7},{9,8},{10,9},{11,1... | collective-permute-start | bytes 1544 | tf_op jit(solution)/shard_map/ppermute | solution.py:17
  327.5 8.4 %collective-permute-start.5 = (f32[32,128]{1,0:T(8,128)S(1)}, f32[32,128]{1,0:T(8,128)S(1)}, u32[]{:S(2)}, u32[]{:S(2)}) collective-permute-start(f32[32,128]{1,0:T(8,128)S(1)} %get-tuple-element.79), channel_id=1, source_target_pairs={{255,0},{0,1},{1,2},{2,3},{3,4},{4,5},{5,6},{6,7},{7,8},{8,9},{9,1... | collective-permute-start | bytes 49160 | tf_op jit(solution)/shard_map/ppermute | solution.py:17

commit v2 on v1

--- a/solution.py
+++ b/solution.py
@@ -9,6 +9,7 @@
 LEVELS = 64
 STEPS = 2
 ALL = ("band", "bin")
+EXTRA = 8
 
 
 def shifted(block, axis, distance):
@@ -75,8 +76,14 @@
     bins = spectrum.shape[1] * bin_count
 
     cell_first = device * cell_dev
-    local_map = lax.dynamic_slice_in_dim(column_map, cell_first, cell_dev)
-    local_mask = lax.dynamic_slice_in_dim(land_mask, cell_first, cell_dev).astype(jnp.float32)
+    ext_map = lax.dynamic_slice_in_dim(
+        jnp.concatenate([column_map[-EXTRA:], column_map]), cell_first, cell_dev + EXTRA
+    )
+    ext_mask = lax.dynamic_slice_in_dim(
+        jnp.concatenate([land_mask[-EXTRA:], land_mask]), cell_first, cell_dev + EXTRA
+    ).astype(jnp.float32)
+    local_map = ext_map[EXTRA:]
+    local_mask = ext_mask[EXTRA:]
     cos_b, sin_b = bin_angles(bins)
 
     first = device * columns + half
@@ -90,23 +97,38 @@
     below = velocity[half - 1 : half]
     above = upper[half:]
 
-    field = lax.all_to_all(spectrum, "bin", split_axis=0, concat_axis=1, tiled=True)
+    own = jnp.concatenate([velocity, upper[:half]], 0)
+    ext_where = jnp.mod(ext_map - device * columns, total)
+    table = jnp.stack([own[:, 0], own[:, LEVELS]])
+    current = jnp.take(table, ext_where, axis=1)
+
+    tail = from_behind(spectrum[-EXTRA:], "band", 1)
+    blocks = spectrum.reshape(bin_count, cell_dev, spectrum.shape[1])
+    heads = jnp.concatenate([tail[None], blocks[:-1, -EXTRA:]], 0)
+    sent = jnp.concatenate([heads, blocks], 1).reshape(-1, spectrum.shape[1])
+    field = lax.all_to_all(sent, "bin", split_axis=0, concat_axis=1, tiled=True)
+    prev = jnp.zeros((1, bins), jnp.float32)
+    mask = ext_mask
     for step in range(STEPS):
-        current = jnp.stack(
-            [jnp.take(window[:, 0], where, axis=0), jnp.take(window[:, LEVELS], where, axis=0)]
-        )
-        prev = from_behind(field[-1:], ALL, 1)
-        moved = propagate(field, prev, current, group_speed, cos_b, sin_b, local_mask)
+        moved = propagate(field, prev, current, group_speed, cos_b, sin_b, mask)
         increment, stokes = sources(
-            moved.astype(jnp.bfloat16), local_mask, source_a, source_b, stokes_kernel
+            moved.astype(jnp.bfloat16), mask, source_a, source_b, stokes_kernel
         )
         field = moved + increment.astype(jnp.float32)
+        if step == 0:
+            prev = field[EXTRA - 1 : EXTRA]
+            field = field[EXTRA:]
+            stokes = stokes[EXTRA:]
+            mask = local_mask
         sums = jnp.dot(onehot, stokes, precision=lax.Precision.HIGHEST)
         forcing = sums / counts[:, None]
         if step > 0:
             below = shifted(window[-1:], ALL, 1)
             above = shifted(window[:1], ALL, -1)
         window = ocean_step(window, below, above, forcing, joint)
+        if step + 1 < STEPS:
+            table = jnp.stack([window[:, 0], window[:, LEVELS]])
+            current = jnp.take(table, where, axis=1)
     velocity_out = jnp.concatenate([shifted(window[half:], ALL, 1), window[:half]], 0)
     spectrum_out = lax.all_to_all(field, "bin", split_axis=1, concat_axis=0, tiled=True)
     return (spectrum_out, velocity_out)

time: 344 us -> 205 us (0.60)
  other arithmetic: 167 us -> 9.68 us
  starting transfers between devices: 38 us -> 53.2 us
  matrix products: 12.1 us -> 17.1 us
  waiting for transfers between devices: 92.7 us -> 96.6 us
    tanh x4 -> x0, other arithmetic: 160 us -> none  [the longest x2 80.3 us: propagate(): jnp.tanh(current[0])[:, None] * cos_b[None, :]]
    ppermute x4, starting transfers between devices: 14.3 us -> 33 us  [shifted(): return lax.ppermute(block, axis, route)]
    gather x15 -> x2, local copies, waits for them, and re-layouts: 10.8 us -> 2.61 us  [the longest x1 1.57 us: per_device(): current = jnp.take(table, ext_where, axis=1)]
    convert_element_type x0 -> x1, other arithmetic: none -> 4.85 us  [per_device(): moved.astype(jnp.bfloat16)]
    ppermute x4, waiting for transfers between devices: 90.3 us -> 95 us  [shifted(): return lax.ppermute(block, axis, route)]
    unnamed x12 -> x17, local copies, waits for them, and re-layouts: 0.03 us -> 3.81 us
    dot_general x2, matrix products: 5.31 us -> 8.84 us  [sources(): other = jnp.dot(rounded, source_b, preferred_element_type=jnp.float32)]
  transfers between devices with their start and end apart: 8 -> 7, of which waited for: 4 -> 4; matrix products, arithmetic and copies ran while one was open for 52% -> 6% of each run, Pallas kernels for 0% -> 0%
where the time goes in v2:
time: 205 us; the launch traced here: 204 us
  waiting for transfers between devices  96.6 us (47%)
  starting transfers between devices  53.2 us (26%)
  local copies, waits for them, and re-layouts  26 us (13%)
  matrix products  17.1 us (8%)
  other arithmetic  9.68 us (5%)
    ppermute x4, waiting for transfers between devices, shifted(): return lax.ppermute(block, axis, route)  95 us
    ppermute x4, starting transfers between devices, shifted(): return lax.ppermute(block, axis, route)  33 us
    dot_general x2, matrix products, sources(): other = jnp.dot(rounded, source_b, preferred_element_type=jnp.float32)  8.84 us
    all_to_all x1, starting transfers between devices, per_device(): field = lax.all_to_all(sent, 'bin', split_axis=0, concat_axis=1, tiled=True)  8.51 us
    all_to_all x1, starting transfers between devices, per_device(): lax.all_to_all(field, 'bin', split_axis=1, concat_axis=0, tiled=True)  7.85 us
    dot_general x2, matrix products, sources(): gain = jnp.dot(rounded, source_a, preferred_element_type=jnp.float32)  5.17 us
    convert_element_type x1, other arithmetic, per_device(): moved.astype(jnp.bfloat16)  4.85 us
  transfers between devices with their start and end apart: 7, of which 4 were waited for; matrix products, arithmetic and copies ran while one was open for 6% of the time, Pallas kernels for 0%

profile of v2, /device:TPU:88, one launch (start us, length us, event | category | flops | bytes accessed | tf_op | source)
XLA Modules:
  0.0 203.5 jit_solution(14181367169813425673)
XLA Ops:
  0.6 0.0 copy-start
  0.6 1.0 slice.132
  1.6 3.8 %collective-permute-start = (f32[8,72]{0,1:T(8,128)S(1)}, f32[8,72]{0,1:T(8,128)S(1)}, u32[]{:S(2)}, u32[]{:S(2)}) collective-permute-start(f32[8,72]{0,1:T(8,128)S(1)} %slice.132), channel_id=1, source_target_pairs={{0,16},{16,32},{32,48},{48,64},{64,80},{80,96},{96,112},{112,128},... | collective-permute-start | bytes 6920 | tf_op jit(solution)/shard_map/ppermute | solution.py:24
  5.5 3.1 %copy.80 = f32[9,8,16,512]{3,2,1,0:T(8,128)S(1)} copy(f32[9,8,16,512]{3,1,2,0:T(8,128)} %bitcast.35) | data formatting | bytes 4718592
  8.5 0.2 slice.173
  8.7 0.0 collective-permute-done
  8.7 0.8 pad_maximum_fusion
  9.6 2.6 %copy.71 = f32[16,520,72]{1,2,0:T(8,128)} copy(f32[16,520,72]{1,0,2:T(8,128)S(1)} %pad_maximum_fusion) | data formatting | bytes 4792320 | tf_op jit(solution)/shard_map/concatenate | solution.py:108
  12.1 8.5 %all-to-all-start = ((f32[16,520,72]{1,2,0:T(8,128)}), f32[16,520,72]{1,2,0:T(8,128)}, u32[]{:S(2)}, u32[]{:S(2)}) async-start(f32[16,520,72]{1,2,0:T(8,128)} %copy.71), calls=%async_computation | async-start | bytes 5898240 | tf_op jit(solution)/shard_map/all_to_all | solution.py:109
  20.7 7.4 %collective-permute-start.1 = (f32[33,128]{1,0:T(8,128)S(1)}, f32[33,128]{1,0:T(8,128)S(1)}, u32[]{:S(2)}, u32[]{:S(2)}) collective-permute-start(f32[33,128]{1,0:T(8,128)S(1)} %get-tuple-element.28), channel_id=1, source_target_pairs={{1,0},{2,1},{3,2},{4,3},{5,4},{6,5},{7,6},{8,7},{9,8},{10,9},{11,1... | collective-permute-start | bytes 50696 | tf_op jit(solution)/shard_map/ppermute | solution.py:18
  28.1 0.1 slice.134
  28.2 0.8 slice.130
  28.9 0.1 compare_and_fusion
  29.0 0.1 compare_and_fusion.3
  29.1 0.8 broadcast_multiply_fusion
  29.9 0.1 fusion.53
  30.0 0.1 convert_reduce_fusion
  30.1 0.1 broadcast_multiply_fusion.1
  30.2 40.4 %collective-permute-done.1 = f32[33,128]{1,0:T(8,128)S(1)} collective-permute-done((f32[33,128]{1,0:T(8,128)S(1)}, f32[33,128]{1,0:T(8,128)S(1)}, u32[]{:S(2)}, u32[]{:S(2)}) %collective-permute-start.1) | collective-permute-done | bytes 16928 | tf_op jit(solution)/shard_map/ppermute | solution.py:18
  70.6 0.2 maximum_reduce_fusion
  70.8 0.1 copy.72
  70.9 0.1 reshape.101
  71.0 0.1 fusion.70
  71.2 0.3 fusion.28
  71.5 0.1 mul.233
  71.6 1.6 gather_fusion
  73.1 0.1 select_bitcast_fusion
  73.3 0.3 fusion.20
  73.6 1.6 all-to-all-done
  75.2 3.4 %copy.75 = f32[520,1152]{1,0:T(8,128)} copy(f32[520,1152]{0,1:T(8,128)} %bitcast.2) | data formatting | bytes 4792320 | tf_op jit(solution)/shard_map/all_to_all | solution.py:109
  78.6 3.5 %copy.73 = f32[519,1152]{1,0:T(8,128)} copy(f32[519,1152]{0,1:T(8,128)} %bitcast.5) | data formatting | bytes 4783104 | tf_op jit(solution)/shard_map/slice | solution.py:38
  82.1 4.9 %fusion.67 = (bf16[520,1152]{1,0:T(8,128)(2,1)S(1)}, f32[520,1152]{1,0:T(8,128)}) fusion(f32[520,1152]{1,0:T(8,128)} %copy.75, f32[519,1152]{1,0:T(8,128)} %copy.73, f32[1152]{0:T(1024)S(1)} %get-tuple-element.31, f32[520]{0:T(1024)S(1)} %get-tuple-element.3, f32[1152]{0:T(1024)S(1)} %get-tuple-element.32, f32[520]{0:T(1024)S(1)} %get-tuple-element.2, ...), kind=kLoop, calls=%fused_computation.122 | loop fusion | flops 5990400 | bytes 8402016 | tf_op jit(solution)/shard_map/convert_element_type | solution.py:115
  86.9 3.3 %fusion.74 = f32[520,1152]{1,0:T(8,128)} fusion(bf16[520,1152]{1,0:T(8,128)(2,1)S(1)} %get-tuple-element.14, bf16[1152,1152]{1,0:T(8,128)(2,1)S(1)} %copy-done), kind=kOutput, calls=%fused_computation.128 | convolution fusion | flops 1380188160 | bytes 6248448 | tf_op jit(solution)/shard_map/dot_general | solution.py:43
  90.3 0.5 fusion.13
  90.8 0.2 fusion.16
  91.0 0.1 fusion.40
  91.1 0.2 slice_reduce_fusion.1
  91.3 0.1 copy.76
  91.4 1.0 gather_fusion.1
  92.4 0.1 select_bitcast_fusion.1
  92.6 0.3 fusion.22
  92.9 5.5 %fusion.6 = f32[520,1152]{1,0:T(8,128)S(1)} fusion(f32[520,1152]{1,0:T(8,128)} %get-tuple-element.15, f32[520,1152]{1,0:T(8,128)} %fusion.74, bf16[520,1152]{1,0:T(8,128)(2,1)} %copy-done.2, bf16[1152,1152]{1,0:T(8,128)(2,1)} %param.11, f32[520]{0:T(1024)S(1)} %get-tuple-element.12), kind=kOutput, calls=%fused_computation.10 | convolution fusion | flops 1384381440 | bytes 11042848 | tf_op jit(solution)/shard_map/dot_general | solution.py:44
  98.3 1.0 fusion.12
  99.4 0.0 copy-start.7
  99.4 1.9 fusion.64
  101.3 0.7 copy-done.7
  102.0 3.4 %fusion.9 = f32[512,1152]{1,0:T(8,128)} fusion(f32[512,1152]{1,0:T(8,128)S(1)} %fusion.12, f32[512,1152]{1,0:T(8,128)S(1)} %fusion.64, bf16[1152,1152]{1,0:T(8,128)(2,1)S(1)} %copy-done.7, f32[512]{0:T(512)S(1)} %get-tuple-element.29), kind=kOutput, calls=%fused_computation.13 | convolution fusion | flops 1363673088 | bytes 9734144 | tf_op jit(solution)/shard_map/dot_general | solution.py:44
  105.4 3.1 %copy.77 = f32[512,1152]{0,1:T(8,128)} copy(f32[512,1152]{1,0:T(8,128)} %fusion.9) | data formatting | bytes 4718592 | tf_op jit(solution)/shard_map/add | solution.py:117
  108.4 7.9 %all-to-all-start.1 = ((f32[512,16,72]{0,2,1:T(8,128)}), f32[512,16,72]{0,2,1:T(8,128)}, u32[]{:S(2)}, u32[]{:S(2)}) async-start(f32[512,16,72]{0,2,1:T(8,128)} %bitcast.34), calls=%async_computation.1 | async-start | bytes 4718592 | tf_op jit(solution)/shard_map/all_to_all | solution.py:133
  116.3 0.1 reshape.102
  116.4 0.7 collective-permute-start.3
  117.1 24.9 %collective-permute-start.2 = (f32[1,128]{1,0:T(1,128)S(1)}, f32[1,128]{1,0:T(1,128)S(1)}, u32[]{:S(2)}, u32[]{:S(2)}) collective-permute-start(f32[1,128]{1,0:T(1,128)S(1)} %get-tuple-element.25), channel_id=1, source_target_pairs={{1,0},{2,1},{3,2},{4,3},{5,4},{6,5},{7,6},{8,7},{9,8},{10,9},{11,1... | collective-permute-start | bytes 1544 | tf_op jit(solution)/shard_map/ppermute | solution.py:18
  141.9 0.1 fusion.69
  142.1 2.1 %fusion.61 = f32[512,128]{1,0:T(8,128)S(1)} fusion(bf16[1152,128]{1,0:T(8,128)(2,1)S(1)} %copy-done.4, f32[512,1152]{1,0:T(8,128)} %copy-done.1), kind=kOutput, calls=%fused_computation.117 | convolution fusion | flops 151584768 | bytes 2916352 | tf_op jit(solution)/shard_map/dot_general | solution.py:46
  144.2 0.3 fusion.25
  144.5 0.1 mul.257
  144.6 46.3 %collective-permute-done.3 = f32[1,128]{1,0:T(1,128)S(1)} collective-permute-done((f32[1,128]{1,0:T(1,128)S(1)}, f32[1,128]{1,0:T(1,128)S(1)}, u32[]{:S(2)}, u32[]{:S(2)}) %collective-permute-start.3) | collective-permute-done | bytes 544 | tf_op jit(solution)/shard_map/ppermute | solution.py:18
  190.9 0.0 collective-permute-done.2
  190.9 0.2 fusion.18
  191.2 0.1 collective-permute-start.4
  191.3 8.3 %collective-permute-done.4 = f32[32,128]{1,0:T(8,128)S(1)} collective-permute-done((f32[32,128]{1,0:T(8,128)S(1)}, f32[32,128]{1,0:T(8,128)S(1)}, u32[]{:S(2)}, u32[]{:S(2)}) %collective-permute-start.4) | collective-permute-done | bytes 16416 | tf_op jit(solution)/shard_map/ppermute | solution.py:18
  199.5 0.6 pad_maximum_fusion.10
  200.2 0.0 all-to-all-done.1
  200.2 3.4 %copy.79 = f32[16,9,8,512]{3,2,0,1:T(8,128)} copy(f32[16,9,8,512]{3,2,1,0:T(8,128)} %bitcast.13) | data formatting | bytes 4718592 | tf_op jit(solution)/shard_map/all_to_all | solution.py:133
  (25 shorter events, 0.1 us)
Async XLA Ops:
  0.6 86.3 %copy-start = (bf16[1152,1152]{1,0:T(8,128)(2,1)S(1)}, bf16[1152,1152]{1,0:T(8,128)(2,1)}, u32[]{:S(2)}) copy-start(bf16[1152,1152]{1,0:T(8,128)(2,1)} %param.10) | copy-start | bytes 7962628
  1.6 7.1 %collective-permute-start = (f32[8,72]{0,1:T(8,128)S(1)}, f32[8,72]{0,1:T(8,128)S(1)}, u32[]{:S(2)}, u32[]{:S(2)}) collective-permute-start(f32[8,72]{0,1:T(8,128)S(1)} %slice.132), channel_id=1, source_target_pairs={{0,16},{16,32},{32,48},{48,64},{64,80},{80,96},{96,112},{112,128},... | collective-permute-start | bytes 6920 | tf_op jit(solution)/shard_map/ppermute | solution.py:24
  12.1 8.5 %copy-start.5 = (f32[64,128]{1,0:T(8,128)S(1)}, f32[64,128]{1,0:T(8,128)}, u32[]{:S(2)}) copy-start(f32[64,128]{1,0:T(8,128)} %param.9) | copy-start | bytes 98308
  12.1 16.0 %copy-start.3 = (s32[131072]{0:T(1024)S(1)}, s32[131072]{0:T(1024)}, u32[]{:S(2)}) copy-start(s32[131072]{0:T(1024)} %param.14) | copy-start | bytes 1572868
  12.1 63.0 %all-to-all-start = ((f32[16,520,72]{1,2,0:T(8,128)}), f32[16,520,72]{1,2,0:T(8,128)}, u32[]{:S(2)}, u32[]{:S(2)}) async-start(f32[16,520,72]{1,2,0:T(8,128)} %copy.71), calls=%async_computation | async-start | bytes 5898240 | tf_op jit(solution)/shard_map/all_to_all | solution.py:109
  20.7 49.9 %collective-permute-start.1 = (f32[33,128]{1,0:T(8,128)S(1)}, f32[33,128]{1,0:T(8,128)S(1)}, u32[]{:S(2)}, u32[]{:S(2)}) collective-permute-start(f32[33,128]{1,0:T(8,128)S(1)} %get-tuple-element.28), channel_id=1, source_target_pairs={{1,0},{2,1},{3,2},{4,3},{5,4},{6,5},{7,6},{8,7},{9,8},{10,9},{11,1... | collective-permute-start | bytes 50696 | tf_op jit(solution)/shard_map/ppermute | solution.py:18
  78.6 3.5 %copy-start.6 = (f32[1152]{0:T(1024)S(1)}, f32[1152]{0:T(1024)}, u32[]{:S(2)}) copy-start(f32[1152]{0:T(1024)} %param.13) | copy-start | bytes 13828
  86.9 3.3 %copy-start.2 = (bf16[520,1152]{1,0:T(8,128)(2,1)}, bf16[520,1152]{1,0:T(8,128)(2,1)S(1)}, u32[]{:S(2)}) copy-start(bf16[520,1152]{1,0:T(8,128)(2,1)S(1)} %get-tuple-element.14) | copy-start | bytes 3594244
  86.9 3.3 %copy-start.4 = (bf16[1152,128]{1,0:T(8,128)(2,1)S(1)}, bf16[1152,128]{1,0:T(8,128)(2,1)}, u32[]{:S(2)}) copy-start(bf16[1152,128]{1,0:T(8,128)(2,1)} %param.12) | copy-start | bytes 884740
  99.4 1.9 copy-start.1
  99.4 2.6 %copy-start.7 = (bf16[1152,1152]{1,0:T(8,128)(2,1)S(1)}, bf16[1152,1152]{1,0:T(8,128)(2,1)}, u32[]{:S(2)}) copy-start(bf16[1152,1152]{1,0:T(8,128)(2,1)} %param.11) | copy-start | bytes 7962628
  108.4 91.7 %all-to-all-start.1 = ((f32[512,16,72]{0,2,1:T(8,128)}), f32[512,16,72]{0,2,1:T(8,128)}, u32[]{:S(2)}, u32[]{:S(2)}) async-start(f32[512,16,72]{0,2,1:T(8,128)} %bitcast.34), calls=%async_computation.1 | async-start | bytes 4718592 | tf_op jit(solution)/shard_map/all_to_all | solution.py:133
  116.4 74.5 %collective-permute-start.3 = (f32[1,128]{1,0:T(1,128)S(1)}, f32[1,128]{1,0:T(1,128)S(1)}, u32[]{:S(2)}, u32[]{:S(2)}) collective-permute-start(f32[1,128]{1,0:T(1,128)S(1)} %get-tuple-element.26), channel_id=1, source_target_pairs={{255,0},{0,1},{1,2},{2,3},{3,4},{4,5},{5,6},{6,7},{7,8},{8,9},{9,1... | collective-permute-start | bytes 1544 | tf_op jit(solution)/shard_map/ppermute | solution.py:18
  117.1 73.9 %collective-permute-start.2 = (f32[1,128]{1,0:T(1,128)S(1)}, f32[1,128]{1,0:T(1,128)S(1)}, u32[]{:S(2)}, u32[]{:S(2)}) collective-permute-start(f32[1,128]{1,0:T(1,128)S(1)} %get-tuple-element.25), channel_id=1, source_target_pairs={{1,0},{2,1},{3,2},{4,3},{5,4},{6,5},{7,6},{8,7},{9,8},{10,9},{11,1... | collective-permute-start | bytes 1544 | tf_op jit(solution)/shard_map/ppermute | solution.py:18
  191.2 8.4 %collective-permute-start.4 = (f32[32,128]{1,0:T(8,128)S(1)}, f32[32,128]{1,0:T(8,128)S(1)}, u32[]{:S(2)}, u32[]{:S(2)}) collective-permute-start(f32[32,128]{1,0:T(8,128)S(1)} %get-tuple-element.23), channel_id=1, source_target_pairs={{255,0},{0,1},{1,2},{2,3},{3,4},{4,5},{5,6},{6,7},{7,8},{8,9},{9,1... | collective-permute-start | bytes 49160 | tf_op jit(solution)/shard_map/ppermute | solution.py:18

commit v3 on v2

--- a/solution.py
+++ b/solution.py
@@ -104,9 +104,10 @@
 
     tail = from_behind(spectrum[-EXTRA:], "band", 1)
     blocks = spectrum.reshape(bin_count, cell_dev, spectrum.shape[1])
-    heads = jnp.concatenate([tail[None], blocks[:-1, -EXTRA:]], 0)
-    sent = jnp.concatenate([heads, blocks], 1).reshape(-1, spectrum.shape[1])
-    field = lax.all_to_all(sent, "bin", split_axis=0, concat_axis=1, tiled=True)
+    heads = jnp.concatenate([tail[None], blocks[:-1, -EXTRA:]], 0).reshape(-1, spectrum.shape[1])
+    body = lax.all_to_all(spectrum, "bin", split_axis=0, concat_axis=1, tiled=True)
+    head = lax.all_to_all(heads, "bin", split_axis=0, concat_axis=1, tiled=True)
+    field = jnp.concatenate([head, body], 0)
     prev = jnp.zeros((1, bins), jnp.float32)
     mask = ext_mask
     for step in range(STEPS):

time: 205 us -> 196 us (0.956)
  starting transfers between devices: 53.2 us -> 46 us
  waiting for transfers between devices: 96.6 us -> 102 us
  matrix products: 17.1 us -> 13.7 us
    all_to_all x1 -> x2, waiting for transfers between devices: 1.56 us -> 14.8 us  [the longest x1 8.04 us: per_device(): lax.all_to_all(spectrum, 'bin', split_axis=0, concat_axis=1, tiled=True)]
    ppermute x4, waiting for transfers between devices: 95 us -> 86.8 us  [shifted(): return lax.ppermute(block, axis, route)]
    ppermute x4, starting transfers between devices: 33 us -> 24.8 us  [shifted(): return lax.ppermute(block, axis, route)]
    all_to_all x1 -> x2, starting transfers between devices: 8.51 us -> 12.9 us  [the longest x1 8.33 us: per_device(): head = lax.all_to_all(heads, 'bin', split_axis=0, concat_axis=1, tiled=True)]
    all_to_all x1, starting transfers between devices: 7.85 us -> 4.44 us  [per_device(): lax.all_to_all(field, 'bin', split_axis=1, concat_axis=0, tiled=True)]
    dot_general x2, matrix products: 8.84 us -> 5.44 us  [sources(): other = jnp.dot(rounded, source_b, preferred_element_type=jnp.float32)]
    reshape x0 -> x1, local copies, waits for them, and re-layouts: none -> 3.29 us  [per_device(): blocks = spectrum.reshape(bin_count, cell_dev, spectrum.shape[1])]
    slice x2, local copies, waits for them, and re-layouts: 3.68 us -> 0.47 us  [per_device(): blocks[:-1, -EXTRA:]]
  transfers between devices with their start and end apart: 7 -> 8, of which waited for: 4 -> 6; matrix products, arithmetic and copies ran while one was open for 6% -> 8% of each run, Pallas kernels for 0% -> 0%
where the time goes in v3:
time: 196 us; the launch traced here: 195 us
  waiting for transfers between devices  102 us (52%)
  starting transfers between devices  46 us (23%)
  local copies, waits for them, and re-layouts  24 us (12%)
  matrix products  13.7 us (7%)
  other arithmetic  9.09 us (5%)
    ppermute x4, waiting for transfers between devices, shifted(): return lax.ppermute(block, axis, route)  86.8 us
    ppermute x4, starting transfers between devices, shifted(): return lax.ppermute(block, axis, route)  24.8 us
    all_to_all x1, starting transfers between devices, per_device(): head = lax.all_to_all(heads, 'bin', split_axis=0, concat_axis=1, tiled=True)  8.33 us
    all_to_all x1, waiting for transfers between devices, per_device(): lax.all_to_all(spectrum, 'bin', split_axis=0, concat_axis=1, tiled=True)  8.04 us
    all_to_all x1, waiting for transfers between devices, per_device(): head = lax.all_to_all(heads, 'bin', split_axis=0, concat_axis=1, tiled=True)  6.78 us
    dot_general x2, matrix products, sources(): other = jnp.dot(rounded, source_b, preferred_element_type=jnp.float32)  5.44 us
    dot_general x2, matrix products, sources(): gain = jnp.dot(rounded, source_a, preferred_element_type=jnp.float32)  5.18 us
    all_to_all x1, starting transfers between devices, per_device(): lax.all_to_all(spectrum, 'bin', split_axis=0, concat_axis=1, tiled=True)  4.57 us
  transfers between devices with their start and end apart: 8, of which 6 were waited for; matrix products, arithmetic and copies ran while one was open for 8% of the time, Pallas kernels for 0%

profile of v3, /device:TPU:88, one launch (start us, length us, event | category | flops | bytes accessed | tf_op | source)
XLA Modules:
  0.0 195.4 jit_solution(12530463510146233651)
XLA Ops:
  0.6 1.0 slice.129
  1.6 0.1 copy.52
  1.7 3.8 %collective-permute-start = (f32[8,72]{1,0:T(8,128)S(1)}, f32[8,72]{1,0:T(8,128)S(1)}, u32[]{:S(2)}, u32[]{:S(2)}) collective-permute-start(f32[8,72]{1,0:T(8,128)S(1)} %copy.52), channel_id=1, source_target_pairs={{0,16},{16,32},{32,48},{48,64},{64,80},{80,96},{96,112},{112,128},... | collective-permute-start | bytes 6920 | tf_op jit(solution)/shard_map/ppermute | solution.py:24
  5.5 3.1 %copy.55 = f32[9,8,16,512]{3,2,1,0:T(8,128)S(1)} copy(f32[9,8,16,512]{3,1,2,0:T(8,128)} %bitcast.35) | data formatting | bytes 4718592
  8.6 0.2 slice.169
  8.8 0.3 copy.44
  9.1 0.6 pad_maximum_fusion.5
  9.7 8.3 %all-to-all-start = ((f32[16,8,72]{2,1,0:T(8,128)}), f32[16,8,72]{2,1,0:T(8,128)S(1)}, u32[]{:S(2)}, u32[]{:S(2)}) async-start(f32[16,8,72]{2,1,0:T(8,128)} %pad_maximum_fusion.5), calls=%async_computation | async-start | bytes 131072 | tf_op jit(solution)/shard_map/all_to_all | solution.py:109
  18.0 3.3 %copy.57 = f32[9,16,8,512]{3,2,0,1:T(8,128)} copy(f32[9,16,8,512]{3,2,1,0:T(8,128)} %bitcast.36) | data formatting | bytes 4718592 | tf_op jit(solution)/shard_map/reshape | solution.py:106
  21.3 6.8 %all-to-all-done = f32[16,8,72]{2,1,0:T(8,128)S(1)} async-done(((f32[16,8,72]{2,1,0:T(8,128)}), f32[16,8,72]{2,1,0:T(8,128)S(1)}, u32[]{:S(2)}, u32[]{:S(2)}) %all-to-all-start) | async-done | bytes 36896 | tf_op jit(solution)/shard_map/all_to_all | solution.py:109
  28.1 4.6 %all-to-all-start.1 = ((f32[16,512,72]{1,2,0:T(8,128)}), f32[16,512,72]{1,2,0:T(8,128)}, u32[]{:S(2)}, u32[]{:S(2)}) async-start(f32[16,512,72]{1,2,0:T(8,128)} %bitcast.37), calls=%async_computation.1 | async-start | bytes 4718592 | tf_op jit(solution)/shard_map/all_to_all | solution.py:108
  32.7 7.8 %collective-permute-start.1 = (f32[33,128]{1,0:T(8,128)S(1)}, f32[33,128]{1,0:T(8,128)S(1)}, u32[]{:S(2)}, u32[]{:S(2)}) collective-permute-start(f32[33,128]{1,0:T(8,128)S(1)} %get-tuple-element.28), channel_id=1, source_target_pairs={{1,0},{2,1},{3,2},{4,3},{5,4},{6,5},{7,6},{8,7},{9,8},{10,9},{11,1... | collective-permute-start | bytes 50696 | tf_op jit(solution)/shard_map/ppermute | solution.py:18
  40.5 0.1 slice.131
  40.6 0.8 slice.127
  41.3 0.1 compare_and_fusion
  41.4 0.1 compare_and_fusion.3
  41.5 0.8 broadcast_multiply_fusion
  42.4 0.1 convert_reduce_fusion
  42.5 0.1 broadcast_multiply_fusion.1
  42.6 31.2 %collective-permute-done.1 = f32[33,128]{1,0:T(8,128)S(1)} collective-permute-done((f32[33,128]{1,0:T(8,128)S(1)}, f32[33,128]{1,0:T(8,128)S(1)}, u32[]{:S(2)}, u32[]{:S(2)}) %collective-permute-start.1) | collective-permute-done | bytes 16928 | tf_op jit(solution)/shard_map/ppermute | solution.py:18
  73.8 0.2 maximum_reduce_fusion
  74.0 0.1 copy.48
  74.1 0.1 reshape.103
  74.2 0.1 fusion.71
  74.3 0.3 fusion.29
  74.6 0.1 mul.233
  74.7 1.6 gather_fusion
  76.3 0.1 select_bitcast_fusion
  76.5 0.3 fusion.21
  76.8 0.1 all_to_all.40
  76.9 8.0 %all-to-all-done.1 = f32[16,512,72]{1,2,0:T(8,128)} async-done(((f32[16,512,72]{1,2,0:T(8,128)}), f32[16,512,72]{1,2,0:T(8,128)}, u32[]{:S(2)}, u32[]{:S(2)}) %all-to-all-start.1) | async-done | bytes 2359328 | tf_op jit(solution)/shard_map/all_to_all | solution.py:108
  84.9 3.0 %copy.47 = f32[512,1152]{1,0:T(8,128)} copy(f32[512,1152]{0,1:T(8,128)} %bitcast.3) | data formatting | bytes 4718592 | tf_op jit(solution)/shard_map/all_to_all | solution.py:108
  88.0 2.0 %fusion.10 = f32[519,1152]{1,0:T(8,128)S(1)} fusion(f32[8,1152]{1,0:T(8,128)S(1)} %all_to_all.40, f32[512,1152]{1,0:T(8,128)} %copy.47), kind=kLoop, calls=%fused_computation.16 | loop fusion | flops 597888 | bytes 4787712 | tf_op jit(solution)/shard_map/concatenate | solution.py:110
  90.0 0.4 copy-done.1
  90.4 2.5 %fusion.68 = (bf16[520,1152]{1,0:T(8,128)(2,1)S(1)}, f32[520,1152]{1,0:T(8,128)}) fusion(f32[519,1152]{1,0:T(8,128)S(1)} %fusion.10, f32[1152]{0:T(1024)S(1)} %get-tuple-element.31, f32[520]{0:T(1024)S(1)} %get-tuple-element.3, f32[1152]{0:T(1024)S(1)} %get-tuple-element.32, f32[520]{0:T(1024)S(1)} %get-tuple-element.2, f32[1152]{0:T(1024)S(1)} %copy-done.9, ...), kind=kLoop, calls=%fused_computation.126 | loop fusion | flops 6589440 | bytes 8402016 | tf_op jit(solution)/shard_map/convert_element_type | solution.py:116
  92.9 1.0 copy-done.4
  93.9 0.5 fusion.14
  94.4 0.2 fusion.17
  94.6 0.1 fusion.41
  94.7 0.2 slice_reduce_fusion.1
  94.9 0.1 copy.49
  95.0 1.0 gather_fusion.1
  96.0 0.1 select_bitcast_fusion.1
  96.2 0.3 fusion.23
  96.5 3.3 %fusion.75 = f32[520,1152]{1,0:T(8,128)S(1)} fusion(bf16[520,1152]{1,0:T(8,128)(2,1)} %copy-done.4, bf16[1152,1152]{1,0:T(8,128)(2,1)S(1)} %copy-done), kind=kOutput, calls=%fused_computation.132 | convolution fusion | flops 1380188160 | bytes 6248448 | tf_op jit(solution)/shard_map/dot_general | solution.py:43
  99.9 2.0 %fusion.6 = f32[520,1152]{1,0:T(8,128)S(1)} fusion(f32[520,1152]{1,0:T(8,128)S(1)} %copy-done.3, f32[520,1152]{1,0:T(8,128)S(1)} %fusion.75, bf16[520,1152]{1,0:T(8,128)(2,1)S(1)} %copy-done.5, bf16[1152,1152]{1,0:T(8,128)(2,1)S(1)} %copy-done.10, f32[520]{0:T(1024)S(1)} %get-tuple-element.12), kind=kOutput, calls=%fused_computation.12 | convolution fusion | flops 1384381440 | bytes 11042848 | tf_op jit(solution)/shard_map/dot_general | solution.py:44
  101.9 1.0 fusion.13
  103.0 1.9 fusion.65
  104.8 3.4 %fusion.9 = f32[512,1152]{1,0:T(8,128)} fusion(f32[512,1152]{1,0:T(8,128)S(1)} %fusion.13, f32[512,1152]{1,0:T(8,128)S(1)} %fusion.65, bf16[1152,1152]{1,0:T(8,128)(2,1)S(1)} %copy-done.10, f32[512]{0:T(512)S(1)} %get-tuple-element.29), kind=kOutput, calls=%fused_computation.15 | convolution fusion | flops 1363673088 | bytes 9734144 | tf_op jit(solution)/shard_map/dot_general | solution.py:44
  108.3 3.1 %copy.50 = f32[512,1152]{0,1:T(8,128)} copy(f32[512,1152]{1,0:T(8,128)} %fusion.9) | data formatting | bytes 4718592 | tf_op jit(solution)/shard_map/add | solution.py:118
  111.3 4.4 %all-to-all-start.2 = ((f32[512,16,72]{0,2,1:T(8,128)}), f32[512,16,72]{0,2,1:T(8,128)}, u32[]{:S(2)}, u32[]{:S(2)}) async-start(f32[512,16,72]{0,2,1:T(8,128)} %bitcast.38), calls=%async_computation.2 | async-start | bytes 4718592 | tf_op jit(solution)/shard_map/all_to_all | solution.py:134
  115.8 0.1 reshape.104
  115.9 17.0 %collective-permute-start.2 = (f32[1,128]{1,0:T(1,128)S(1)}, f32[1,128]{1,0:T(1,128)S(1)}, u32[]{:S(2)}, u32[]{:S(2)}) collective-permute-start(f32[1,128]{1,0:T(1,128)S(1)} %get-tuple-element.25), channel_id=1, source_target_pairs={{1,0},{2,1},{3,2},{4,3},{5,4},{6,5},{7,6},{8,7},{9,8},{10,9},{11,1... | collective-permute-start | bytes 1544 | tf_op jit(solution)/shard_map/ppermute | solution.py:18
  132.9 0.1 fusion.70
  133.0 2.1 %fusion.62 = f32[512,128]{1,0:T(8,128)S(1)} fusion(bf16[1152,128]{1,0:T(8,128)(2,1)S(1)} %copy-done.7, f32[512,1152]{1,0:T(8,128)} %copy-done.2), kind=kOutput, calls=%fused_computation.121 | convolution fusion | flops 151584768 | bytes 2916352 | tf_op jit(solution)/shard_map/dot_general | solution.py:46
  135.2 0.3 fusion.26
  135.4 0.1 mul.257
  135.5 11.5 %collective-permute-done.2 = f32[1,128]{1,0:T(1,128)S(1)} collective-permute-done((f32[1,128]{1,0:T(1,128)S(1)}, f32[1,128]{1,0:T(1,128)S(1)}, u32[]{:S(2)}, u32[]{:S(2)}) %collective-permute-start.2) | collective-permute-done | bytes 544 | tf_op jit(solution)/shard_map/ppermute | solution.py:18
  147.1 35.8 %collective-permute-done.3 = f32[1,128]{1,0:T(1,128)S(1)} collective-permute-done((f32[1,128]{1,0:T(1,128)S(1)}, f32[1,128]{1,0:T(1,128)S(1)}, u32[]{:S(2)}, u32[]{:S(2)}) %collective-permute-start.3) | collective-permute-done | bytes 544 | tf_op jit(solution)/shard_map/ppermute | solution.py:18
  182.8 0.2 fusion.19
  183.1 0.1 collective-permute-start.4
  183.2 8.3 %collective-permute-done.4 = f32[32,128]{1,0:T(8,128)S(1)} collective-permute-done((f32[32,128]{1,0:T(8,128)S(1)}, f32[32,128]{1,0:T(8,128)S(1)}, u32[]{:S(2)}, u32[]{:S(2)}) %collective-permute-start.4) | collective-permute-done | bytes 16416 | tf_op jit(solution)/shard_map/ppermute | solution.py:18
  191.4 0.6 pad_maximum_fusion.11
  192.1 3.4 %copy.54 = f32[16,9,8,512]{3,2,0,1:T(8,128)} copy(f32[16,9,8,512]{3,2,1,0:T(8,128)} %bitcast.15) | data formatting | bytes 4718592 | tf_op jit(solution)/shard_map/all_to_all | solution.py:134
  (37 shorter events, 0.2 us)
Async XLA Ops:
  0.6 95.9 %copy-start = (bf16[1152,1152]{1,0:T(8,128)(2,1)S(1)}, bf16[1152,1152]{1,0:T(8,128)(2,1)}, u32[]{:S(2)}) copy-start(bf16[1152,1152]{1,0:T(8,128)(2,1)} %param.10) | copy-start | bytes 7962628
  1.7 7.4 %collective-permute-start = (f32[8,72]{1,0:T(8,128)S(1)}, f32[8,72]{1,0:T(8,128)S(1)}, u32[]{:S(2)}, u32[]{:S(2)}) collective-permute-start(f32[8,72]{1,0:T(8,128)S(1)} %copy.52), channel_id=1, source_target_pairs={{0,16},{16,32},{32,48},{48,64},{64,80},{80,96},{96,112},{112,128},... | collective-permute-start | bytes 6920 | tf_op jit(solution)/shard_map/ppermute | solution.py:24
  9.7 18.4 %all-to-all-start = ((f32[16,8,72]{2,1,0:T(8,128)}), f32[16,8,72]{2,1,0:T(8,128)S(1)}, u32[]{:S(2)}, u32[]{:S(2)}) async-start(f32[16,8,72]{2,1,0:T(8,128)} %pad_maximum_fusion.5), calls=%async_computation | async-start | bytes 131072 | tf_op jit(solution)/shard_map/all_to_all | solution.py:109
  28.1 4.6 %copy-start.8 = (f32[64,128]{1,0:T(8,128)S(1)}, f32[64,128]{1,0:T(8,128)}, u32[]{:S(2)}) copy-start(f32[64,128]{1,0:T(8,128)} %param.9) | copy-start | bytes 98308
  28.1 12.4 %copy-start.6 = (s32[131072]{0:T(1024)S(1)}, s32[131072]{0:T(1024)}, u32[]{:S(2)}) copy-start(s32[131072]{0:T(1024)} %param.14) | copy-start | bytes 1572868
  28.1 56.8 %all-to-all-start.1 = ((f32[16,512,72]{1,2,0:T(8,128)}), f32[16,512,72]{1,2,0:T(8,128)}, u32[]{:S(2)}, u32[]{:S(2)}) async-start(f32[16,512,72]{1,2,0:T(8,128)} %bitcast.37), calls=%async_computation.1 | async-start | bytes 4718592 | tf_op jit(solution)/shard_map/all_to_all | solution.py:108
  32.7 41.1 %collective-permute-start.1 = (f32[33,128]{1,0:T(8,128)S(1)}, f32[33,128]{1,0:T(8,128)S(1)}, u32[]{:S(2)}, u32[]{:S(2)}) collective-permute-start(f32[33,128]{1,0:T(8,128)S(1)} %get-tuple-element.28), channel_id=1, source_target_pairs={{1,0},{2,1},{3,2},{4,3},{5,4},{6,5},{7,6},{8,7},{9,8},{10,9},{11,1... | collective-permute-start | bytes 50696 | tf_op jit(solution)/shard_map/ppermute | solution.py:18
  88.0 2.4 %copy-start.1 = (f32[512,1152]{1,0:T(8,128)S(1)}, f32[512,1152]{1,0:T(8,128)}, u32[]{:S(2)}) copy-start(f32[512,1152]{1,0:T(8,128)} %copy.47) | copy-start | bytes 7077892
  88.0 2.4 %copy-start.9 = (f32[1152]{0:T(1024)S(1)}, f32[1152]{0:T(1024)}, u32[]{:S(2)}) copy-start(f32[1152]{0:T(1024)} %param.13) | copy-start | bytes 13828
  90.4 3.5 %copy-start.7 = (bf16[1152,128]{1,0:T(8,128)(2,1)S(1)}, bf16[1152,128]{1,0:T(8,128)(2,1)}, u32[]{:S(2)}) copy-start(bf16[1152,128]{1,0:T(8,128)(2,1)} %param.12) | copy-start | bytes 884740
  92.9 1.0 copy-start.4
  96.5 3.4 %copy-start.3 = (f32[520,1152]{1,0:T(8,128)S(1)}, f32[520,1152]{1,0:T(8,128)}, u32[]{:S(2)}) copy-start(f32[520,1152]{1,0:T(8,128)} %get-tuple-element.15) | copy-start | bytes 7188484
  96.5 3.4 %copy-start.5 = (bf16[520,1152]{1,0:T(8,128)(2,1)S(1)}, bf16[520,1152]{1,0:T(8,128)(2,1)}, u32[]{:S(2)}) copy-start(bf16[520,1152]{1,0:T(8,128)(2,1)} %copy-done.4) | copy-start | bytes 3594244
  96.5 3.4 %copy-start.10 = (bf16[1152,1152]{1,0:T(8,128)(2,1)S(1)}, bf16[1152,1152]{1,0:T(8,128)(2,1)}, u32[]{:S(2)}) copy-start(bf16[1152,1152]{1,0:T(8,128)(2,1)} %param.11) | copy-start | bytes 7962628
  103.0 1.9 copy-start.2
  111.3 80.7 %all-to-all-start.2 = ((f32[512,16,72]{0,2,1:T(8,128)}), f32[512,16,72]{0,2,1:T(8,128)}, u32[]{:S(2)}, u32[]{:S(2)}) async-start(f32[512,16,72]{0,2,1:T(8,128)} %bitcast.38), calls=%async_computation.2 | async-start | bytes 4718592 | tf_op jit(solution)/shard_map/all_to_all | solution.py:134
  115.9 31.2 %collective-permute-start.2 = (f32[1,128]{1,0:T(1,128)S(1)}, f32[1,128]{1,0:T(1,128)S(1)}, u32[]{:S(2)}, u32[]{:S(2)}) collective-permute-start(f32[1,128]{1,0:T(1,128)S(1)} %get-tuple-element.25), channel_id=1, source_target_pairs={{1,0},{2,1},{3,2},{4,3},{5,4},{6,5},{7,6},{8,7},{9,8},{10,9},{11,1... | collective-permute-start | bytes 1544 | tf_op jit(solution)/shard_map/ppermute | solution.py:18
  132.9 50.0 %collective-permute-start.3 = (f32[1,128]{1,0:T(1,128)S(1)}, f32[1,128]{1,0:T(1,128)S(1)}, u32[]{:S(2)}, u32[]{:S(2)}) collective-permute-start(f32[1,128]{1,0:T(1,128)S(1)} %get-tuple-element.26), channel_id=1, source_target_pairs={{255,0},{0,1},{1,2},{2,3},{3,4},{4,5},{5,6},{6,7},{7,8},{8,9},{9,1... | collective-permute-start | bytes 1544 | tf_op jit(solution)/shard_map/ppermute | solution.py:18
  183.1 8.4 %collective-permute-start.4 = (f32[32,128]{1,0:T(8,128)S(1)}, f32[32,128]{1,0:T(8,128)S(1)}, u32[]{:S(2)}, u32[]{:S(2)}) collective-permute-start(f32[32,128]{1,0:T(8,128)S(1)} %get-tuple-element.23), channel_id=1, source_target_pairs={{255,0},{0,1},{1,2},{2,3},{3,4},{4,5},{5,6},{6,7},{7,8},{8,9},{9,1... | collective-permute-start | bytes 49160 | tf_op jit(solution)/shard_map/ppermute | solution.py:18

commit v4 on v2

--- a/solution.py
+++ b/solution.py
@@ -102,11 +102,18 @@
     table = jnp.stack([own[:, 0], own[:, LEVELS]])
     current = jnp.take(table, ext_where, axis=1)
 
-    tail = from_behind(spectrum[-EXTRA:], "band", 1)
-    blocks = spectrum.reshape(bin_count, cell_dev, spectrum.shape[1])
-    heads = jnp.concatenate([tail[None], blocks[:-1, -EXTRA:]], 0)
-    sent = jnp.concatenate([heads, blocks], 1).reshape(-1, spectrum.shape[1])
-    field = lax.all_to_all(sent, "bin", split_axis=0, concat_axis=1, tiled=True)
+    width = spectrum.shape[1]
+    tail = from_behind(spectrum[-2:], "band", 1)
+    before = [tail] + [spectrum[j * cell_dev - 2 : j * cell_dev] for j in range(1, bin_count)]
+    heads = jnp.stack([h[::-1] for h in before]).reshape(bin_count, 2 * width)
+    heads = jnp.pad(heads, ((0, 0), (0, cell_dev - 2 * width)))
+    slab = jnp.pad(heads[:, :, None], ((0, 0), (0, 0), (0, 7)))
+    sent = jnp.concatenate([spectrum.reshape(bin_count, cell_dev, width), slab], 2)
+    got = lax.all_to_all(sent, "bin", split_axis=0, concat_axis=0, tiled=True)
+    body = got[:, :, :width].transpose(1, 0, 2).reshape(cell_dev, bins)
+    head = got[:, : 2 * width, width].reshape(bin_count, 2, width).transpose(1, 0, 2)
+    head = head.reshape(2, bins)[::-1]
+    field = jnp.concatenate([jnp.zeros((EXTRA - 2, bins), jnp.float32), head, body], 0)
     prev = jnp.zeros((1, bins), jnp.float32)
     mask = ext_mask
     for step in range(STEPS):

time: 205 us -> 204 us (level)
  starting transfers between devices: 53.2 us -> 34.4 us
  waiting for transfers between devices: 96.6 us -> 108 us
  local copies, waits for them, and re-layouts: 26 us -> 33.6 us
  matrix products: 17.1 us -> 13.7 us
    ppermute x4, starting transfers between devices: 33 us -> 14.5 us  [shifted(): return lax.ppermute(block, axis, route)]
    ppermute x4, waiting for transfers between devices: 95 us -> 104 us  [shifted(): return lax.ppermute(block, axis, route)]
    all_to_all x1 -> x0, local copies, waits for them, and re-layouts: 3.43 us -> none  [per_device(): field = lax.all_to_all(sent, 'bin', split_axis=0, concat_axis=1, tiled=True)]
    dot_general x2, matrix products: 8.84 us -> 5.44 us  [sources(): other = jnp.dot(rounded, source_b, preferred_element_type=jnp.float32)]
    reshape x0 -> x2, local copies, waits for them, and re-layouts: none -> 3.17 us  [the longest x1 3.08 us: per_device(): body = got[:, :, :width].transpose(1, 0, 2).reshape(cell_dev, bins)]
    concatenate x1 -> x2, other arithmetic: 0.83 us -> 3.93 us  [the longest x1 2.04 us: per_device(): jnp.concatenate([jnp.zeros((EXTRA - 2, bins), jnp.float32), head, body], 0)]
    rev x0 -> x33, local copies, waits for them, and re-layouts: none -> 2.8 us  [the longest x32 2.55 us: per_device(): heads = jnp.stack([h[::-1] for h in before]).reshape(bin_count, 2 * width)]
    unnamed x17 -> x23, local copies, waits for them, and re-layouts: 3.81 us -> 5.85 us
  transfers between devices with their start and end apart: 7 -> 7, of which waited for: 4 -> 5; matrix products, arithmetic and copies ran while one was open for 6% -> 8% of each run, Pallas kernels for 0% -> 0%
where the time goes in v4:
time: 204 us; the launch traced here: 201 us
  waiting for transfers between devices  108 us (53%)
  starting transfers between devices  34.4 us (17%)
  local copies, waits for them, and re-layouts  33.6 us (16%)
  matrix products  13.7 us (7%)
  other arithmetic  11 us (5%)
    ppermute x4, waiting for transfers between devices, shifted(): return lax.ppermute(block, axis, route)  104 us
    ppermute x4, starting transfers between devices, shifted(): return lax.ppermute(block, axis, route)  14.5 us
    all_to_all x1, starting transfers between devices, per_device(): got = lax.all_to_all(sent, 'bin', split_axis=0, concat_axis=0, tiled=True)  8.51 us
    all_to_all x1, starting transfers between devices, per_device(): lax.all_to_all(field, 'bin', split_axis=1, concat_axis=0, tiled=True)  7.59 us
    unnamed x23, local copies, waits for them, and re-layouts  5.85 us
    dot_general x2, matrix products, sources(): other = jnp.dot(rounded, source_b, preferred_element_type=jnp.float32)  5.44 us
    dot_general x2, matrix products, sources(): gain = jnp.dot(rounded, source_a, preferred_element_type=jnp.float32)  5.18 us
  transfers between devices with their start and end apart: 7, of which 5 were waited for; matrix products, arithmetic and copies ran while one was open for 8% of the time, Pallas kernels for 0%

profile of v4, /device:TPU:88, one launch (start us, length us, event | category | flops | bytes accessed | tf_op | source)
XLA Modules:
  0.0 201.3 jit_solution(12188754331530332890)
XLA Ops:
  0.6 1.4 fusion.69
  2.1 3.8 %collective-permute-start = (f32[2,72]{0,1:T(8,128)S(1)}, f32[2,72]{0,1:T(8,128)S(1)}, u32[]{:S(2)}, u32[]{:S(2)}) collective-permute-start(f32[2,72]{0,1:T(8,128)S(1)} %get-tuple-element.33), channel_id=1, source_target_pairs={{0,16},{16,32},{32,48},{48,64},{64,80},{80,96},{96,112},{112,128},... | collective-permute-start | bytes 1736 | tf_op jit(solution)/shard_map/ppermute | solution.py:24
  6.4 0.1 copy.92
  6.7 0.1 copy.93
  6.9 0.1 copy.94
  7.2 0.1 copy.95
  7.4 0.1 copy.96
  8.4 0.1 copy.100
  9.6 4.5 %copy.113 = f32[9,8,16,512]{3,2,1,0:T(8,128)} copy(f32[9,8,16,512]{3,1,2,0:T(8,128)} %bitcast.37) | data formatting | bytes 4718592
  14.4 1.9 select_maximum_fusion
  16.3 3.0 %copy.105 = f32[16,512,80]{1,2,0:T(8,128)} copy(f32[16,512,80]{1,0,2:T(8,128)S(1)} %select_maximum_fusion) | data formatting | bytes 5242880 | tf_op jit(solution)/shard_map/concatenate | solution.py:111
  19.3 8.5 %all-to-all-start = ((f32[16,512,80]{1,2,0:T(8,128)}), f32[16,512,80]{1,2,0:T(8,128)}, u32[]{:S(2)}, u32[]{:S(2)}) async-start(f32[16,512,80]{1,2,0:T(8,128)} %copy.105), calls=%async_computation | async-start | bytes 5242880 | tf_op jit(solution)/shard_map/all_to_all | solution.py:112
  27.9 7.4 %collective-permute-start.1 = (f32[33,128]{1,0:T(8,128)S(1)}, f32[33,128]{1,0:T(8,128)S(1)}, u32[]{:S(2)}, u32[]{:S(2)}) collective-permute-start(f32[33,128]{1,0:T(8,128)S(1)} %get-tuple-element.44), channel_id=1, source_target_pairs={{1,0},{2,1},{3,2},{4,3},{5,4},{6,5},{7,6},{8,7},{9,8},{10,9},{11,1... | collective-permute-start | bytes 50696 | tf_op jit(solution)/shard_map/ppermute | solution.py:18
  35.4 0.8 slice.175
  36.1 0.1 compare_and_fusion
  36.3 0.8 broadcast_multiply_fusion
  37.2 0.1 convert_reduce_fusion
  37.4 49.5 %collective-permute-done.1 = f32[33,128]{1,0:T(8,128)S(1)} collective-permute-done((f32[33,128]{1,0:T(8,128)S(1)}, f32[33,128]{1,0:T(8,128)S(1)}, u32[]{:S(2)}, u32[]{:S(2)}) %collective-permute-start.1) | collective-permute-done | bytes 16928 | tf_op jit(solution)/shard_map/ppermute | solution.py:18
  86.9 0.2 maximum_reduce_fusion
  87.1 0.1 copy.108
  87.2 0.1 reshape.136
  87.3 0.1 fusion.71
  87.5 0.3 fusion.28
  87.7 0.1 mul.233
  87.8 1.6 gather_fusion
  89.4 0.1 select_bitcast_fusion
  89.6 0.3 fusion.20
  89.9 3.2 %all-to-all-done = f32[16,512,80]{1,2,0:T(8,128)} async-done(((f32[16,512,80]{1,2,0:T(8,128)}), f32[16,512,80]{1,2,0:T(8,128)}, u32[]{:S(2)}, u32[]{:S(2)}) %all-to-all-start) | async-done | bytes 2621472 | tf_op jit(solution)/shard_map/all_to_all | solution.py:112
  93.1 3.3 %slice.234 = f32[16,512,72]{1,2,0:T(8,128)} slice(f32[16,512,80]{1,2,0:T(8,128)} %all-to-all-done), slice={[0:16], [0:512], [0:72]} | slice | bytes 4718592 | tf_op jit(solution)/shard_map/slice | solution.py:113
  96.4 3.1 %copy.107 = f32[512,1152]{1,0:T(8,128)} copy(f32[512,1152]{0,1:T(8,128)} %bitcast.36) | data formatting | bytes 4718592 | tf_op jit(solution)/shard_map/reshape | solution.py:113
  99.4 0.9 slice_reduce_fusion.2
  100.5 0.1 reshape.134
  100.6 0.2 rev.67
  100.9 2.0 %pad_maximum_fusion = f32[520,1152]{1,0:T(8,128)S(1)} fusion(f32[512,1152]{1,0:T(8,128)} %copy.107, f32[2,1152]{1,0:T(2,128)S(1)} %rev.67, f32[520]{0:T(1024)S(1)} %pad.37.clone), kind=kLoop, calls=%fused_computation.16 | loop fusion | flops 1198080 | bytes 4766752 | tf_op jit(solution)/shard_map/concatenate | solution.py:116
  102.9 0.3 copy-done.1
  103.2 3.0 %fusion.67 = (bf16[520,1152]{1,0:T(8,128)(2,1)S(1)}, f32[520,1152]{1,0:T(8,128)}) fusion(f32[519,1152]{1,0:T(8,128)S(1)} %bitcast.33, f32[1152]{0:T(1024)S(1)} %get-tuple-element.47, f32[520]{0:T(1024)S(1)} %get-tuple-element.3, f32[1152]{0:T(1024)S(1)} %get-tuple-element.48, f32[520]{0:T(1024)S(1)} %get-tuple-element.2, f32[1152]{0:T(1024)S(1)} %copy-done.9, ...), kind=kLoop, calls=%fused_computation.126 | loop fusion | flops 7188480 | bytes 8376448 | tf_op jit(solution)/shard_map/convert_element_type | solution.py:122
  106.3 1.0 copy-done.4
  107.3 0.5 fusion.13
  107.8 0.2 fusion.16
  108.0 0.1 fusion.40
  108.1 0.2 slice_reduce_fusion.1
  108.3 0.1 copy.109
  108.4 1.0 gather_fusion.1
  109.5 0.1 select_bitcast_fusion.1
  109.6 0.3 fusion.22
  109.9 3.3 %fusion.75 = f32[520,1152]{1,0:T(8,128)S(1)} fusion(bf16[520,1152]{1,0:T(8,128)(2,1)} %copy-done.4, bf16[1152,1152]{1,0:T(8,128)(2,1)S(1)} %copy-done), kind=kOutput, calls=%fused_computation.133 | convolution fusion | flops 1380188160 | bytes 6248448 | tf_op jit(solution)/shard_map/dot_general | solution.py:43
  113.3 2.0 %fusion.6 = f32[520,1152]{1,0:T(8,128)S(1)} fusion(f32[520,1152]{1,0:T(8,128)S(1)} %copy-done.3, f32[520,1152]{1,0:T(8,128)S(1)} %fusion.75, bf16[520,1152]{1,0:T(8,128)(2,1)S(1)} %copy-done.5, bf16[1152,1152]{1,0:T(8,128)(2,1)S(1)} %copy-done.10, f32[520]{0:T(1024)S(1)} %get-tuple-element.12), kind=kOutput, calls=%fused_computation.10 | convolution fusion | flops 1384381440 | bytes 11042848 | tf_op jit(solution)/shard_map/dot_general | solution.py:44
  115.3 1.0 fusion.12
  116.4 1.9 fusion.64
  118.3 3.4 %fusion.9 = f32[512,1152]{1,0:T(8,128)} fusion(f32[512,1152]{1,0:T(8,128)S(1)} %fusion.12, f32[512,1152]{1,0:T(8,128)S(1)} %fusion.64, bf16[1152,1152]{1,0:T(8,128)(2,1)S(1)} %copy-done.10, f32[512]{0:T(512)S(1)} %get-tuple-element.45), kind=kOutput, calls=%fused_computation.13 | convolution fusion | flops 1363673088 | bytes 9734144 | tf_op jit(solution)/shard_map/dot_general | solution.py:44
  121.7 3.1 %copy.110 = f32[512,1152]{0,1:T(8,128)} copy(f32[512,1152]{1,0:T(8,128)} %fusion.9) | data formatting | bytes 4718592 | tf_op jit(solution)/shard_map/add | solution.py:124
  124.7 7.6 %all-to-all-start.1 = ((f32[512,16,72]{0,2,1:T(8,128)}), f32[512,16,72]{0,2,1:T(8,128)}, u32[]{:S(2)}, u32[]{:S(2)}) async-start(f32[512,16,72]{0,2,1:T(8,128)} %bitcast.35), calls=%async_computation.1 | async-start | bytes 4718592 | tf_op jit(solution)/shard_map/all_to_all | solution.py:140
  132.3 0.1 reshape.137
  132.4 6.9 %collective-permute-start.2 = (f32[1,128]{1,0:T(1,128)S(1)}, f32[1,128]{1,0:T(1,128)S(1)}, u32[]{:S(2)}, u32[]{:S(2)}) collective-permute-start(f32[1,128]{1,0:T(1,128)S(1)} %get-tuple-element.41), channel_id=1, source_target_pairs={{1,0},{2,1},{3,2},{4,3},{5,4},{6,5},{7,6},{8,7},{9,8},{10,9},{11,1... | collective-permute-start | bytes 1544 | tf_op jit(solution)/shard_map/ppermute | solution.py:18
  139.4 0.1 fusion.70
  139.5 2.1 %fusion.61 = f32[512,128]{1,0:T(8,128)S(1)} fusion(bf16[1152,128]{1,0:T(8,128)(2,1)S(1)} %copy-done.7, f32[512,1152]{1,0:T(8,128)} %copy-done.2), kind=kOutput, calls=%fused_computation.121 | convolution fusion | flops 151584768 | bytes 2916352 | tf_op jit(solution)/shard_map/dot_general | solution.py:46
  141.7 0.3 fusion.25
  141.9 0.1 mul.257
  142.0 39.4 %collective-permute-done.2 = f32[1,128]{1,0:T(1,128)S(1)} collective-permute-done((f32[1,128]{1,0:T(1,128)S(1)}, f32[1,128]{1,0:T(1,128)S(1)}, u32[]{:S(2)}, u32[]{:S(2)}) %collective-permute-start.2) | collective-permute-done | bytes 544 | tf_op jit(solution)/shard_map/ppermute | solution.py:18
  181.4 7.3 %collective-permute-done.3 = f32[1,128]{1,0:T(1,128)S(1)} collective-permute-done((f32[1,128]{1,0:T(1,128)S(1)}, f32[1,128]{1,0:T(1,128)S(1)}, u32[]{:S(2)}, u32[]{:S(2)}) %collective-permute-start.3) | collective-permute-done | bytes 544 | tf_op jit(solution)/shard_map/ppermute | solution.py:18
  188.7 0.2 fusion.18
  189.0 8.3 %collective-permute-done.4 = f32[32,128]{1,0:T(8,128)S(1)} collective-permute-done((f32[32,128]{1,0:T(8,128)S(1)}, f32[32,128]{1,0:T(8,128)S(1)}, u32[]{:S(2)}, u32[]{:S(2)}) %collective-permute-start.4) | collective-permute-done | bytes 16416 | tf_op jit(solution)/shard_map/ppermute | solution.py:18
  197.3 0.6 pad_maximum_fusion.10
  197.9 3.4 %copy.112 = f32[16,9,8,512]{3,2,0,1:T(8,128)} copy(f32[16,9,8,512]{3,2,1,0:T(8,128)} %bitcast.13) | data formatting | bytes 4718592 | tf_op jit(solution)/shard_map/all_to_all | solution.py:140
  (88 shorter events, 4.0 us)
Async XLA Ops:
  0.6 109.3 %copy-start = (bf16[1152,1152]{1,0:T(8,128)(2,1)S(1)}, bf16[1152,1152]{1,0:T(8,128)(2,1)}, u32[]{:S(2)}) copy-start(bf16[1152,1152]{1,0:T(8,128)(2,1)} %param.10) | copy-start | bytes 7962628
  2.1 12.0 %collective-permute-start = (f32[2,72]{0,1:T(8,128)S(1)}, f32[2,72]{0,1:T(8,128)S(1)}, u32[]{:S(2)}, u32[]{:S(2)}) collective-permute-start(f32[2,72]{0,1:T(8,128)S(1)} %get-tuple-element.33), channel_id=1, source_target_pairs={{0,16},{16,32},{32,48},{48,64},{64,80},{80,96},{96,112},{112,128},... | collective-permute-start | bytes 1736 | tf_op jit(solution)/shard_map/ppermute | solution.py:24
  19.3 8.5 %copy-start.8 = (f32[64,128]{1,0:T(8,128)S(1)}, f32[64,128]{1,0:T(8,128)}, u32[]{:S(2)}) copy-start(f32[64,128]{1,0:T(8,128)} %param.9) | copy-start | bytes 98308
  19.3 16.0 %copy-start.6 = (s32[131072]{0:T(1024)S(1)}, s32[131072]{0:T(1024)}, u32[]{:S(2)}) copy-start(s32[131072]{0:T(1024)} %param.14) | copy-start | bytes 1572868
  19.3 73.7 %all-to-all-start = ((f32[16,512,80]{1,2,0:T(8,128)}), f32[16,512,80]{1,2,0:T(8,128)}, u32[]{:S(2)}, u32[]{:S(2)}) async-start(f32[16,512,80]{1,2,0:T(8,128)} %copy.105), calls=%async_computation | async-start | bytes 5242880 | tf_op jit(solution)/shard_map/all_to_all | solution.py:112
  27.9 59.0 %collective-permute-start.1 = (f32[33,128]{1,0:T(8,128)S(1)}, f32[33,128]{1,0:T(8,128)S(1)}, u32[]{:S(2)}, u32[]{:S(2)}) collective-permute-start(f32[33,128]{1,0:T(8,128)S(1)} %get-tuple-element.44), channel_id=1, source_target_pairs={{1,0},{2,1},{3,2},{4,3},{5,4},{6,5},{7,6},{8,7},{9,8},{10,9},{11,1... | collective-permute-start | bytes 50696 | tf_op jit(solution)/shard_map/ppermute | solution.py:18
  100.6 2.3 %copy-start.9 = (f32[1152]{0:T(1024)S(1)}, f32[1152]{0:T(1024)}, u32[]{:S(2)}) copy-start(f32[1152]{0:T(1024)} %param.13) | copy-start | bytes 13828
  100.8 2.4 %copy-start.1 = (f32[512,1152]{1,0:T(8,128)S(1)}, f32[512,1152]{1,0:T(8,128)}, u32[]{:S(2)}) copy-start(f32[512,1152]{1,0:T(8,128)} %copy.107) | copy-start | bytes 7077892
  103.2 4.1 %copy-start.7 = (bf16[1152,128]{1,0:T(8,128)(2,1)S(1)}, bf16[1152,128]{1,0:T(8,128)(2,1)}, u32[]{:S(2)}) copy-start(bf16[1152,128]{1,0:T(8,128)(2,1)} %param.12) | copy-start | bytes 884740
  106.3 1.0 copy-start.4
  109.9 3.4 %copy-start.3 = (f32[520,1152]{1,0:T(8,128)S(1)}, f32[520,1152]{1,0:T(8,128)}, u32[]{:S(2)}) copy-start(f32[520,1152]{1,0:T(8,128)} %get-tuple-element.15) | copy-start | bytes 7188484
  109.9 3.4 %copy-start.5 = (bf16[520,1152]{1,0:T(8,128)(2,1)S(1)}, bf16[520,1152]{1,0:T(8,128)(2,1)}, u32[]{:S(2)}) copy-start(bf16[520,1152]{1,0:T(8,128)(2,1)} %copy-done.4) | copy-start | bytes 3594244
  109.9 3.4 %copy-start.10 = (bf16[1152,1152]{1,0:T(8,128)(2,1)S(1)}, bf16[1152,1152]{1,0:T(8,128)(2,1)}, u32[]{:S(2)}) copy-start(bf16[1152,1152]{1,0:T(8,128)(2,1)} %param.11) | copy-start | bytes 7962628
  116.4 1.9 copy-start.2
  124.7 73.2 %all-to-all-start.1 = ((f32[512,16,72]{0,2,1:T(8,128)}), f32[512,16,72]{0,2,1:T(8,128)}, u32[]{:S(2)}, u32[]{:S(2)}) async-start(f32[512,16,72]{0,2,1:T(8,128)} %bitcast.35), calls=%async_computation.1 | async-start | bytes 4718592 | tf_op jit(solution)/shard_map/all_to_all | solution.py:140
  132.4 49.0 %collective-permute-start.2 = (f32[1,128]{1,0:T(1,128)S(1)}, f32[1,128]{1,0:T(1,128)S(1)}, u32[]{:S(2)}, u32[]{:S(2)}) collective-permute-start(f32[1,128]{1,0:T(1,128)S(1)} %get-tuple-element.41), channel_id=1, source_target_pairs={{1,0},{2,1},{3,2},{4,3},{5,4},{6,5},{7,6},{8,7},{9,8},{10,9},{11,1... | collective-permute-start | bytes 1544 | tf_op jit(solution)/shard_map/ppermute | solution.py:18
  139.4 49.3 %collective-permute-start.3 = (f32[1,128]{1,0:T(1,128)S(1)}, f32[1,128]{1,0:T(1,128)S(1)}, u32[]{:S(2)}, u32[]{:S(2)}) collective-permute-start(f32[1,128]{1,0:T(1,128)S(1)} %get-tuple-element.42), channel_id=1, source_target_pairs={{255,0},{0,1},{1,2},{2,3},{3,4},{4,5},{5,6},{6,7},{7,8},{8,9},{9,1... | collective-permute-start | bytes 1544 | tf_op jit(solution)/shard_map/ppermute | solution.py:18
  188.9 8.4 %collective-permute-start.4 = (f32[32,128]{1,0:T(8,128)S(1)}, f32[32,128]{1,0:T(8,128)S(1)}, u32[]{:S(2)}, u32[]{:S(2)}) collective-permute-start(f32[32,128]{1,0:T(8,128)S(1)} %get-tuple-element.39), channel_id=1, source_target_pairs={{255,0},{0,1},{1,2},{2,3},{3,4},{4,5},{5,6},{6,7},{7,8},{8,9},{9,1... | collective-permute-start | bytes 49160 | tf_op jit(solution)/shard_map/ppermute | solution.py:18

commit v5 on v3

--- a/solution.py
+++ b/solution.py
@@ -102,11 +102,15 @@
     table = jnp.stack([own[:, 0], own[:, LEVELS]])
     current = jnp.take(table, ext_where, axis=1)
 
-    tail = from_behind(spectrum[-EXTRA:], "band", 1)
-    blocks = spectrum.reshape(bin_count, cell_dev, spectrum.shape[1])
-    heads = jnp.concatenate([tail[None], blocks[:-1, -EXTRA:]], 0).reshape(-1, spectrum.shape[1])
-    body = lax.all_to_all(spectrum, "bin", split_axis=0, concat_axis=1, tiled=True)
-    head = lax.all_to_all(heads, "bin", split_axis=0, concat_axis=1, tiled=True)
+    width = spectrum.shape[1]
+    across = spectrum.T.reshape(width, bin_count, cell_dev)
+    tail = from_behind(spectrum.T[:, -EXTRA:], "band", 1)
+    before = jnp.concatenate([tail[:, None], across[:, :-1, -EXTRA:]], 1)
+    slab = jnp.pad(before.transpose(1, 2, 0), ((0, 0), (0, 0), (0, cell_dev - width)))
+    sent = jnp.concatenate([across.transpose(1, 0, 2), slab], 1)
+    got = lax.all_to_all(sent, "bin", split_axis=0, concat_axis=0, tiled=True)
+    body = got[:, :width, :].transpose(2, 0, 1).reshape(cell_dev, bins)
+    head = got[:, width:, :width].transpose(1, 0, 2).reshape(EXTRA, bins)
     field = jnp.concatenate([head, body], 0)
     prev = jnp.zeros((1, bins), jnp.float32)
     mask = ext_mask

time: 196 us -> 203 us (1.036); the launches traced: 195 us -> 200 us
  starting transfers between devices: 46 us -> 34.2 us
  local copies, waits for them, and re-layouts: 24 us -> 31.8 us
  waiting for transfers between devices: 102 us -> 108 us
  other arithmetic: 9.09 us -> 11.9 us
    ppermute x4, waiting for transfers between devices: 86.8 us -> 105 us  [shifted(): return lax.ppermute(block, axis, route)]
    all_to_all x2 -> x1, waiting for transfers between devices: 14.8 us -> 3 us  [per_device(): got = lax.all_to_all(sent, 'bin', split_axis=0, concat_axis=0, tiled=True)]
    ppermute x4, starting transfers between devices: 24.8 us -> 14.1 us  [shifted(): return lax.ppermute(block, axis, route)]
    transpose x0 -> x3, local copies, waits for them, and re-layouts: none -> 5.87 us  [the longest x1 5.01 us: per_device(): sent = jnp.concatenate([across.transpose(1, 0, 2), slab], 1)]
    all_to_all x2 -> x1, starting transfers between devices: 12.9 us -> 8.51 us  [per_device(): got = lax.all_to_all(sent, 'bin', split_axis=0, concat_axis=0, tiled=True)]
    slice x3, local copies, waits for them, and re-layouts: 1.46 us -> 4.82 us  [the longest x1 3.3 us: per_device(): body = got[:, :width, :].transpose(2, 0, 1).reshape(cell_dev, bins)]
    all_to_all x1, starting transfers between devices: 4.44 us -> 7.76 us  [per_device(): lax.all_to_all(field, 'bin', split_axis=1, concat_axis=0, tiled=True)]
    all_to_all x3 -> x0, local copies, waits for them, and re-layouts: 3.15 us -> none  [the longest x1 3.04 us: per_device(): lax.all_to_all(spectrum, 'bin', split_axis=0, concat_axis=1, tiled=True)]
  transfers between devices with their start and end apart: 8 -> 7, of which waited for: 6 -> 5; matrix products, arithmetic and copies ran while one was open for 8% -> 7% of each run, Pallas kernels for 0% -> 0%
where the time goes in v5:
time: 203 us; the launch traced here: 200 us
  waiting for transfers between devices  108 us (53%)
  starting transfers between devices  34.2 us (17%)
  local copies, waits for them, and re-layouts  31.8 us (16%)
  matrix products  13.7 us (7%)
  other arithmetic  11.9 us (6%)
    ppermute x4, waiting for transfers between devices, shifted(): return lax.ppermute(block, axis, route)  105 us
    ppermute x4, starting transfers between devices, shifted(): return lax.ppermute(block, axis, route)  14.1 us
    all_to_all x1, starting transfers between devices, per_device(): got = lax.all_to_all(sent, 'bin', split_axis=0, concat_axis=0, tiled=True)  8.51 us
    all_to_all x1, starting transfers between devices, per_device(): lax.all_to_all(field, 'bin', split_axis=1, concat_axis=0, tiled=True)  7.76 us
    unnamed x23, local copies, waits for them, and re-layouts  6.35 us
    dot_general x2, matrix products, sources(): other = jnp.dot(rounded, source_b, preferred_element_type=jnp.float32)  5.44 us
    dot_general x2, matrix products, sources(): gain = jnp.dot(rounded, source_a, preferred_element_type=jnp.float32)  5.18 us
    transpose x1, local copies, waits for them, and re-layouts, per_device(): sent = jnp.concatenate([across.transpose(1, 0, 2), slab], 1)  5.01 us
  transfers between devices with their start and end apart: 7, of which 5 were waited for; matrix products, arithmetic and copies ran while one was open for 7% of the time, Pallas kernels for 0%

profile of v5, /device:TPU:88, one launch (start us, length us, event | category | flops | bytes accessed | tf_op | source)
XLA Modules:
  0.0 200.3 jit_solution(10917311964633292288)
XLA Ops:
  0.6 0.0 copy-start
  0.6 4.9 %copy.45 = f32[8192,72]{1,0:T(8,128)} copy(f32[8192,72]{0,1:T(8,128)} %param.8) | data formatting | bytes 4718592 | tf_op args[0]
  5.5 0.7 slice.177
  6.2 3.8 %collective-permute-start = (f32[72,8]{0,1:T(8,128)S(1)}, f32[72,8]{0,1:T(8,128)S(1)}, u32[]{:S(2)}, u32[]{:S(2)}) collective-permute-start(f32[72,8]{0,1:T(8,128)S(1)} %slice.177), channel_id=1, source_target_pairs={{0,16},{16,32},{32,48},{48,64},{64,80},{80,96},{96,112},{112,128},... | collective-permute-start | bytes 6920 | tf_op jit(solution)/shard_map/ppermute | solution.py:24
  10.1 0.8 slice.178
  10.9 5.0 %copy.46 = f32[16,72,512]{2,1,0:T(8,128)} copy(f32[16,72,512]{1,2,0:T(8,128)} %bitcast.37) | data formatting | bytes 4718592 | tf_op jit(solution)/shard_map/transpose | solution.py:110
  15.9 3.5 %select_maximum_fusion = f32[16,80,512]{2,1,0:T(8,128)} fusion(f32[16,8,72]{2,1,0:T(8,128)S(1)} %maximum_bitcast_fusion, f32[16,72,512]{2,1,0:T(8,128)} %copy.46), kind=kLoop, calls=%fused_computation.16 | loop fusion | flops 1966080 | bytes 5017600 | tf_op jit(solution)/shard_map/concatenate | solution.py:110
  19.4 8.5 %all-to-all-start = ((f32[16,80,512]{2,1,0:T(8,128)}), f32[16,80,512]{2,1,0:T(8,128)}, u32[]{:S(2)}, u32[]{:S(2)}) async-start(f32[16,80,512]{2,1,0:T(8,128)} %select_maximum_fusion), calls=%async_computation | async-start | bytes 5242880 | tf_op jit(solution)/shard_map/all_to_all | solution.py:111
  27.9 7.2 %collective-permute-start.1 = (f32[33,128]{1,0:T(8,128)S(1)}, f32[33,128]{1,0:T(8,128)S(1)}, u32[]{:S(2)}, u32[]{:S(2)}) collective-permute-start(f32[33,128]{1,0:T(8,128)S(1)} %get-tuple-element.28), channel_id=1, source_target_pairs={{1,0},{2,1},{3,2},{4,3},{5,4},{6,5},{7,6},{8,7},{9,8},{10,9},{11,1... | collective-permute-start | bytes 50696 | tf_op jit(solution)/shard_map/ppermute | solution.py:18
  35.2 0.1 slice.139
  35.3 0.8 slice.133
  36.0 0.1 compare_and_fusion
  36.1 0.1 compare_and_fusion.3
  36.2 0.8 broadcast_multiply_fusion
  37.0 0.1 fusion.54
  37.1 0.1 convert_reduce_fusion
  37.2 0.1 broadcast_multiply_fusion.1
  37.3 49.9 %collective-permute-done.1 = f32[33,128]{1,0:T(8,128)S(1)} collective-permute-done((f32[33,128]{1,0:T(8,128)S(1)}, f32[33,128]{1,0:T(8,128)S(1)}, u32[]{:S(2)}, u32[]{:S(2)}) %collective-permute-start.1) | collective-permute-done | bytes 16928 | tf_op jit(solution)/shard_map/ppermute | solution.py:18
  87.1 0.2 maximum_reduce_fusion
  87.3 0.1 copy.49
  87.5 0.1 reshape.103
  87.6 0.1 fusion.71
  87.7 0.3 fusion.29
  88.0 0.1 mul.233
  88.1 1.6 gather_fusion
  89.7 0.1 select_bitcast_fusion
  89.8 0.3 fusion.21
  90.1 3.0 %all-to-all-done = f32[16,80,512]{2,1,0:T(8,128)} async-done(((f32[16,80,512]{2,1,0:T(8,128)}), f32[16,80,512]{2,1,0:T(8,128)}, u32[]{:S(2)}, u32[]{:S(2)}) %all-to-all-start) | async-done | bytes 2621472 | tf_op jit(solution)/shard_map/all_to_all | solution.py:111
  93.1 3.3 %slice.180 = f32[16,72,512]{2,1,0:T(8,128)} slice(f32[16,80,512]{2,1,0:T(8,128)} %all-to-all-done), slice={[0:16], [0:72], [0:512]} | slice | bytes 4718592 | tf_op jit(solution)/shard_map/slice | solution.py:112
  96.4 3.1 %copy.48 = f32[512,1152]{1,0:T(8,128)} copy(f32[512,1152]{0,1:T(8,128)} %bitcast.39) | data formatting | bytes 4718592 | tf_op jit(solution)/shard_map/reshape | solution.py:112
  99.5 0.8 slice_bitcast_fusion
  100.4 0.1 reshape.101
  100.5 2.0 fusion.10
  102.5 0.4 copy-done.1
  102.9 2.5 %fusion.68 = (bf16[520,1152]{1,0:T(8,128)(2,1)S(1)}, f32[520,1152]{1,0:T(8,128)}) fusion(f32[519,1152]{1,0:T(8,128)S(1)} %fusion.10, f32[1152]{0:T(1024)S(1)} %get-tuple-element.31, f32[520]{0:T(1024)S(1)} %get-tuple-element.3, f32[1152]{0:T(1024)S(1)} %get-tuple-element.32, f32[520]{0:T(1024)S(1)} %get-tuple-element.2, f32[1152]{0:T(1024)S(1)} %copy-done.9, ...), kind=kLoop, calls=%fused_computation.128 | loop fusion | flops 6589440 | bytes 8402016 | tf_op jit(solution)/shard_map/convert_element_type | solution.py:120
  105.4 1.0 copy-done.4
  106.4 0.5 fusion.14
  106.9 0.2 fusion.17
  107.1 0.1 fusion.41
  107.2 0.2 slice_reduce_fusion.1
  107.4 0.1 copy.50
  107.5 1.0 gather_fusion.1
  108.5 0.1 select_bitcast_fusion.1
  108.7 0.3 fusion.23
  109.0 3.3 %fusion.75 = f32[520,1152]{1,0:T(8,128)S(1)} fusion(bf16[520,1152]{1,0:T(8,128)(2,1)} %copy-done.4, bf16[1152,1152]{1,0:T(8,128)(2,1)S(1)} %copy-done), kind=kOutput, calls=%fused_computation.134 | convolution fusion | flops 1380188160 | bytes 6248448 | tf_op jit(solution)/shard_map/dot_general | solution.py:43
  112.4 2.0 %fusion.6 = f32[520,1152]{1,0:T(8,128)S(1)} fusion(f32[520,1152]{1,0:T(8,128)S(1)} %copy-done.3, f32[520,1152]{1,0:T(8,128)S(1)} %fusion.75, bf16[520,1152]{1,0:T(8,128)(2,1)S(1)} %copy-done.5, bf16[1152,1152]{1,0:T(8,128)(2,1)S(1)} %copy-done.10, f32[520]{0:T(1024)S(1)} %get-tuple-element.12), kind=kOutput, calls=%fused_computation.12 | convolution fusion | flops 1384381440 | bytes 11042848 | tf_op jit(solution)/shard_map/dot_general | solution.py:44
  114.4 1.0 fusion.13
  115.5 1.9 fusion.65
  117.3 3.4 %fusion.9 = f32[512,1152]{1,0:T(8,128)} fusion(f32[512,1152]{1,0:T(8,128)S(1)} %fusion.13, f32[512,1152]{1,0:T(8,128)S(1)} %fusion.65, bf16[1152,1152]{1,0:T(8,128)(2,1)S(1)} %copy-done.10, f32[512]{0:T(512)S(1)} %get-tuple-element.29), kind=kOutput, calls=%fused_computation.15 | convolution fusion | flops 1363673088 | bytes 9734144 | tf_op jit(solution)/shard_map/dot_general | solution.py:44
  120.7 3.1 %copy.51 = f32[512,1152]{0,1:T(8,128)} copy(f32[512,1152]{1,0:T(8,128)} %fusion.9) | data formatting | bytes 4718592 | tf_op jit(solution)/shard_map/add | solution.py:122
  123.8 7.8 %all-to-all-start.1 = ((f32[512,16,72]{0,2,1:T(8,128)}), f32[512,16,72]{0,2,1:T(8,128)}, u32[]{:S(2)}, u32[]{:S(2)}) async-start(f32[512,16,72]{0,2,1:T(8,128)} %bitcast.38), calls=%async_computation.1 | async-start | bytes 4718592 | tf_op jit(solution)/shard_map/all_to_all | solution.py:138
  131.6 0.1 reshape.104
  131.7 6.8 %collective-permute-start.2 = (f32[1,128]{1,0:T(1,128)S(1)}, f32[1,128]{1,0:T(1,128)S(1)}, u32[]{:S(2)}, u32[]{:S(2)}) collective-permute-start(f32[1,128]{1,0:T(1,128)S(1)} %get-tuple-element.25), channel_id=1, source_target_pairs={{1,0},{2,1},{3,2},{4,3},{5,4},{6,5},{7,6},{8,7},{9,8},{10,9},{11,1... | collective-permute-start | bytes 1544 | tf_op jit(solution)/shard_map/ppermute | solution.py:18
  138.5 0.1 fusion.70
  138.6 2.1 %fusion.62 = f32[512,128]{1,0:T(8,128)S(1)} fusion(bf16[1152,128]{1,0:T(8,128)(2,1)S(1)} %copy-done.7, f32[512,1152]{1,0:T(8,128)} %copy-done.2), kind=kOutput, calls=%fused_computation.123 | convolution fusion | flops 151584768 | bytes 2916352 | tf_op jit(solution)/shard_map/dot_general | solution.py:46
  140.8 0.3 fusion.26
  141.0 0.1 mul.257
  141.1 39.3 %collective-permute-done.2 = f32[1,128]{1,0:T(1,128)S(1)} collective-permute-done((f32[1,128]{1,0:T(1,128)S(1)}, f32[1,128]{1,0:T(1,128)S(1)}, u32[]{:S(2)}, u32[]{:S(2)}) %collective-permute-start.2) | collective-permute-done | bytes 544 | tf_op jit(solution)/shard_map/ppermute | solution.py:18
  180.4 7.3 %collective-permute-done.3 = f32[1,128]{1,0:T(1,128)S(1)} collective-permute-done((f32[1,128]{1,0:T(1,128)S(1)}, f32[1,128]{1,0:T(1,128)S(1)}, u32[]{:S(2)}, u32[]{:S(2)}) %collective-permute-start.3) | collective-permute-done | bytes 544 | tf_op jit(solution)/shard_map/ppermute | solution.py:18
  187.7 0.2 fusion.19
  188.0 0.1 collective-permute-start.4
  188.1 8.3 %collective-permute-done.4 = f32[32,128]{1,0:T(8,128)S(1)} collective-permute-done((f32[32,128]{1,0:T(8,128)S(1)}, f32[32,128]{1,0:T(8,128)S(1)}, u32[]{:S(2)}, u32[]{:S(2)}) %collective-permute-start.4) | collective-permute-done | bytes 16416 | tf_op jit(solution)/shard_map/ppermute | solution.py:18
  196.4 0.6 pad_maximum_fusion.10
  197.0 3.4 %copy.53 = f32[16,9,8,512]{3,2,0,1:T(8,128)} copy(f32[16,9,8,512]{3,2,1,0:T(8,128)} %bitcast.19) | data formatting | bytes 4718592 | tf_op jit(solution)/shard_map/all_to_all | solution.py:138
  (36 shorter events, 0.1 us)
Async XLA Ops:
  0.6 108.3 %copy-start = (bf16[1152,1152]{1,0:T(8,128)(2,1)S(1)}, bf16[1152,1152]{1,0:T(8,128)(2,1)}, u32[]{:S(2)}) copy-start(bf16[1152,1152]{1,0:T(8,128)(2,1)} %param.10) | copy-start | bytes 7962628
  6.2 9.7 %collective-permute-start = (f32[72,8]{0,1:T(8,128)S(1)}, f32[72,8]{0,1:T(8,128)S(1)}, u32[]{:S(2)}, u32[]{:S(2)}) collective-permute-start(f32[72,8]{0,1:T(8,128)S(1)} %slice.177), channel_id=1, source_target_pairs={{0,16},{16,32},{32,48},{48,64},{64,80},{80,96},{96,112},{112,128},... | collective-permute-start | bytes 6920 | tf_op jit(solution)/shard_map/ppermute | solution.py:24
  19.4 8.5 %copy-start.8 = (f32[64,128]{1,0:T(8,128)S(1)}, f32[64,128]{1,0:T(8,128)}, u32[]{:S(2)}) copy-start(f32[64,128]{1,0:T(8,128)} %param.9) | copy-start | bytes 98308
  19.4 15.8 %copy-start.6 = (s32[131072]{0:T(1024)S(1)}, s32[131072]{0:T(1024)}, u32[]{:S(2)}) copy-start(s32[131072]{0:T(1024)} %param.14) | copy-start | bytes 1572868
  19.4 73.7 %all-to-all-start = ((f32[16,80,512]{2,1,0:T(8,128)}), f32[16,80,512]{2,1,0:T(8,128)}, u32[]{:S(2)}, u32[]{:S(2)}) async-start(f32[16,80,512]{2,1,0:T(8,128)} %select_maximum_fusion), calls=%async_computation | async-start | bytes 5242880 | tf_op jit(solution)/shard_map/all_to_all | solution.py:111
  27.9 59.2 %collective-permute-start.1 = (f32[33,128]{1,0:T(8,128)S(1)}, f32[33,128]{1,0:T(8,128)S(1)}, u32[]{:S(2)}, u32[]{:S(2)}) collective-permute-start(f32[33,128]{1,0:T(8,128)S(1)} %get-tuple-element.28), channel_id=1, source_target_pairs={{1,0},{2,1},{3,2},{4,3},{5,4},{6,5},{7,6},{8,7},{9,8},{10,9},{11,1... | collective-permute-start | bytes 50696 | tf_op jit(solution)/shard_map/ppermute | solution.py:18
  100.5 2.4 %copy-start.1 = (f32[512,1152]{1,0:T(8,128)S(1)}, f32[512,1152]{1,0:T(8,128)}, u32[]{:S(2)}) copy-start(f32[512,1152]{1,0:T(8,128)} %copy.48) | copy-start | bytes 7077892
  100.5 2.4 %copy-start.9 = (f32[1152]{0:T(1024)S(1)}, f32[1152]{0:T(1024)}, u32[]{:S(2)}) copy-start(f32[1152]{0:T(1024)} %param.13) | copy-start | bytes 13828
  102.9 3.5 %copy-start.7 = (bf16[1152,128]{1,0:T(8,128)(2,1)S(1)}, bf16[1152,128]{1,0:T(8,128)(2,1)}, u32[]{:S(2)}) copy-start(bf16[1152,128]{1,0:T(8,128)(2,1)} %param.12) | copy-start | bytes 884740
  105.3 1.0 copy-start.4
  109.0 3.4 %copy-start.3 = (f32[520,1152]{1,0:T(8,128)S(1)}, f32[520,1152]{1,0:T(8,128)}, u32[]{:S(2)}) copy-start(f32[520,1152]{1,0:T(8,128)} %get-tuple-element.15) | copy-start | bytes 7188484
  109.0 3.4 %copy-start.5 = (bf16[520,1152]{1,0:T(8,128)(2,1)S(1)}, bf16[520,1152]{1,0:T(8,128)(2,1)}, u32[]{:S(2)}) copy-start(bf16[520,1152]{1,0:T(8,128)(2,1)} %copy-done.4) | copy-start | bytes 3594244
  109.0 3.4 %copy-start.10 = (bf16[1152,1152]{1,0:T(8,128)(2,1)S(1)}, bf16[1152,1152]{1,0:T(8,128)(2,1)}, u32[]{:S(2)}) copy-start(bf16[1152,1152]{1,0:T(8,128)(2,1)} %param.11) | copy-start | bytes 7962628
  115.4 1.9 copy-start.2
  123.8 73.2 %all-to-all-start.1 = ((f32[512,16,72]{0,2,1:T(8,128)}), f32[512,16,72]{0,2,1:T(8,128)}, u32[]{:S(2)}, u32[]{:S(2)}) async-start(f32[512,16,72]{0,2,1:T(8,128)} %bitcast.38), calls=%async_computation.1 | async-start | bytes 4718592 | tf_op jit(solution)/shard_map/all_to_all | solution.py:138
  131.7 48.8 %collective-permute-start.2 = (f32[1,128]{1,0:T(1,128)S(1)}, f32[1,128]{1,0:T(1,128)S(1)}, u32[]{:S(2)}, u32[]{:S(2)}) collective-permute-start(f32[1,128]{1,0:T(1,128)S(1)} %get-tuple-element.25), channel_id=1, source_target_pairs={{1,0},{2,1},{3,2},{4,3},{5,4},{6,5},{7,6},{8,7},{9,8},{10,9},{11,1... | collective-permute-start | bytes 1544 | tf_op jit(solution)/shard_map/ppermute | solution.py:18
  138.5 49.3 %collective-permute-start.3 = (f32[1,128]{1,0:T(1,128)S(1)}, f32[1,128]{1,0:T(1,128)S(1)}, u32[]{:S(2)}, u32[]{:S(2)}) collective-permute-start(f32[1,128]{1,0:T(1,128)S(1)} %get-tuple-element.26), channel_id=1, source_target_pairs={{255,0},{0,1},{1,2},{2,3},{3,4},{4,5},{5,6},{6,7},{7,8},{8,9},{9,1... | collective-permute-start | bytes 1544 | tf_op jit(solution)/shard_map/ppermute | solution.py:18
  188.0 8.4 %collective-permute-start.4 = (f32[32,128]{1,0:T(8,128)S(1)}, f32[32,128]{1,0:T(8,128)S(1)}, u32[]{:S(2)}, u32[]{:S(2)}) collective-permute-start(f32[32,128]{1,0:T(8,128)S(1)} %get-tuple-element.23), channel_id=1, source_target_pairs={{255,0},{0,1},{1,2},{2,3},{3,4},{4,5},{5,6},{6,7},{7,8},{8,9},{9,1... | collective-permute-start | bytes 49160 | tf_op jit(solution)/shard_map/ppermute | solution.py:18

commit v6 on v3

--- a/solution.py
+++ b/solution.py
@@ -102,11 +102,8 @@
     table = jnp.stack([own[:, 0], own[:, LEVELS]])
     current = jnp.take(table, ext_where, axis=1)
 
-    tail = from_behind(spectrum[-EXTRA:], "band", 1)
-    blocks = spectrum.reshape(bin_count, cell_dev, spectrum.shape[1])
-    heads = jnp.concatenate([tail[None], blocks[:-1, -EXTRA:]], 0).reshape(-1, spectrum.shape[1])
     body = lax.all_to_all(spectrum, "bin", split_axis=0, concat_axis=1, tiled=True)
-    head = lax.all_to_all(heads, "bin", split_axis=0, concat_axis=1, tiled=True)
+    head = from_behind(body[-EXTRA:], ALL, 1)
     field = jnp.concatenate([head, body], 0)
     prev = jnp.zeros((1, bins), jnp.float32)
     mask = ext_mask

time: 196 us -> 184 us (0.939)
  starting transfers between devices: 46 us -> 31.1 us
  other arithmetic: 9.09 us -> 12.8 us
    ppermute x4, starting transfers between devices: 24.8 us -> 14.7 us  [shifted(): return lax.ppermute(block, axis, route)]
    all_to_all x1 -> x0, starting transfers between devices: 8.33 us -> none  [per_device(): head = lax.all_to_all(heads, 'bin', split_axis=0, concat_axis=1, tiled=True)]
    ppermute x4, waiting for transfers between devices: 86.8 us -> 94.2 us  [shifted(): return lax.ppermute(block, axis, route)]
    all_to_all x1 -> x0, waiting for transfers between devices: 6.78 us -> none  [per_device(): head = lax.all_to_all(heads, 'bin', split_axis=0, concat_axis=1, tiled=True)]
    all_to_all x1, starting transfers between devices: 4.57 us -> 9.41 us  [per_device(): lax.all_to_all(spectrum, 'bin', split_axis=0, concat_axis=1, tiled=True)]
    all_to_all x1, waiting for transfers between devices: 8.04 us -> 3.82 us  [per_device(): lax.all_to_all(spectrum, 'bin', split_axis=0, concat_axis=1, tiled=True)]
    ppermute x1, waiting for transfers between devices: 0.01 us -> 4.16 us  [from_behind(): return lax.ppermute(shard, axis, pairs)]
    unnamed x24 -> x50, local copies, waits for them, and re-layouts: 4.57 us -> 1.12 us
  transfers between devices with their start and end apart: 8 -> 7, of which waited for: 6 -> 6; matrix products, arithmetic and copies ran while one was open for 8% -> 10% of each run, Pallas kernels for 0% -> 0%
where the time goes in v6:
time: 184 us
  waiting for transfers between devices  102 us (55%)
  starting transfers between devices  31.1 us (17%)
  local copies, waits for them, and re-layouts  22.8 us (12%)
  matrix products  13.7 us (7%)
  other arithmetic  12.8 us (7%)
    ppermute x4, waiting for transfers between devices, shifted(): return lax.ppermute(block, axis, route)  94.2 us
    ppermute x4, starting transfers between devices, shifted(): return lax.ppermute(block, axis, route)  14.7 us
    all_to_all x1, starting transfers between devices, per_device(): lax.all_to_all(spectrum, 'bin', split_axis=0, concat_axis=1, tiled=True)  9.41 us
    all_to_all x2, local copies, waits for them, and re-layouts, per_device(): lax.all_to_all(spectrum, 'bin', split_axis=0, concat_axis=1, tiled=True)  6.48 us
    dot_general x2, matrix products, sources(): other = jnp.dot(rounded, source_b, preferred_element_type=jnp.float32)  5.44 us
    dot_general x2, matrix products, sources(): gain = jnp.dot(rounded, source_a, preferred_element_type=jnp.float32)  5.18 us
    all_to_all x1, starting transfers between devices, per_device(): lax.all_to_all(field, 'bin', split_axis=1, concat_axis=0, tiled=True)  4.87 us
    ppermute x1, waiting for transfers between devices, from_behind(): return lax.ppermute(shard, axis, pairs)  4.16 us
  transfers between devices with their start and end apart: 7, of which 6 were waited for; matrix products, arithmetic and copies ran while one was open for 10% of the time, Pallas kernels for 0%

profile of v6, /device:TPU:88, one launch (start us, length us, event | category | flops | bytes accessed | tf_op | source)
XLA Modules:
  0.0 183.8 jit_solution(8125481447117881454)
XLA Ops:
  0.6 0.0 copy-start
  0.6 3.4 %copy.50 = f32[9,16,8,512]{3,2,0,1:T(8,128)} copy(f32[9,16,8,512]{3,2,1,0:T(8,128)} %bitcast.32) | data formatting | bytes 4718592 | tf_op jit(solution)/shard_map/all_to_all | solution.py:105
  4.1 9.4 %all-to-all-start = ((f32[16,512,72]{1,2,0:T(8,128)}), f32[16,512,72]{1,2,0:T(8,128)}, u32[]{:S(2)}, u32[]{:S(2)}) async-start(f32[16,512,72]{1,2,0:T(8,128)} %bitcast.30), calls=%async_computation | async-start | bytes 4718592 | tf_op jit(solution)/shard_map/all_to_all | solution.py:105
  13.5 0.6 fusion.74
  14.1 7.2 %collective-permute-start.1 = (f32[33,128]{1,0:T(8,128)S(1)}, f32[33,128]{1,0:T(8,128)S(1)}, u32[]{:S(2)}, u32[]{:S(2)}) collective-permute-start(f32[33,128]{1,0:T(8,128)S(1)} %get-tuple-element.28), channel_id=1, source_target_pairs={{1,0},{2,1},{3,2},{4,3},{5,4},{6,5},{7,6},{8,7},{9,8},{10,9},{11,1... | collective-permute-start | bytes 50696 | tf_op jit(solution)/shard_map/ppermute | solution.py:18
  21.3 0.1 slice.131
  21.4 0.8 slice.127
  22.1 0.1 compare_and_fusion
  22.2 0.6 compare_and_fusion.3
  22.8 0.6 pad_clamp_fusion
  23.4 1.4 broadcast_multiply_fusion
  24.8 0.6 fusion.54
  25.5 0.7 convert_reduce_fusion
  26.2 0.7 broadcast_multiply_fusion.1
  26.8 0.5 compare_and_fusion.1
  27.3 39.0 %collective-permute-done.1 = f32[33,128]{1,0:T(8,128)S(1)} collective-permute-done((f32[33,128]{1,0:T(8,128)S(1)}, f32[33,128]{1,0:T(8,128)S(1)}, u32[]{:S(2)}, u32[]{:S(2)}) %collective-permute-start.1) | collective-permute-done | bytes 16928 | tf_op jit(solution)/shard_map/ppermute | solution.py:18
  66.3 0.2 maximum_reduce_fusion
  66.5 0.1 copy.42
  66.6 0.1 reshape.95
  66.8 1.6 gather_fusion
  68.3 0.1 fusion.71
  68.5 0.9 fusion.29
  69.4 0.1 select_bitcast_fusion
  69.5 3.8 %all-to-all-done = f32[16,512,72]{1,2,0:T(8,128)} async-done(((f32[16,512,72]{1,2,0:T(8,128)}), f32[16,512,72]{1,2,0:T(8,128)}, u32[]{:S(2)}, u32[]{:S(2)}) %all-to-all-start) | async-done | bytes 2359328 | tf_op jit(solution)/shard_map/all_to_all | solution.py:105
  73.3 1.3 slice.169
  74.6 0.8 copy.46
  75.4 2.1 %collective-permute-start = (f32[8,1152]{1,0:T(8,128)}, f32[8,1152]{1,0:T(8,128)S(1)}, u32[]{:S(2)}, u32[]{:S(2)}) collective-permute-start(f32[8,1152]{1,0:T(8,128)} %copy.46), channel_id=1, source_target_pairs={{0,1},{1,2},{2,3},{3,4},{4,5},{5,6},{6,7},{7,8},{8,9},{9,10},{10,1... | collective-permute-start | bytes 110600 | tf_op jit(solution)/shard_map/ppermute | solution.py:24
  77.5 0.3 fusion.21
  77.9 0.9 mul.233
  78.8 3.0 %copy.41 = f32[512,1152]{1,0:T(8,128)} copy(f32[512,1152]{0,1:T(8,128)} %bitcast.2) | data formatting | bytes 4718592 | tf_op jit(solution)/shard_map/all_to_all | solution.py:105
  81.9 4.2 %collective-permute-done = f32[8,1152]{1,0:T(8,128)S(1)} collective-permute-done((f32[8,1152]{1,0:T(8,128)}, f32[8,1152]{1,0:T(8,128)S(1)}, u32[]{:S(2)}, u32[]{:S(2)}) %collective-permute-start) | collective-permute-done | bytes 36896 | tf_op jit(solution)/shard_map/ppermute | solution.py:24
  86.0 1.8 fusion.10
  87.9 0.0 copy-start.7
  88.0 2.5 %fusion.68 = (bf16[520,1152]{1,0:T(8,128)(2,1)S(1)}, f32[520,1152]{1,0:T(8,128)}) fusion(f32[519,1152]{1,0:T(8,128)S(1)} %fusion.10, f32[1152]{0:T(1024)S(1)} %get-tuple-element.31, f32[520]{0:T(1024)S(1)} %get-tuple-element.3, f32[1152]{0:T(1024)S(1)} %copy-done.10, f32[520]{0:T(1024)S(1)} %get-tuple-element.2, f32[1152]{0:T(1024)S(1)} %copy-done.13, ...), kind=kLoop, calls=%fused_computation.125 | loop fusion | flops 6589440 | bytes 8402016 | tf_op jit(solution)/shard_map/convert_element_type | solution.py:113
  90.4 1.0 copy-done.4
  91.4 0.5 fusion.14
  91.9 0.2 fusion.17
  92.2 0.1 fusion.41
  92.3 0.2 slice_reduce_fusion.1
  92.5 0.1 copy.43
  92.6 1.0 gather_fusion.1
  93.7 0.1 select_bitcast_fusion.1
  93.8 0.3 fusion.23
  94.1 0.0 copy-start.5
  94.2 3.3 %fusion.75 = f32[520,1152]{1,0:T(8,128)S(1)} fusion(bf16[520,1152]{1,0:T(8,128)(2,1)} %copy-done.4, bf16[1152,1152]{1,0:T(8,128)(2,1)S(1)} %copy-done), kind=kOutput, calls=%fused_computation.131 | convolution fusion | flops 1380188160 | bytes 6248448 | tf_op jit(solution)/shard_map/dot_general | solution.py:43
  97.6 2.0 %fusion.6 = f32[520,1152]{1,0:T(8,128)S(1)} fusion(f32[520,1152]{1,0:T(8,128)S(1)} %copy-done.3, f32[520,1152]{1,0:T(8,128)S(1)} %fusion.75, bf16[520,1152]{1,0:T(8,128)(2,1)S(1)} %copy-done.5, bf16[1152,1152]{1,0:T(8,128)(2,1)S(1)} %copy-done.24, f32[520]{0:T(1024)S(1)} %copy-done.19), kind=kOutput, calls=%fused_computation.12 | convolution fusion | flops 1384381440 | bytes 11042848 | tf_op jit(solution)/shard_map/dot_general | solution.py:44
  99.6 1.0 fusion.13
  100.7 1.9 %fusion.65 = f32[512,1152]{1,0:T(8,128)S(1)} fusion(bf16[1152,1152]{1,0:T(8,128)(2,1)S(1)} %copy-done, f32[512,1152]{1,0:T(8,128)S(1)} %fusion.13), kind=kOutput, calls=%fused_computation.123 | convolution fusion | flops 1359544320 | bytes 7372800 | tf_op jit(solution)/shard_map/dot_general | solution.py:43
  102.5 3.4 %fusion.9 = f32[512,1152]{1,0:T(8,128)} fusion(f32[512,1152]{1,0:T(8,128)S(1)} %fusion.13, f32[512,1152]{1,0:T(8,128)S(1)} %fusion.65, bf16[1152,1152]{1,0:T(8,128)(2,1)S(1)} %copy-done.24, f32[512]{0:T(512)S(1)} %copy-done.23), kind=kOutput, calls=%fused_computation.15 | convolution fusion | flops 1363673088 | bytes 9734144 | tf_op jit(solution)/shard_map/dot_general | solution.py:44
  105.9 3.2 %copy.44 = f32[512,1152]{0,1:T(8,128)} copy(f32[512,1152]{1,0:T(8,128)} %fusion.9) | data formatting | bytes 4718592 | tf_op jit(solution)/shard_map/add | solution.py:115
  109.1 4.9 %all-to-all-start.1 = ((f32[512,16,72]{0,2,1:T(8,128)}), f32[512,16,72]{0,2,1:T(8,128)}, u32[]{:S(2)}, u32[]{:S(2)}) async-start(f32[512,16,72]{0,2,1:T(8,128)} %bitcast.31), calls=%async_computation.1 | async-start | bytes 4718592 | tf_op jit(solution)/shard_map/all_to_all | solution.py:131
  114.0 0.1 reshape.96
  114.1 7.4 %collective-permute-start.2 = (f32[1,128]{1,0:T(1,128)S(1)}, f32[1,128]{1,0:T(1,128)S(1)}, u32[]{:S(2)}, u32[]{:S(2)}) collective-permute-start(f32[1,128]{1,0:T(1,128)S(1)} %get-tuple-element.25), channel_id=1, source_target_pairs={{1,0},{2,1},{3,2},{4,3},{5,4},{6,5},{7,6},{8,7},{9,8},{10,9},{11,1... | collective-permute-start | bytes 1544 | tf_op jit(solution)/shard_map/ppermute | solution.py:18
  121.6 0.1 fusion.70
  121.7 2.1 %fusion.62 = f32[512,128]{1,0:T(8,128)S(1)} fusion(bf16[1152,128]{1,0:T(8,128)(2,1)S(1)} %copy-done.7, f32[512,1152]{1,0:T(8,128)} %copy-done.2), kind=kOutput, calls=%fused_computation.120 | convolution fusion | flops 151584768 | bytes 2916352 | tf_op jit(solution)/shard_map/dot_general | solution.py:46
  123.8 0.3 fusion.26
  124.1 0.1 mul.257
  124.2 41.9 %collective-permute-done.2 = f32[1,128]{1,0:T(1,128)S(1)} collective-permute-done((f32[1,128]{1,0:T(1,128)S(1)}, f32[1,128]{1,0:T(1,128)S(1)}, u32[]{:S(2)}, u32[]{:S(2)}) %collective-permute-start.2) | collective-permute-done | bytes 544 | tf_op jit(solution)/shard_map/ppermute | solution.py:18
  166.2 5.0 %collective-permute-done.3 = f32[1,128]{1,0:T(1,128)S(1)} collective-permute-done((f32[1,128]{1,0:T(1,128)S(1)}, f32[1,128]{1,0:T(1,128)S(1)}, u32[]{:S(2)}, u32[]{:S(2)}) %collective-permute-start.3) | collective-permute-done | bytes 544 | tf_op jit(solution)/shard_map/ppermute | solution.py:18
  171.2 0.2 fusion.19
  171.4 0.1 collective-permute-start.4
  171.5 8.3 %collective-permute-done.4 = f32[32,128]{1,0:T(8,128)S(1)} collective-permute-done((f32[32,128]{1,0:T(8,128)S(1)}, f32[32,128]{1,0:T(8,128)S(1)}, u32[]{:S(2)}, u32[]{:S(2)}) %collective-permute-start.4) | collective-permute-done | bytes 16416 | tf_op jit(solution)/shard_map/ppermute | solution.py:18
  179.8 0.6 pad_maximum_fusion.10
  180.4 3.4 %copy.48 = f32[16,9,8,512]{3,2,0,1:T(8,128)} copy(f32[16,9,8,512]{3,2,1,0:T(8,128)} %bitcast.14) | data formatting | bytes 4718592 | tf_op jit(solution)/shard_map/all_to_all | solution.py:131
  (57 shorter events, 0.1 us)
Async XLA Ops:
  0.6 93.5 %copy-start = (bf16[1152,1152]{1,0:T(8,128)(2,1)S(1)}, bf16[1152,1152]{1,0:T(8,128)(2,1)}, u32[]{:S(2)}) copy-start(bf16[1152,1152]{1,0:T(8,128)(2,1)} %param.10) | copy-start | bytes 7962628
  4.1 9.4 %copy-start.8 = (f32[64,128]{1,0:T(8,128)S(1)}, f32[64,128]{1,0:T(8,128)}, u32[]{:S(2)}) copy-start(f32[64,128]{1,0:T(8,128)} %param.9) | copy-start | bytes 98308
  4.1 17.2 %copy-start.6 = (s32[131072]{0:T(1024)S(1)}, s32[131072]{0:T(1024)}, u32[]{:S(2)}) copy-start(s32[131072]{0:T(1024)} %param.14) | copy-start | bytes 1572868
  4.1 69.2 %all-to-all-start = ((f32[16,512,72]{1,2,0:T(8,128)}), f32[16,512,72]{1,2,0:T(8,128)}, u32[]{:S(2)}, u32[]{:S(2)}) async-start(f32[16,512,72]{1,2,0:T(8,128)} %bitcast.30), calls=%async_computation | async-start | bytes 4718592 | tf_op jit(solution)/shard_map/all_to_all | solution.py:105
  14.1 52.2 %collective-permute-start.1 = (f32[33,128]{1,0:T(8,128)S(1)}, f32[33,128]{1,0:T(8,128)S(1)}, u32[]{:S(2)}, u32[]{:S(2)}) collective-permute-start(f32[33,128]{1,0:T(8,128)S(1)} %get-tuple-element.28), channel_id=1, source_target_pairs={{1,0},{2,1},{3,2},{4,3},{5,4},{6,5},{7,6},{8,7},{9,8},{10,9},{11,1... | collective-permute-start | bytes 50696 | tf_op jit(solution)/shard_map/ppermute | solution.py:18
  24.8 48.5 %copy-start.14 = (f32[520]{0:T(1024)}, f32[520]{0:T(1024)S(1)}, u32[]{:S(2)}) copy-start(f32[520]{0:T(1024)S(1)} %get-tuple-element.13) | copy-start | bytes 6244
  66.3 7.0 %copy-start.11 = (f32[33,128]{1,0:T(8,128)}, f32[33,128]{1,0:T(8,128)S(1)}, u32[]{:S(2)}) copy-start(f32[33,128]{1,0:T(8,128)S(1)} %collective-permute-done.1) | copy-start | bytes 50692
  75.4 10.6 %collective-permute-start = (f32[8,1152]{1,0:T(8,128)}, f32[8,1152]{1,0:T(8,128)S(1)}, u32[]{:S(2)}, u32[]{:S(2)}) collective-permute-start(f32[8,1152]{1,0:T(8,128)} %copy.46), channel_id=1, source_target_pairs={{0,1},{1,2},{2,3},{3,4},{4,5},{5,6},{6,7},{7,8},{8,9},{9,10},{10,1... | collective-permute-start | bytes 110600 | tf_op jit(solution)/shard_map/ppermute | solution.py:24
  81.9 6.0 %copy-start.1 = (f32[512,1152]{1,0:T(8,128)S(1)}, f32[512,1152]{1,0:T(8,128)}, u32[]{:S(2)}) copy-start(f32[512,1152]{1,0:T(8,128)} %copy.41) | copy-start | bytes 7077892
  81.9 6.0 %copy-start.10 = (f32[1152]{0:T(1024)S(1)}, f32[1152]{0:T(1024)}, u32[]{:S(2)}) copy-start(f32[1152]{0:T(1024)} %get-tuple-element.32) | copy-start | bytes 13828
  81.9 6.0 %copy-start.13 = (f32[1152]{0:T(1024)S(1)}, f32[1152]{0:T(1024)}, u32[]{:S(2)}) copy-start(f32[1152]{0:T(1024)} %param.13) | copy-start | bytes 13828
  81.9 6.0 %copy-start.15 = (f32[520]{0:T(1024)S(1)}, f32[520]{0:T(1024)}, u32[]{:S(2)}) copy-start(f32[520]{0:T(1024)} %copy-done.14) | copy-start | bytes 6244
  87.9 3.5 %copy-start.7 = (bf16[1152,128]{1,0:T(8,128)(2,1)S(1)}, bf16[1152,128]{1,0:T(8,128)(2,1)}, u32[]{:S(2)}) copy-start(bf16[1152,128]{1,0:T(8,128)(2,1)} %param.12) | copy-start | bytes 884740
  87.9 4.0 %copy-start.18 = (f32[64]{0:T(128)S(1)}, f32[64]{0:T(128)}, u32[]{:S(2)}) copy-start(f32[64]{0:T(128)} %convert_reduce_fusion) | copy-start | bytes 772
  87.9 4.3 %copy-start.9 = (f32[33,128]{1,0:T(8,128)S(1)}, f32[33,128]{1,0:T(8,128)}, u32[]{:S(2)}) copy-start(f32[33,128]{1,0:T(8,128)} %get-tuple-element.27) | copy-start | bytes 50692
  87.9 4.3 %copy-start.12 = (f32[33,128]{1,0:T(8,128)S(1)}, f32[33,128]{1,0:T(8,128)}, u32[]{:S(2)}) copy-start(f32[33,128]{1,0:T(8,128)} %copy-done.11) | copy-start | bytes 50692
  88.0 4.3 %copy-start.20 = (pred[64]{0:T(512)(128)(4,1)S(1)}, pred[64]{0:T(512)(128)(4,1)}, u32[]{:S(2)}) copy-start(pred[64]{0:T(512)(128)(4,1)} %get-tuple-element.33) | copy-start | bytes 196
  88.0 4.3 %copy-start.21 = (pred[64]{0:T(512)(128)(4,1)S(1)}, pred[64]{0:T(512)(128)(4,1)}, u32[]{:S(2)}) copy-start(pred[64]{0:T(512)(128)(4,1)} %get-tuple-element.34) | copy-start | bytes 196
  90.4 1.0 copy-start.4
  90.4 2.2 %copy-start.16 = (s32[1024]{0:T(1024)S(1)}, s32[1024]{0:T(1024)}, u32[]{:S(2)}) copy-start(s32[1024]{0:T(1024)} %pad_clamp_fusion) | copy-start | bytes 12292
  90.4 3.2 %copy-start.22 = (pred[512]{0:T(512)(128)(4,1)S(1)}, pred[512]{0:T(512)(128)(4,1)}, u32[]{:S(2)}) copy-start(pred[512]{0:T(512)(128)(4,1)} %get-tuple-element.10) | copy-start | bytes 1540
  94.1 3.4 %copy-start.3 = (f32[520,1152]{1,0:T(8,128)S(1)}, f32[520,1152]{1,0:T(8,128)}, u32[]{:S(2)}) copy-start(f32[520,1152]{1,0:T(8,128)} %get-tuple-element.15) | copy-start | bytes 7188484
  94.1 3.4 %copy-start.5 = (bf16[520,1152]{1,0:T(8,128)(2,1)S(1)}, bf16[520,1152]{1,0:T(8,128)(2,1)}, u32[]{:S(2)}) copy-start(bf16[520,1152]{1,0:T(8,128)(2,1)} %copy-done.4) | copy-start | bytes 3594244
  94.2 3.4 %copy-start.19 = (f32[520]{0:T(1024)S(1)}, f32[520]{0:T(1024)}, u32[]{:S(2)}) copy-start(f32[520]{0:T(1024)} %get-tuple-element.12) | copy-start | bytes 6244
  94.2 3.4 %copy-start.24 = (bf16[1152,1152]{1,0:T(8,128)(2,1)S(1)}, bf16[1152,1152]{1,0:T(8,128)(2,1)}, u32[]{:S(2)}) copy-start(bf16[1152,1152]{1,0:T(8,128)(2,1)} %param.11) | copy-start | bytes 7962628
  97.5 2.1 %copy-start.17 = (f32[512]{0:T(512)S(1)}, f32[512]{0:T(512)}, u32[]{:S(2)}) copy-start(f32[512]{0:T(512)} %get-tuple-element.30) | copy-start | bytes 6148
  100.6 1.9 %copy-start.2 = (f32[512,1152]{1,0:T(8,128)}, f32[512,1152]{1,0:T(8,128)S(1)}, u32[]{:S(2)}) copy-start(f32[512,1152]{1,0:T(8,128)S(1)} %fusion.13) | copy-start | bytes 7077892
  100.6 1.9 %copy-start.23 = (f32[512]{0:T(512)S(1)}, f32[512]{0:T(512)}, u32[]{:S(2)}) copy-start(f32[512]{0:T(512)} %get-tuple-element.29) | copy-start | bytes 6148
  109.1 71.3 %all-to-all-start.1 = ((f32[512,16,72]{0,2,1:T(8,128)}), f32[512,16,72]{0,2,1:T(8,128)}, u32[]{:S(2)}, u32[]{:S(2)}) async-start(f32[512,16,72]{0,2,1:T(8,128)} %bitcast.31), calls=%async_computation.1 | async-start | bytes 4718592 | tf_op jit(solution)/shard_map/all_to_all | solution.py:131
  114.1 52.0 %collective-permute-start.2 = (f32[1,128]{1,0:T(1,128)S(1)}, f32[1,128]{1,0:T(1,128)S(1)}, u32[]{:S(2)}, u32[]{:S(2)}) collective-permute-start(f32[1,128]{1,0:T(1,128)S(1)} %get-tuple-element.25), channel_id=1, source_target_pairs={{1,0},{2,1},{3,2},{4,3},{5,4},{6,5},{7,6},{8,7},{9,8},{10,9},{11,1... | collective-permute-start | bytes 1544 | tf_op jit(solution)/shard_map/ppermute | solution.py:18
  121.5 49.6 %collective-permute-start.3 = (f32[1,128]{1,0:T(1,128)S(1)}, f32[1,128]{1,0:T(1,128)S(1)}, u32[]{:S(2)}, u32[]{:S(2)}) collective-permute-start(f32[1,128]{1,0:T(1,128)S(1)} %get-tuple-element.26), channel_id=1, source_target_pairs={{255,0},{0,1},{1,2},{2,3},{3,4},{4,5},{5,6},{6,7},{7,8},{8,9},{9,1... | collective-permute-start | bytes 1544 | tf_op jit(solution)/shard_map/ppermute | solution.py:18
  171.4 8.4 %collective-permute-start.4 = (f32[32,128]{1,0:T(8,128)S(1)}, f32[32,128]{1,0:T(8,128)S(1)}, u32[]{:S(2)}, u32[]{:S(2)}) collective-permute-start(f32[32,128]{1,0:T(8,128)S(1)} %get-tuple-element.23), channel_id=1, source_target_pairs={{255,0},{0,1},{1,2},{2,3},{3,4},{4,5},{5,6},{6,7},{7,8},{8,9},{9,1... | collective-permute-start | bytes 49160 | tf_op jit(solution)/shard_map/ppermute | solution.py:18

commit v7 on v6

--- a/solution.py
+++ b/solution.py
@@ -63,6 +63,16 @@
     return window + 0.2 * lap_h + 0.2 * lap_v + 1.5 * forcing - 0.05 * window
 
 
+def ocean_rows(padded, forcing):
+    columns = padded.shape[0] - 2
+    window = padded[1:-1]
+    lap_h = padded[2:] + padded[:-2] - 2.0 * window
+    cube = window.reshape(columns, 2, LEVELS)
+    edge = jnp.pad(cube, ((0, 0), (0, 0), (1, 1)), mode="edge")
+    lap_v = (edge[:, :, 2:] + edge[:, :, :-2] - 2.0 * cube).reshape(columns, 2 * LEVELS)
+    return window + 0.2 * lap_h + 0.2 * lap_v + 1.5 * forcing - 0.05 * window
+
+
 def per_device(
     spectrum, velocity, source_a, source_b, stokes_kernel, group_speed, column_map, land_mask
 ):
@@ -120,14 +130,22 @@
             mask = local_mask
         sums = jnp.dot(onehot, stokes, precision=lax.Precision.HIGHEST)
         forcing = sums / counts[:, None]
-        if step > 0:
-            below = shifted(window[-1:], ALL, 1)
-            above = shifted(window[:1], ALL, -1)
-        window = ocean_step(window, below, above, forcing, joint)
         if step + 1 < STEPS:
+            if step > 0:
+                below = edge[-1:]
+                above = shifted(window[:1], ALL, -1)
+            window = ocean_step(window, below, above, forcing, joint)
+            edge = shifted(window[half - 1 :], ALL, 1)
             table = jnp.stack([window[:, 0], window[:, LEVELS]])
             current = jnp.take(table, where, axis=1)
-    velocity_out = jnp.concatenate([shifted(window[half:], ALL, 1), window[:half]], 0)
+        else:
+            low_forcing = shifted(forcing[half:], ALL, 1)
+            padded = jnp.concatenate([edge, window[: half + 1]], 0)
+            if device_count > 1:
+                row = jnp.arange(padded.shape[0])[:, None]
+                outside = ((device == 0) & (row == 0)) | (joint & (row == padded.shape[0] - 1))
+                padded = jnp.where(outside, 0.0, padded)
+            velocity_out = ocean_rows(padded, jnp.concatenate([low_forcing, forcing[:half]], 0))
     spectrum_out = lax.all_to_all(field, "bin", split_axis=1, concat_axis=0, tiled=True)
     return (spectrum_out, velocity_out)
 

time: 184 us -> 180 us (0.978); the launches traced: 184 us -> 178 us
  starting transfers between devices: 31.1 us -> 25.7 us
    ppermute x4 -> x3, starting transfers between devices: 14.7 us -> 9.31 us  [shifted(): return lax.ppermute(block, axis, route)]
    ppermute x4 -> x3, waiting for transfers between devices: 94.2 us -> 92.6 us  [shifted(): return lax.ppermute(block, axis, route)]
  transfers between devices with their start and end apart: 7 -> 6, of which waited for: 6 -> 5; matrix products, arithmetic and copies ran while one was open for 10% -> 10% of each run, Pallas kernels for 0% -> 0%
where the time goes in v7:
time: 180 us; the launch traced here: 178 us
  waiting for transfers between devices  101 us (56%)
  starting transfers between devices  25.7 us (14%)
  local copies, waits for them, and re-layouts  22.8 us (13%)
  matrix products  13.7 us (8%)
  other arithmetic  12.9 us (7%)
    ppermute x3, waiting for transfers between devices, shifted(): return lax.ppermute(block, axis, route)  92.6 us
    all_to_all x1, starting transfers between devices, per_device(): lax.all_to_all(spectrum, 'bin', split_axis=0, concat_axis=1, tiled=True)  9.41 us
    ppermute x3, starting transfers between devices, shifted(): return lax.ppermute(block, axis, route)  9.31 us
    all_to_all x2, local copies, waits for them, and re-layouts, per_device(): lax.all_to_all(spectrum, 'bin', split_axis=0, concat_axis=1, tiled=True)  6.48 us
    dot_general x2, matrix products, sources(): other = jnp.dot(rounded, source_b, preferred_element_type=jnp.float32)  5.44 us
    dot_general x2, matrix products, sources(): gain = jnp.dot(rounded, source_a, preferred_element_type=jnp.float32)  5.18 us
    all_to_all x1, starting transfers between devices, per_device(): lax.all_to_all(field, 'bin', split_axis=1, concat_axis=0, tiled=True)  4.89 us
    ppermute x1, waiting for transfers between devices, from_behind(): return lax.ppermute(shard, axis, pairs)  4.16 us
  transfers between devices with their start and end apart: 6, of which 5 were waited for; matrix products, arithmetic and copies ran while one was open for 10% of the time, Pallas kernels for 0%

profile of v7, /device:TPU:88, one launch (start us, length us, event | category | flops | bytes accessed | tf_op | source)
XLA Modules:
  0.0 177.6 jit_solution(10473453872866420865)
XLA Ops:
  0.6 0.0 copy-start
  0.6 3.4 %copy.50 = f32[9,16,8,512]{3,2,0,1:T(8,128)} copy(f32[9,16,8,512]{3,2,1,0:T(8,128)} %bitcast.32) | data formatting | bytes 4718592 | tf_op jit(solution)/shard_map/all_to_all | solution.py:115
  4.1 9.4 %all-to-all-start = ((f32[16,512,72]{1,2,0:T(8,128)}), f32[16,512,72]{1,2,0:T(8,128)}, u32[]{:S(2)}, u32[]{:S(2)}) async-start(f32[16,512,72]{1,2,0:T(8,128)} %bitcast.30), calls=%async_computation | async-start | bytes 4718592 | tf_op jit(solution)/shard_map/all_to_all | solution.py:115
  13.5 0.6 fusion.70
  14.1 7.2 %collective-permute-start.1 = (f32[33,128]{1,0:T(8,128)S(1)}, f32[33,128]{1,0:T(8,128)S(1)}, u32[]{:S(2)}, u32[]{:S(2)}) collective-permute-start(f32[33,128]{1,0:T(8,128)S(1)} %get-tuple-element.28), channel_id=1, source_target_pairs={{1,0},{2,1},{3,2},{4,3},{5,4},{6,5},{7,6},{8,7},{9,8},{10,9},{11,1... | collective-permute-start | bytes 50696 | tf_op jit(solution)/shard_map/ppermute | solution.py:18
  21.3 0.1 slice.132
  21.4 0.8 slice.128
  22.1 0.1 compare_and_fusion
  22.2 0.6 compare_and_fusion.3
  22.8 0.6 pad_clamp_fusion
  23.4 1.4 broadcast_multiply_fusion
  24.8 0.7 fusion.50
  25.4 0.6 convert_reduce_fusion
  26.1 0.6 broadcast_multiply_fusion.1
  26.7 0.6 compare_and_fusion.1
  27.3 39.0 %collective-permute-done.1 = f32[33,128]{1,0:T(8,128)S(1)} collective-permute-done((f32[33,128]{1,0:T(8,128)S(1)}, f32[33,128]{1,0:T(8,128)S(1)}, u32[]{:S(2)}, u32[]{:S(2)}) %collective-permute-start.1) | collective-permute-done | bytes 16928 | tf_op jit(solution)/shard_map/ppermute | solution.py:18
  66.3 0.2 maximum_reduce_fusion
  66.5 0.1 copy.42
  66.6 0.1 reshape.110
  66.8 1.6 gather_fusion
  68.3 0.1 fusion.67
  68.5 0.9 fusion.26
  69.4 0.1 select_bitcast_fusion
  69.5 3.8 %all-to-all-done = f32[16,512,72]{1,2,0:T(8,128)} async-done(((f32[16,512,72]{1,2,0:T(8,128)}), f32[16,512,72]{1,2,0:T(8,128)}, u32[]{:S(2)}, u32[]{:S(2)}) %all-to-all-start) | async-done | bytes 2359328 | tf_op jit(solution)/shard_map/all_to_all | solution.py:115
  73.3 1.3 slice.171
  74.6 0.8 copy.46
  75.4 2.1 %collective-permute-start = (f32[8,1152]{1,0:T(8,128)}, f32[8,1152]{1,0:T(8,128)S(1)}, u32[]{:S(2)}, u32[]{:S(2)}) collective-permute-start(f32[8,1152]{1,0:T(8,128)} %copy.46), channel_id=1, source_target_pairs={{0,1},{1,2},{2,3},{3,4},{4,5},{5,6},{6,7},{7,8},{8,9},{9,10},{10,1... | collective-permute-start | bytes 110600 | tf_op jit(solution)/shard_map/ppermute | solution.py:24
  77.5 0.3 fusion.18
  77.9 0.9 mul.233
  78.8 3.0 %copy.41 = f32[512,1152]{1,0:T(8,128)} copy(f32[512,1152]{0,1:T(8,128)} %bitcast.2) | data formatting | bytes 4718592 | tf_op jit(solution)/shard_map/all_to_all | solution.py:115
  81.9 4.2 %collective-permute-done = f32[8,1152]{1,0:T(8,128)S(1)} collective-permute-done((f32[8,1152]{1,0:T(8,128)}, f32[8,1152]{1,0:T(8,128)S(1)}, u32[]{:S(2)}, u32[]{:S(2)}) %collective-permute-start) | collective-permute-done | bytes 36896 | tf_op jit(solution)/shard_map/ppermute | solution.py:24
  86.0 1.8 %fusion.10 = f32[519,1152]{1,0:T(8,128)S(1)} fusion(f32[8,1152]{1,0:T(8,128)S(1)} %collective-permute-done, f32[512,1152]{1,0:T(8,128)} %copy.41), kind=kLoop, calls=%fused_computation.16 | loop fusion | flops 597888 | bytes 4787712 | tf_op jit(solution)/shard_map/concatenate | solution.py:117
  87.9 0.0 copy-start.9
  88.0 2.5 %fusion.64 = (bf16[520,1152]{1,0:T(8,128)(2,1)S(1)}, f32[520,1152]{1,0:T(8,128)}) fusion(f32[519,1152]{1,0:T(8,128)S(1)} %fusion.10, f32[1152]{0:T(1024)S(1)} %get-tuple-element.31, f32[520]{0:T(1024)S(1)} %get-tuple-element.3, f32[1152]{0:T(1024)S(1)} %copy-done.10, f32[520]{0:T(1024)S(1)} %get-tuple-element.2, f32[1152]{0:T(1024)S(1)} %copy-done.13, ...), kind=kLoop, calls=%fused_computation.122 | loop fusion | flops 6589440 | bytes 8402016 | tf_op jit(solution)/shard_map/convert_element_type | solution.py:123
  90.4 1.0 copy-done.4
  91.4 0.5 fusion.14
  91.9 0.2 fusion.16
  92.2 0.1 fusion.38
  92.3 0.2 slice_reduce_fusion.1
  92.5 0.1 copy.43
  92.6 1.0 gather_fusion.1
  93.7 0.1 select_bitcast_fusion.1
  93.8 0.3 fusion.20
  94.1 0.0 copy-start.5
  94.2 3.3 %fusion.71 = f32[520,1152]{1,0:T(8,128)S(1)} fusion(bf16[520,1152]{1,0:T(8,128)(2,1)} %copy-done.4, bf16[1152,1152]{1,0:T(8,128)(2,1)S(1)} %copy-done), kind=kOutput, calls=%fused_computation.128 | convolution fusion | flops 1380188160 | bytes 6248448 | tf_op jit(solution)/shard_map/dot_general | solution.py:43
  97.5 2.0 %fusion.6 = f32[520,1152]{1,0:T(8,128)S(1)} fusion(f32[520,1152]{1,0:T(8,128)S(1)} %copy-done.3, f32[520,1152]{1,0:T(8,128)S(1)} %fusion.71, bf16[520,1152]{1,0:T(8,128)(2,1)S(1)} %copy-done.5, bf16[1152,1152]{1,0:T(8,128)(2,1)S(1)} %copy-done.24, f32[520]{0:T(1024)S(1)} %copy-done.19), kind=kOutput, calls=%fused_computation.12 | convolution fusion | flops 1384381440 | bytes 11042848 | tf_op jit(solution)/shard_map/dot_general | solution.py:44
  99.6 1.0 fusion.13
  100.6 1.8 %fusion.61 = f32[512,1152]{1,0:T(8,128)S(1)} fusion(bf16[1152,1152]{1,0:T(8,128)(2,1)S(1)} %copy-done, f32[512,1152]{1,0:T(8,128)S(1)} %fusion.13), kind=kOutput, calls=%fused_computation.120 | convolution fusion | flops 1359544320 | bytes 7372800 | tf_op jit(solution)/shard_map/dot_general | solution.py:43
  102.5 3.4 %fusion.9 = f32[512,1152]{1,0:T(8,128)} fusion(f32[512,1152]{1,0:T(8,128)S(1)} %fusion.13, f32[512,1152]{1,0:T(8,128)S(1)} %fusion.61, bf16[1152,1152]{1,0:T(8,128)(2,1)S(1)} %copy-done.24, f32[512]{0:T(512)S(1)} %copy-done.21), kind=kOutput, calls=%fused_computation.15 | convolution fusion | flops 1363673088 | bytes 9734144 | tf_op jit(solution)/shard_map/dot_general | solution.py:44
  105.9 3.2 %copy.44 = f32[512,1152]{0,1:T(8,128)} copy(f32[512,1152]{1,0:T(8,128)} %fusion.9) | data formatting | bytes 4718592 | tf_op jit(solution)/shard_map/add | solution.py:125
  109.1 4.9 %all-to-all-start.1 = ((f32[512,16,72]{0,2,1:T(8,128)}), f32[512,16,72]{0,2,1:T(8,128)}, u32[]{:S(2)}, u32[]{:S(2)}) async-start(f32[512,16,72]{0,2,1:T(8,128)} %bitcast.31), calls=%async_computation.1 | async-start | bytes 4718592 | tf_op jit(solution)/shard_map/all_to_all | solution.py:149
  114.0 0.4 collective-permute-start.2
  114.5 2.1 %fusion.58 = f32[512,128]{1,0:T(8,128)S(1)} fusion(bf16[1152,128]{1,0:T(8,128)(2,1)S(1)} %copy-done.7, f32[512,1152]{1,0:T(8,128)} %copy-done.2), kind=kOutput, calls=%fused_computation.117 | convolution fusion | flops 151584768 | bytes 2916352 | tf_op jit(solution)/shard_map/dot_general | solution.py:46
  116.6 0.2 convolution_divide_fusion
  116.9 1.7 collective-permute-start.3
  118.6 53.5 %collective-permute-done.2 = f32[33,128]{1,0:T(8,128)S(1)} collective-permute-done((f32[33,128]{1,0:T(8,128)S(1)}, f32[33,128]{1,0:T(8,128)S(1)}, u32[]{:S(2)}, u32[]{:S(2)}) %collective-permute-start.2) | collective-permute-done | bytes 16928 | tf_op jit(solution)/shard_map/ppermute | solution.py:18
  172.1 0.1 maximum_select_fusion
  172.2 0.1 reshape.111
  172.3 0.1 fusion.66
  172.4 0.3 fusion.23
  172.7 0.1 mul.257
  172.8 0.6 fusion.44
  173.4 0.8 all-to-all-done.1
  174.2 3.4 %copy.48 = f32[16,9,8,512]{3,2,0,1:T(8,128)} copy(f32[16,9,8,512]{3,2,1,0:T(8,128)} %bitcast.14) | data formatting | bytes 4718592 | tf_op jit(solution)/shard_map/all_to_all | solution.py:149
  (58 shorter events, 0.2 us)
Async XLA Ops:
  0.6 93.5 %copy-start = (bf16[1152,1152]{1,0:T(8,128)(2,1)S(1)}, bf16[1152,1152]{1,0:T(8,128)(2,1)}, u32[]{:S(2)}) copy-start(bf16[1152,1152]{1,0:T(8,128)(2,1)} %param.10) | copy-start | bytes 7962628
  4.1 9.4 %copy-start.8 = (f32[64,128]{1,0:T(8,128)S(1)}, f32[64,128]{1,0:T(8,128)}, u32[]{:S(2)}) copy-start(f32[64,128]{1,0:T(8,128)} %param.9) | copy-start | bytes 98308
  4.1 17.2 %copy-start.6 = (s32[131072]{0:T(1024)S(1)}, s32[131072]{0:T(1024)}, u32[]{:S(2)}) copy-start(s32[131072]{0:T(1024)} %param.14) | copy-start | bytes 1572868
  4.1 69.2 %all-to-all-start = ((f32[16,512,72]{1,2,0:T(8,128)}), f32[16,512,72]{1,2,0:T(8,128)}, u32[]{:S(2)}, u32[]{:S(2)}) async-start(f32[16,512,72]{1,2,0:T(8,128)} %bitcast.30), calls=%async_computation | async-start | bytes 4718592 | tf_op jit(solution)/shard_map/all_to_all | solution.py:115
  14.1 52.2 %collective-permute-start.1 = (f32[33,128]{1,0:T(8,128)S(1)}, f32[33,128]{1,0:T(8,128)S(1)}, u32[]{:S(2)}, u32[]{:S(2)}) collective-permute-start(f32[33,128]{1,0:T(8,128)S(1)} %get-tuple-element.28), channel_id=1, source_target_pairs={{1,0},{2,1},{3,2},{4,3},{5,4},{6,5},{7,6},{8,7},{9,8},{10,9},{11,1... | collective-permute-start | bytes 50696 | tf_op jit(solution)/shard_map/ppermute | solution.py:18
  24.8 48.6 %copy-start.14 = (f32[520]{0:T(1024)}, f32[520]{0:T(1024)S(1)}, u32[]{:S(2)}) copy-start(f32[520]{0:T(1024)S(1)} %get-tuple-element.13) | copy-start | bytes 6244
  66.3 7.0 %copy-start.11 = (f32[33,128]{1,0:T(8,128)}, f32[33,128]{1,0:T(8,128)S(1)}, u32[]{:S(2)}) copy-start(f32[33,128]{1,0:T(8,128)S(1)} %collective-permute-done.1) | copy-start | bytes 50692
  75.4 10.6 %collective-permute-start = (f32[8,1152]{1,0:T(8,128)}, f32[8,1152]{1,0:T(8,128)S(1)}, u32[]{:S(2)}, u32[]{:S(2)}) collective-permute-start(f32[8,1152]{1,0:T(8,128)} %copy.46), channel_id=1, source_target_pairs={{0,1},{1,2},{2,3},{3,4},{4,5},{5,6},{6,7},{7,8},{8,9},{9,10},{10,1... | collective-permute-start | bytes 110600 | tf_op jit(solution)/shard_map/ppermute | solution.py:24
  81.9 6.0 %copy-start.1 = (f32[512,1152]{1,0:T(8,128)S(1)}, f32[512,1152]{1,0:T(8,128)}, u32[]{:S(2)}) copy-start(f32[512,1152]{1,0:T(8,128)} %copy.41) | copy-start | bytes 7077892
  81.9 6.0 %copy-start.10 = (f32[1152]{0:T(1024)S(1)}, f32[1152]{0:T(1024)}, u32[]{:S(2)}) copy-start(f32[1152]{0:T(1024)} %get-tuple-element.32) | copy-start | bytes 13828
  81.9 6.0 %copy-start.13 = (f32[1152]{0:T(1024)S(1)}, f32[1152]{0:T(1024)}, u32[]{:S(2)}) copy-start(f32[1152]{0:T(1024)} %param.13) | copy-start | bytes 13828
  81.9 6.0 %copy-start.15 = (f32[520]{0:T(1024)S(1)}, f32[520]{0:T(1024)}, u32[]{:S(2)}) copy-start(f32[520]{0:T(1024)} %copy-done.14) | copy-start | bytes 6244
  87.9 3.5 %copy-start.7 = (bf16[1152,128]{1,0:T(8,128)(2,1)S(1)}, bf16[1152,128]{1,0:T(8,128)(2,1)}, u32[]{:S(2)}) copy-start(bf16[1152,128]{1,0:T(8,128)(2,1)} %param.12) | copy-start | bytes 884740
  87.9 4.0 %copy-start.18 = (f32[64]{0:T(128)S(1)}, f32[64]{0:T(128)}, u32[]{:S(2)}) copy-start(f32[64]{0:T(128)} %convert_reduce_fusion) | copy-start | bytes 772
  87.9 4.2 %copy-start.9 = (f32[33,128]{1,0:T(8,128)S(1)}, f32[33,128]{1,0:T(8,128)}, u32[]{:S(2)}) copy-start(f32[33,128]{1,0:T(8,128)} %get-tuple-element.27) | copy-start | bytes 50692
  87.9 4.2 %copy-start.12 = (f32[33,128]{1,0:T(8,128)S(1)}, f32[33,128]{1,0:T(8,128)}, u32[]{:S(2)}) copy-start(f32[33,128]{1,0:T(8,128)} %copy-done.11) | copy-start | bytes 50692
  87.9 4.2 %copy-start.22 = (pred[64]{0:T(512)(128)(4,1)S(1)}, pred[64]{0:T(512)(128)(4,1)}, u32[]{:S(2)}) copy-start(pred[64]{0:T(512)(128)(4,1)} %get-tuple-element.33) | copy-start | bytes 196
  88.0 4.2 %copy-start.23 = (pred[64]{0:T(512)(128)(4,1)S(1)}, pred[64]{0:T(512)(128)(4,1)}, u32[]{:S(2)}) copy-start(pred[64]{0:T(512)(128)(4,1)} %get-tuple-element.34) | copy-start | bytes 196
  90.4 1.0 copy-start.4
  90.4 2.2 %copy-start.16 = (s32[1024]{0:T(1024)S(1)}, s32[1024]{0:T(1024)}, u32[]{:S(2)}) copy-start(s32[1024]{0:T(1024)} %pad_clamp_fusion) | copy-start | bytes 12292
  90.4 3.2 %copy-start.20 = (pred[512]{0:T(512)(128)(4,1)S(1)}, pred[512]{0:T(512)(128)(4,1)}, u32[]{:S(2)}) copy-start(pred[512]{0:T(512)(128)(4,1)} %get-tuple-element.10) | copy-start | bytes 1540
  94.1 3.4 %copy-start.3 = (f32[520,1152]{1,0:T(8,128)S(1)}, f32[520,1152]{1,0:T(8,128)}, u32[]{:S(2)}) copy-start(f32[520,1152]{1,0:T(8,128)} %get-tuple-element.15) | copy-start | bytes 7188484
  94.1 3.4 %copy-start.5 = (bf16[520,1152]{1,0:T(8,128)(2,1)S(1)}, bf16[520,1152]{1,0:T(8,128)(2,1)}, u32[]{:S(2)}) copy-start(bf16[520,1152]{1,0:T(8,128)(2,1)} %copy-done.4) | copy-start | bytes 3594244
  94.1 3.4 %copy-start.19 = (f32[520]{0:T(1024)S(1)}, f32[520]{0:T(1024)}, u32[]{:S(2)}) copy-start(f32[520]{0:T(1024)} %get-tuple-element.12) | copy-start | bytes 6244
  94.1 3.4 %copy-start.24 = (bf16[1152,1152]{1,0:T(8,128)(2,1)S(1)}, bf16[1152,1152]{1,0:T(8,128)(2,1)}, u32[]{:S(2)}) copy-start(bf16[1152,1152]{1,0:T(8,128)(2,1)} %param.11) | copy-start | bytes 7962628
  97.5 2.1 %copy-start.17 = (f32[512]{0:T(512)S(1)}, f32[512]{0:T(512)}, u32[]{:S(2)}) copy-start(f32[512]{0:T(512)} %get-tuple-element.30) | copy-start | bytes 6148
  100.6 1.9 %copy-start.2 = (f32[512,1152]{1,0:T(8,128)}, f32[512,1152]{1,0:T(8,128)S(1)}, u32[]{:S(2)}) copy-start(f32[512,1152]{1,0:T(8,128)S(1)} %fusion.13) | copy-start | bytes 7077892
  100.6 1.9 %copy-start.21 = (f32[512]{0:T(512)S(1)}, f32[512]{0:T(512)}, u32[]{:S(2)}) copy-start(f32[512]{0:T(512)} %get-tuple-element.29) | copy-start | bytes 6148
  109.1 65.1 %all-to-all-start.1 = ((f32[512,16,72]{0,2,1:T(8,128)}), f32[512,16,72]{0,2,1:T(8,128)}, u32[]{:S(2)}, u32[]{:S(2)}) async-start(f32[512,16,72]{0,2,1:T(8,128)} %bitcast.31), calls=%async_computation.1 | async-start | bytes 4718592 | tf_op jit(solution)/shard_map/all_to_all | solution.py:149
  114.0 58.1 %collective-permute-start.2 = (f32[33,128]{1,0:T(8,128)S(1)}, f32[33,128]{1,0:T(8,128)S(1)}, u32[]{:S(2)}, u32[]{:S(2)}) collective-permute-start(f32[33,128]{1,0:T(8,128)S(1)} %get-tuple-element.25), channel_id=1, source_target_pairs={{255,0},{0,1},{1,2},{2,3},{3,4},{4,5},{5,6},{6,7},{7,8},{8,9},{9,1... | collective-permute-start | bytes 50696 | tf_op jit(solution)/shard_map/ppermute | solution.py:18
  116.9 55.9 %collective-permute-start.3 = (f32[32,128]{1,0:T(8,128)S(1)}, f32[32,128]{1,0:T(8,128)S(1)}, u32[]{:S(2)}, u32[]{:S(2)}) collective-permute-start(f32[32,128]{1,0:T(8,128)S(1)} %get-tuple-element.23), channel_id=1, source_target_pairs={{255,0},{0,1},{1,2},{2,3},{3,4},{4,5},{5,6},{6,7},{7,8},{8,9},{9,1... | collective-permute-start | bytes 49160 | tf_op jit(solution)/shard_map/ppermute | solution.py:18

commit v8 on v7

--- a/solution.py
+++ b/solution.py
@@ -4,6 +4,7 @@
 import jax.numpy as jnp
 from jax import lax
 from jax.sharding import PartitionSpec as P
+
 
 NDIR = 36
 LEVELS = 64
@@ -73,7 +74,7 @@
     return window + 0.2 * lap_h + 0.2 * lap_v + 1.5 * forcing - 0.05 * window
 
 
-def per_device(
+def steps(
     spectrum, velocity, source_a, source_b, stokes_kernel, group_speed, column_map, land_mask
 ):
     bin_count = lax.axis_size("bin")
@@ -153,6 +154,4 @@
 def solution(mesh):
     in_specs = (P("band", "bin"), P(ALL, None), P(), P(), P(), P(), P(), P())
     out_specs = (P("band", "bin"), P(ALL, None))
-    return jax.shard_map(
-        per_device, mesh=mesh, in_specs=in_specs, out_specs=out_specs, check_vma=False
-    )
+    return jax.shard_map(steps, mesh=mesh, in_specs=in_specs, out_specs=out_specs, check_vma=False)

time: 180 us -> 180 us (level)
  no operation moved by 1% of the time
where the time goes in v8:
time: 180 us; the launch traced here: 178 us
  waiting for transfers between devices  101 us (56%)
  starting transfers between devices  25.7 us (14%)
  local copies, waits for them, and re-layouts  22.8 us (13%)
  matrix products  13.7 us (8%)
  other arithmetic  12.9 us (7%)
    ppermute x3, waiting for transfers between devices, shifted(): return lax.ppermute(block, axis, route)  92.6 us
    all_to_all x1, starting transfers between devices, steps(): lax.all_to_all(spectrum, 'bin', split_axis=0, concat_axis=1, tiled=True)  9.41 us
    ppermute x3, starting transfers between devices, shifted(): return lax.ppermute(block, axis, route)  9.31 us
    all_to_all x2, local copies, waits for them, and re-layouts, steps(): lax.all_to_all(spectrum, 'bin', split_axis=0, concat_axis=1, tiled=True)  6.48 us
    dot_general x2, matrix products, sources(): other = jnp.dot(rounded, source_b, preferred_element_type=jnp.float32)  5.44 us
    dot_general x2, matrix products, sources(): gain = jnp.dot(rounded, source_a, preferred_element_type=jnp.float32)  5.18 us
    all_to_all x1, starting transfers between devices, steps(): lax.all_to_all(field, 'bin', split_axis=1, concat_axis=0, tiled=True)  4.9 us
    ppermute x1, waiting for transfers between devices, from_behind(): return lax.ppermute(shard, axis, pairs)  4.16 us
  transfers between devices with their start and end apart: 6, of which 5 were waited for; matrix products, arithmetic and copies ran while one was open for 10% of the time, Pallas kernels for 0%

profile of v8, /device:TPU:88, one launch (start us, length us, event | category | flops | bytes accessed | tf_op | source)
XLA Modules:
  0.0 177.6 jit_solution(10473453872866420865)
XLA Ops:
  0.6 0.0 copy-start
  0.6 3.4 %copy.50 = f32[9,16,8,512]{3,2,0,1:T(8,128)} copy(f32[9,16,8,512]{3,2,1,0:T(8,128)} %bitcast.32) | data formatting | bytes 4718592 | tf_op jit(solution)/shard_map/all_to_all | solution.py:116
  4.1 9.4 %all-to-all-start = ((f32[16,512,72]{1,2,0:T(8,128)}), f32[16,512,72]{1,2,0:T(8,128)}, u32[]{:S(2)}, u32[]{:S(2)}) async-start(f32[16,512,72]{1,2,0:T(8,128)} %bitcast.30), calls=%async_computation | async-start | bytes 4718592 | tf_op jit(solution)/shard_map/all_to_all | solution.py:116
  13.5 0.6 fusion.70
  14.1 7.2 %collective-permute-start.1 = (f32[33,128]{1,0:T(8,128)S(1)}, f32[33,128]{1,0:T(8,128)S(1)}, u32[]{:S(2)}, u32[]{:S(2)}) collective-permute-start(f32[33,128]{1,0:T(8,128)S(1)} %get-tuple-element.28), channel_id=1, source_target_pairs={{1,0},{2,1},{3,2},{4,3},{5,4},{6,5},{7,6},{8,7},{9,8},{10,9},{11,1... | collective-permute-start | bytes 50696 | tf_op jit(solution)/shard_map/ppermute | solution.py:19
  21.3 0.1 slice.132
  21.4 0.8 slice.128
  22.1 0.1 compare_and_fusion
  22.2 0.6 compare_and_fusion.3
  22.8 0.6 pad_clamp_fusion
  23.4 1.4 broadcast_multiply_fusion
  24.8 0.7 fusion.50
  25.4 0.6 convert_reduce_fusion
  26.1 0.6 broadcast_multiply_fusion.1
  26.7 0.6 compare_and_fusion.1
  27.3 39.0 %collective-permute-done.1 = f32[33,128]{1,0:T(8,128)S(1)} collective-permute-done((f32[33,128]{1,0:T(8,128)S(1)}, f32[33,128]{1,0:T(8,128)S(1)}, u32[]{:S(2)}, u32[]{:S(2)}) %collective-permute-start.1) | collective-permute-done | bytes 16928 | tf_op jit(solution)/shard_map/ppermute | solution.py:19
  66.3 0.2 maximum_reduce_fusion
  66.5 0.1 copy.42
  66.6 0.1 reshape.110
  66.8 1.6 gather_fusion
  68.3 0.1 fusion.67
  68.5 0.9 fusion.26
  69.4 0.1 select_bitcast_fusion
  69.5 3.8 %all-to-all-done = f32[16,512,72]{1,2,0:T(8,128)} async-done(((f32[16,512,72]{1,2,0:T(8,128)}), f32[16,512,72]{1,2,0:T(8,128)}, u32[]{:S(2)}, u32[]{:S(2)}) %all-to-all-start) | async-done | bytes 2359328 | tf_op jit(solution)/shard_map/all_to_all | solution.py:116
  73.3 1.3 slice.171
  74.6 0.8 copy.46
  75.4 2.1 %collective-permute-start = (f32[8,1152]{1,0:T(8,128)}, f32[8,1152]{1,0:T(8,128)S(1)}, u32[]{:S(2)}, u32[]{:S(2)}) collective-permute-start(f32[8,1152]{1,0:T(8,128)} %copy.46), channel_id=1, source_target_pairs={{0,1},{1,2},{2,3},{3,4},{4,5},{5,6},{6,7},{7,8},{8,9},{9,10},{10,1... | collective-permute-start | bytes 110600 | tf_op jit(solution)/shard_map/ppermute | solution.py:25
  77.5 0.3 fusion.18
  77.9 0.9 mul.233
  78.8 3.0 %copy.41 = f32[512,1152]{1,0:T(8,128)} copy(f32[512,1152]{0,1:T(8,128)} %bitcast.2) | data formatting | bytes 4718592 | tf_op jit(solution)/shard_map/all_to_all | solution.py:116
  81.9 4.2 %collective-permute-done = f32[8,1152]{1,0:T(8,128)S(1)} collective-permute-done((f32[8,1152]{1,0:T(8,128)}, f32[8,1152]{1,0:T(8,128)S(1)}, u32[]{:S(2)}, u32[]{:S(2)}) %collective-permute-start) | collective-permute-done | bytes 36896 | tf_op jit(solution)/shard_map/ppermute | solution.py:25
  86.0 1.8 %fusion.10 = f32[519,1152]{1,0:T(8,128)S(1)} fusion(f32[8,1152]{1,0:T(8,128)S(1)} %collective-permute-done, f32[512,1152]{1,0:T(8,128)} %copy.41), kind=kLoop, calls=%fused_computation.16 | loop fusion | flops 597888 | bytes 4787712 | tf_op jit(solution)/shard_map/concatenate | solution.py:118
  88.0 2.5 %fusion.64 = (bf16[520,1152]{1,0:T(8,128)(2,1)S(1)}, f32[520,1152]{1,0:T(8,128)}) fusion(f32[519,1152]{1,0:T(8,128)S(1)} %fusion.10, f32[1152]{0:T(1024)S(1)} %get-tuple-element.31, f32[520]{0:T(1024)S(1)} %get-tuple-element.3, f32[1152]{0:T(1024)S(1)} %copy-done.10, f32[520]{0:T(1024)S(1)} %get-tuple-element.2, f32[1152]{0:T(1024)S(1)} %copy-done.13, ...), kind=kLoop, calls=%fused_computation.122 | loop fusion | flops 6589440 | bytes 8402016 | tf_op jit(solution)/shard_map/convert_element_type | solution.py:124
  90.4 1.0 copy-done.4
  91.4 0.5 fusion.14
  91.9 0.2 fusion.16
  92.2 0.1 fusion.38
  92.3 0.2 slice_reduce_fusion.1
  92.5 0.1 copy.43
  92.6 1.0 gather_fusion.1
  93.7 0.1 select_bitcast_fusion.1
  93.8 0.3 fusion.20
  94.1 0.0 copy-start.5
  94.1 0.0 copy-start.24
  94.2 3.3 %fusion.71 = f32[520,1152]{1,0:T(8,128)S(1)} fusion(bf16[520,1152]{1,0:T(8,128)(2,1)} %copy-done.4, bf16[1152,1152]{1,0:T(8,128)(2,1)S(1)} %copy-done), kind=kOutput, calls=%fused_computation.128 | convolution fusion | flops 1380188160 | bytes 6248448 | tf_op jit(solution)/shard_map/dot_general | solution.py:44
  97.5 2.0 %fusion.6 = f32[520,1152]{1,0:T(8,128)S(1)} fusion(f32[520,1152]{1,0:T(8,128)S(1)} %copy-done.3, f32[520,1152]{1,0:T(8,128)S(1)} %fusion.71, bf16[520,1152]{1,0:T(8,128)(2,1)S(1)} %copy-done.5, bf16[1152,1152]{1,0:T(8,128)(2,1)S(1)} %copy-done.24, f32[520]{0:T(1024)S(1)} %copy-done.19), kind=kOutput, calls=%fused_computation.12 | convolution fusion | flops 1384381440 | bytes 11042848 | tf_op jit(solution)/shard_map/dot_general | solution.py:45
  99.6 1.0 fusion.13
  100.6 1.8 %fusion.61 = f32[512,1152]{1,0:T(8,128)S(1)} fusion(bf16[1152,1152]{1,0:T(8,128)(2,1)S(1)} %copy-done, f32[512,1152]{1,0:T(8,128)S(1)} %fusion.13), kind=kOutput, calls=%fused_computation.120 | convolution fusion | flops 1359544320 | bytes 7372800 | tf_op jit(solution)/shard_map/dot_general | solution.py:44
  102.5 3.4 %fusion.9 = f32[512,1152]{1,0:T(8,128)} fusion(f32[512,1152]{1,0:T(8,128)S(1)} %fusion.13, f32[512,1152]{1,0:T(8,128)S(1)} %fusion.61, bf16[1152,1152]{1,0:T(8,128)(2,1)S(1)} %copy-done.24, f32[512]{0:T(512)S(1)} %copy-done.21), kind=kOutput, calls=%fused_computation.15 | convolution fusion | flops 1363673088 | bytes 9734144 | tf_op jit(solution)/shard_map/dot_general | solution.py:45
  105.9 3.2 %copy.44 = f32[512,1152]{0,1:T(8,128)} copy(f32[512,1152]{1,0:T(8,128)} %fusion.9) | data formatting | bytes 4718592 | tf_op jit(solution)/shard_map/add | solution.py:126
  109.1 4.9 %all-to-all-start.1 = ((f32[512,16,72]{0,2,1:T(8,128)}), f32[512,16,72]{0,2,1:T(8,128)}, u32[]{:S(2)}, u32[]{:S(2)}) async-start(f32[512,16,72]{0,2,1:T(8,128)} %bitcast.31), calls=%async_computation.1 | async-start | bytes 4718592 | tf_op jit(solution)/shard_map/all_to_all | solution.py:150
  114.0 0.4 collective-permute-start.2
  114.5 2.1 %fusion.58 = f32[512,128]{1,0:T(8,128)S(1)} fusion(bf16[1152,128]{1,0:T(8,128)(2,1)S(1)} %copy-done.7, f32[512,1152]{1,0:T(8,128)} %copy-done.2), kind=kOutput, calls=%fused_computation.117 | convolution fusion | flops 151584768 | bytes 2916352 | tf_op jit(solution)/shard_map/dot_general | solution.py:47
  116.6 0.2 convolution_divide_fusion
  116.9 1.7 collective-permute-start.3
  118.6 53.5 %collective-permute-done.2 = f32[33,128]{1,0:T(8,128)S(1)} collective-permute-done((f32[33,128]{1,0:T(8,128)S(1)}, f32[33,128]{1,0:T(8,128)S(1)}, u32[]{:S(2)}, u32[]{:S(2)}) %collective-permute-start.2) | collective-permute-done | bytes 16928 | tf_op jit(solution)/shard_map/ppermute | solution.py:19
  172.1 0.1 maximum_select_fusion
  172.2 0.1 reshape.111
  172.3 0.1 fusion.66
  172.4 0.3 fusion.23
  172.7 0.1 mul.257
  172.8 0.6 fusion.44
  173.4 0.8 all-to-all-done.1
  174.2 3.4 %copy.48 = f32[16,9,8,512]{3,2,0,1:T(8,128)} copy(f32[16,9,8,512]{3,2,1,0:T(8,128)} %bitcast.14) | data formatting | bytes 4718592 | tf_op jit(solution)/shard_map/all_to_all | solution.py:150
  (58 shorter events, 0.2 us)
Async XLA Ops:
  0.6 93.5 %copy-start = (bf16[1152,1152]{1,0:T(8,128)(2,1)S(1)}, bf16[1152,1152]{1,0:T(8,128)(2,1)}, u32[]{:S(2)}) copy-start(bf16[1152,1152]{1,0:T(8,128)(2,1)} %param.10) | copy-start | bytes 7962628
  4.1 9.4 %copy-start.8 = (f32[64,128]{1,0:T(8,128)S(1)}, f32[64,128]{1,0:T(8,128)}, u32[]{:S(2)}) copy-start(f32[64,128]{1,0:T(8,128)} %param.9) | copy-start | bytes 98308
  4.1 17.2 %copy-start.6 = (s32[131072]{0:T(1024)S(1)}, s32[131072]{0:T(1024)}, u32[]{:S(2)}) copy-start(s32[131072]{0:T(1024)} %param.14) | copy-start | bytes 1572868
  4.1 69.2 %all-to-all-start = ((f32[16,512,72]{1,2,0:T(8,128)}), f32[16,512,72]{1,2,0:T(8,128)}, u32[]{:S(2)}, u32[]{:S(2)}) async-start(f32[16,512,72]{1,2,0:T(8,128)} %bitcast.30), calls=%async_computation | async-start | bytes 4718592 | tf_op jit(solution)/shard_map/all_to_all | solution.py:116
  14.1 52.2 %collective-permute-start.1 = (f32[33,128]{1,0:T(8,128)S(1)}, f32[33,128]{1,0:T(8,128)S(1)}, u32[]{:S(2)}, u32[]{:S(2)}) collective-permute-start(f32[33,128]{1,0:T(8,128)S(1)} %get-tuple-element.28), channel_id=1, source_target_pairs={{1,0},{2,1},{3,2},{4,3},{5,4},{6,5},{7,6},{8,7},{9,8},{10,9},{11,1... | collective-permute-start | bytes 50696 | tf_op jit(solution)/shard_map/ppermute | solution.py:19
  24.8 48.6 %copy-start.14 = (f32[520]{0:T(1024)}, f32[520]{0:T(1024)S(1)}, u32[]{:S(2)}) copy-start(f32[520]{0:T(1024)S(1)} %get-tuple-element.13) | copy-start | bytes 6244
  66.3 7.0 %copy-start.11 = (f32[33,128]{1,0:T(8,128)}, f32[33,128]{1,0:T(8,128)S(1)}, u32[]{:S(2)}) copy-start(f32[33,128]{1,0:T(8,128)S(1)} %collective-permute-done.1) | copy-start | bytes 50692
  75.4 10.6 %collective-permute-start = (f32[8,1152]{1,0:T(8,128)}, f32[8,1152]{1,0:T(8,128)S(1)}, u32[]{:S(2)}, u32[]{:S(2)}) collective-permute-start(f32[8,1152]{1,0:T(8,128)} %copy.46), channel_id=1, source_target_pairs={{0,1},{1,2},{2,3},{3,4},{4,5},{5,6},{6,7},{7,8},{8,9},{9,10},{10,1... | collective-permute-start | bytes 110600 | tf_op jit(solution)/shard_map/ppermute | solution.py:25
  81.9 6.0 %copy-start.1 = (f32[512,1152]{1,0:T(8,128)S(1)}, f32[512,1152]{1,0:T(8,128)}, u32[]{:S(2)}) copy-start(f32[512,1152]{1,0:T(8,128)} %copy.41) | copy-start | bytes 7077892
  81.9 6.0 %copy-start.10 = (f32[1152]{0:T(1024)S(1)}, f32[1152]{0:T(1024)}, u32[]{:S(2)}) copy-start(f32[1152]{0:T(1024)} %get-tuple-element.32) | copy-start | bytes 13828
  81.9 6.0 %copy-start.13 = (f32[1152]{0:T(1024)S(1)}, f32[1152]{0:T(1024)}, u32[]{:S(2)}) copy-start(f32[1152]{0:T(1024)} %param.13) | copy-start | bytes 13828
  81.9 6.0 %copy-start.15 = (f32[520]{0:T(1024)S(1)}, f32[520]{0:T(1024)}, u32[]{:S(2)}) copy-start(f32[520]{0:T(1024)} %copy-done.14) | copy-start | bytes 6244
  87.9 3.5 %copy-start.7 = (bf16[1152,128]{1,0:T(8,128)(2,1)S(1)}, bf16[1152,128]{1,0:T(8,128)(2,1)}, u32[]{:S(2)}) copy-start(bf16[1152,128]{1,0:T(8,128)(2,1)} %param.12) | copy-start | bytes 884740
  87.9 4.0 %copy-start.18 = (f32[64]{0:T(128)S(1)}, f32[64]{0:T(128)}, u32[]{:S(2)}) copy-start(f32[64]{0:T(128)} %convert_reduce_fusion) | copy-start | bytes 772
  87.9 4.2 %copy-start.9 = (f32[33,128]{1,0:T(8,128)S(1)}, f32[33,128]{1,0:T(8,128)}, u32[]{:S(2)}) copy-start(f32[33,128]{1,0:T(8,128)} %get-tuple-element.27) | copy-start | bytes 50692
  87.9 4.2 %copy-start.12 = (f32[33,128]{1,0:T(8,128)S(1)}, f32[33,128]{1,0:T(8,128)}, u32[]{:S(2)}) copy-start(f32[33,128]{1,0:T(8,128)} %copy-done.11) | copy-start | bytes 50692
  87.9 4.2 %copy-start.22 = (pred[64]{0:T(512)(128)(4,1)S(1)}, pred[64]{0:T(512)(128)(4,1)}, u32[]{:S(2)}) copy-start(pred[64]{0:T(512)(128)(4,1)} %get-tuple-element.33) | copy-start | bytes 196
  88.0 4.2 %copy-start.23 = (pred[64]{0:T(512)(128)(4,1)S(1)}, pred[64]{0:T(512)(128)(4,1)}, u32[]{:S(2)}) copy-start(pred[64]{0:T(512)(128)(4,1)} %get-tuple-element.34) | copy-start | bytes 196
  90.4 1.0 copy-start.4
  90.4 2.2 %copy-start.16 = (s32[1024]{0:T(1024)S(1)}, s32[1024]{0:T(1024)}, u32[]{:S(2)}) copy-start(s32[1024]{0:T(1024)} %pad_clamp_fusion) | copy-start | bytes 12292
  90.4 3.2 %copy-start.20 = (pred[512]{0:T(512)(128)(4,1)S(1)}, pred[512]{0:T(512)(128)(4,1)}, u32[]{:S(2)}) copy-start(pred[512]{0:T(512)(128)(4,1)} %get-tuple-element.10) | copy-start | bytes 1540
  94.1 3.4 %copy-start.3 = (f32[520,1152]{1,0:T(8,128)S(1)}, f32[520,1152]{1,0:T(8,128)}, u32[]{:S(2)}) copy-start(f32[520,1152]{1,0:T(8,128)} %get-tuple-element.15) | copy-start | bytes 7188484
  94.1 3.4 %copy-start.5 = (bf16[520,1152]{1,0:T(8,128)(2,1)S(1)}, bf16[520,1152]{1,0:T(8,128)(2,1)}, u32[]{:S(2)}) copy-start(bf16[520,1152]{1,0:T(8,128)(2,1)} %copy-done.4) | copy-start | bytes 3594244
  94.1 3.4 %copy-start.19 = (f32[520]{0:T(1024)S(1)}, f32[520]{0:T(1024)}, u32[]{:S(2)}) copy-start(f32[520]{0:T(1024)} %get-tuple-element.12) | copy-start | bytes 6244
  94.1 3.4 %copy-start.24 = (bf16[1152,1152]{1,0:T(8,128)(2,1)S(1)}, bf16[1152,1152]{1,0:T(8,128)(2,1)}, u32[]{:S(2)}) copy-start(bf16[1152,1152]{1,0:T(8,128)(2,1)} %param.11) | copy-start | bytes 7962628
  97.5 2.1 %copy-start.17 = (f32[512]{0:T(512)S(1)}, f32[512]{0:T(512)}, u32[]{:S(2)}) copy-start(f32[512]{0:T(512)} %get-tuple-element.30) | copy-start | bytes 6148
  100.6 1.9 %copy-start.2 = (f32[512,1152]{1,0:T(8,128)}, f32[512,1152]{1,0:T(8,128)S(1)}, u32[]{:S(2)}) copy-start(f32[512,1152]{1,0:T(8,128)S(1)} %fusion.13) | copy-start | bytes 7077892
  100.6 1.9 %copy-start.21 = (f32[512]{0:T(512)S(1)}, f32[512]{0:T(512)}, u32[]{:S(2)}) copy-start(f32[512]{0:T(512)} %get-tuple-element.29) | copy-start | bytes 6148
  109.1 65.1 %all-to-all-start.1 = ((f32[512,16,72]{0,2,1:T(8,128)}), f32[512,16,72]{0,2,1:T(8,128)}, u32[]{:S(2)}, u32[]{:S(2)}) async-start(f32[512,16,72]{0,2,1:T(8,128)} %bitcast.31), calls=%async_computation.1 | async-start | bytes 4718592 | tf_op jit(solution)/shard_map/all_to_all | solution.py:150
  114.0 58.1 %collective-permute-start.2 = (f32[33,128]{1,0:T(8,128)S(1)}, f32[33,128]{1,0:T(8,128)S(1)}, u32[]{:S(2)}, u32[]{:S(2)}) collective-permute-start(f32[33,128]{1,0:T(8,128)S(1)} %get-tuple-element.25), channel_id=1, source_target_pairs={{255,0},{0,1},{1,2},{2,3},{3,4},{4,5},{5,6},{6,7},{7,8},{8,9},{9,1... | collective-permute-start | bytes 50696 | tf_op jit(solution)/shard_map/ppermute | solution.py:19
  116.9 55.9 %collective-permute-start.3 = (f32[32,128]{1,0:T(8,128)S(1)}, f32[32,128]{1,0:T(8,128)S(1)}, u32[]{:S(2)}, u32[]{:S(2)}) collective-permute-start(f32[32,128]{1,0:T(8,128)S(1)} %get-tuple-element.23), channel_id=1, source_target_pairs={{255,0},{0,1},{1,2},{2,3},{3,4},{4,5},{5,6},{6,7},{7,8},{8,9},{9,1... | collective-permute-start | bytes 49160 | tf_op jit(solution)/shard_map/ppermute | solution.py:19

commit v9 on v7

--- a/solution.py
+++ b/solution.py
@@ -114,20 +114,25 @@
 
     body = lax.all_to_all(spectrum, "bin", split_axis=0, concat_axis=1, tiled=True)
     head = from_behind(body[-EXTRA:], ALL, 1)
-    field = jnp.concatenate([head, body], 0)
-    prev = jnp.zeros((1, bins), jnp.float32)
-    mask = ext_mask
+    head_current = current[:, :EXTRA]
+    current = current[:, EXTRA:]
+    head_mask = ext_mask[:EXTRA]
+    head_moved = propagate(
+        head, jnp.zeros((1, bins), jnp.float32), head_current, group_speed, cos_b, sin_b, head_mask
+    )
+    head_increment, _ = sources(
+        head_moved.astype(jnp.bfloat16), head_mask, source_a, source_b, stokes_kernel
+    )
+    later_prev = (head_moved + head_increment.astype(jnp.float32))[-1:]
+    field = body
+    prev = head[-1:]
     for step in range(STEPS):
-        moved = propagate(field, prev, current, group_speed, cos_b, sin_b, mask)
+        moved = propagate(field, prev, current, group_speed, cos_b, sin_b, local_mask)
         increment, stokes = sources(
-            moved.astype(jnp.bfloat16), mask, source_a, source_b, stokes_kernel
+            moved.astype(jnp.bfloat16), local_mask, source_a, source_b, stokes_kernel
         )
         field = moved + increment.astype(jnp.float32)
-        if step == 0:
-            prev = field[EXTRA - 1 : EXTRA]
-            field = field[EXTRA:]
-            stokes = stokes[EXTRA:]
-            mask = local_mask
+        prev = later_prev
         sums = jnp.dot(onehot, stokes, precision=lax.Precision.HIGHEST)
         forcing = sums / counts[:, None]
         if step + 1 < STEPS:

time: 180 us -> 186 us (1.033)
  matrix products: 13.7 us -> 20.1 us
  local copies, waits for them, and re-layouts: 22.8 us -> 27.6 us
  waiting for transfers between devices: 101 us -> 96.2 us
  other arithmetic: 12.9 us -> 10.6 us
    dot_general x2 -> x3, matrix products: 5.44 us -> 11.4 us  [sources(): other = jnp.dot(rounded, source_b, preferred_element_type=jnp.float32)]
    slice x0 -> x3, local copies, waits for them, and re-layouts: none -> 3.74 us  [the longest x1 3.08 us: propagate(): behind = jnp.concatenate([prev, field[:-1]], 0)]
    ppermute x1, waiting for transfers between devices: 4.16 us -> 1.23 us  [from_behind(): return lax.ppermute(shard, axis, pairs)]
    ppermute x3, waiting for transfers between devices: 92.6 us -> 89.8 us  [shifted(): return lax.ppermute(block, axis, route)]
    dot_general x2 -> x3, matrix products: 5.18 us -> 5.61 us  [sources(): gain = jnp.dot(rounded, source_a, preferred_element_type=jnp.float32)]
  transfers between devices with their start and end apart: 6 -> 6, of which waited for: 5 -> 5; matrix products, arithmetic and copies ran while one was open for 10% -> 12% of each run, Pallas kernels for 0% -> 0%
where the time goes in v9:
time: 186 us; the launch traced here: 183 us
  waiting for transfers between devices  96.2 us (52%)
  local copies, waits for them, and re-layouts  27.6 us (15%)
  starting transfers between devices  27.5 us (15%)
  matrix products  20.1 us (11%)
  other arithmetic  10.6 us (6%)
    ppermute x3, waiting for transfers between devices, shifted(): return lax.ppermute(block, axis, route)  89.8 us
    dot_general x3, matrix products, sources(): other = jnp.dot(rounded, source_b, preferred_element_type=jnp.float32)  11.4 us
    all_to_all x1, starting transfers between devices, per_device(): lax.all_to_all(spectrum, 'bin', split_axis=0, concat_axis=1, tiled=True)  9.41 us
    ppermute x3, starting transfers between devices, shifted(): return lax.ppermute(block, axis, route)  9.3 us
    all_to_all x1, starting transfers between devices, per_device(): lax.all_to_all(field, 'bin', split_axis=1, concat_axis=0, tiled=True)  6.69 us
    all_to_all x2, local copies, waits for them, and re-layouts, per_device(): lax.all_to_all(spectrum, 'bin', split_axis=0, concat_axis=1, tiled=True)  6.48 us
    dot_general x3, matrix products, sources(): gain = jnp.dot(rounded, source_a, preferred_element_type=jnp.float32)  5.61 us
  transfers between devices with their start and end apart: 6, of which 5 were waited for; matrix products, arithmetic and copies ran while one was open for 12% of the time, Pallas kernels for 0%

profile of v9, /device:TPU:88, one launch (start us, length us, event | category | flops | bytes accessed | tf_op | source)
XLA Modules:
  0.0 183.1 jit_solution(4554173794178693183)
XLA Ops:
  0.6 3.4 %copy.59 = f32[9,16,8,512]{3,2,0,1:T(8,128)} copy(f32[9,16,8,512]{3,2,1,0:T(8,128)} %bitcast.37) | data formatting | bytes 4718592 | tf_op jit(solution)/shard_map/all_to_all | solution.py:115
  4.1 9.4 %all-to-all-start = ((f32[16,512,72]{1,2,0:T(8,128)}), f32[16,512,72]{1,2,0:T(8,128)}, u32[]{:S(2)}, u32[]{:S(2)}) async-start(f32[16,512,72]{1,2,0:T(8,128)} %bitcast.34), calls=%async_computation | async-start | bytes 4718592 | tf_op jit(solution)/shard_map/all_to_all | solution.py:115
  13.5 0.6 fusion.80
  14.1 7.2 %collective-permute-start = (f32[33,128]{1,0:T(8,128)S(1)}, f32[33,128]{1,0:T(8,128)S(1)}, u32[]{:S(2)}, u32[]{:S(2)}) collective-permute-start(f32[33,128]{1,0:T(8,128)S(1)} %get-tuple-element.26), channel_id=1, source_target_pairs={{1,0},{2,1},{3,2},{4,3},{5,4},{6,5},{7,6},{8,7},{9,8},{10,9},{11,1... | collective-permute-start | bytes 50696 | tf_op jit(solution)/shard_map/ppermute | solution.py:18
  21.4 0.8 slice.148
  22.1 0.8 fusion.63
  23.0 0.6 compare_and_fusion.3
  23.6 0.6 pad_clamp_fusion
  24.2 0.7 fusion.54
  24.9 0.7 convert_reduce_fusion
  25.6 0.6 broadcast_multiply_fusion.2
  26.2 0.6 broadcast_multiply_fusion.1
  26.8 0.5 compare_and_fusion.1
  27.4 0.6 slice.218
  28.0 38.3 %collective-permute-done = f32[33,128]{1,0:T(8,128)S(1)} collective-permute-done((f32[33,128]{1,0:T(8,128)S(1)}, f32[33,128]{1,0:T(8,128)S(1)}, u32[]{:S(2)}, u32[]{:S(2)}) %collective-permute-start) | collective-permute-done | bytes 16928 | tf_op jit(solution)/shard_map/ppermute | solution.py:18
  66.3 0.1 reshape.123
  66.4 0.2 maximum_reduce_fusion
  66.6 0.3 copy-done.12
  66.9 0.1 copy.47
  67.0 1.6 gather_fusion
  68.6 0.1 select_bitcast_fusion
  68.8 0.9 fusion.20
  69.7 0.1 fusion.77
  69.8 0.9 fusion.26
  70.7 2.6 %all-to-all-done = f32[16,512,72]{1,2,0:T(8,128)} async-done(((f32[16,512,72]{1,2,0:T(8,128)}), f32[16,512,72]{1,2,0:T(8,128)}, u32[]{:S(2)}, u32[]{:S(2)}) %all-to-all-start) | async-done | bytes 2359328 | tf_op jit(solution)/shard_map/all_to_all | solution.py:115
  73.3 1.3 slice.201
  74.6 0.8 copy.55
  75.4 2.1 %collective-permute-start.1 = (f32[8,1152]{1,0:T(8,128)}, f32[8,1152]{1,0:T(8,128)S(1)}, u32[]{:S(2)}, u32[]{:S(2)}) collective-permute-start(f32[8,1152]{1,0:T(8,128)} %copy.55), channel_id=1, source_target_pairs={{0,1},{1,2},{2,3},{3,4},{4,5},{5,6},{6,7},{7,8},{8,9},{9,10},{10,1... | collective-permute-start | bytes 110600 | tf_op jit(solution)/shard_map/ppermute | solution.py:24
  77.5 0.2 fusion.62
  77.7 1.0 mul.272
  78.7 3.0 %copy.51 = f32[512,1152]{1,0:T(8,128)} copy(f32[512,1152]{0,1:T(8,128)} %bitcast.1) | data formatting | bytes 4718592 | tf_op jit(solution)/shard_map/all_to_all | solution.py:115
  81.7 3.1 %copy.49 = f32[511,1152]{1,0:T(8,128)} copy(f32[511,1152]{0,1:T(8,128)} %bitcast.5) | data formatting | bytes 4709376 | tf_op jit(solution)/shard_map/slice | solution.py:38
  84.8 1.2 collective-permute-done.1
  86.2 2.4 %fusion.46 = f32[8,1152]{1,0:T(8,128)S(1)} fusion(bf16[1152,1152]{1,0:T(8,128)(2,1)} %param.11, f32[8,1152]{1,0:T(8,128)S(1)} %subtract_multiply_fusion), kind=kOutput, calls=%fused_computation.86 | convolution fusion | flops 21242880 | bytes 2727936 | tf_op jit(solution)/shard_map/dot_general | solution.py:44
  88.5 0.5 broadcast_multiply_fusion
  89.0 0.3 copy-done.4
  89.3 1.1 fusion.12
  90.4 3.3 %fusion.73 = f32[512,1152]{1,0:T(8,128)} fusion(bf16[1152,1152]{1,0:T(8,128)(2,1)S(1)} %copy-done, f32[512,1152]{1,0:T(8,128)S(1)} %fusion.12), kind=kOutput, calls=%fused_computation.137 | convolution fusion | flops 1359544320 | bytes 7372800 | tf_op jit(solution)/shard_map/dot_general | solution.py:43
  93.8 0.5 fusion.70
  94.4 0.2 fusion.16
  94.8 0.2 slice_reduce_fusion.1
  95.1 1.0 gather_fusion.1
  96.1 0.1 select_bitcast_fusion.1
  96.2 0.3 fusion.18
  96.6 5.7 %fusion.9 = f32[512,1152]{1,0:T(8,128)S(1)} fusion(f32[512,1152]{1,0:T(8,128)} %copy-done.1, f32[512,1152]{1,0:T(8,128)} %fusion.73, bf16[1152,1152]{1,0:T(8,128)(2,1)} %param.11, f32[512]{0:T(512)S(1)} %copy-done.20), kind=kOutput, calls=%fused_computation.13 | convolution fusion | flops 1363673088 | bytes 9734144 | tf_op jit(solution)/shard_map/dot_general | solution.py:44
  102.3 0.7 slice_add_fusion.1
  102.9 1.1 fusion.15
  104.0 1.8 %fusion.68 = f32[512,1152]{1,0:T(8,128)S(1)} fusion(bf16[1152,1152]{1,0:T(8,128)(2,1)S(1)} %copy-done, f32[512,1152]{1,0:T(8,128)S(1)} %fusion.15), kind=kOutput, calls=%fused_computation.132 | convolution fusion | flops 1359544320 | bytes 7372800 | tf_op jit(solution)/shard_map/dot_general | solution.py:43
  105.9 0.7 copy-done.5
  106.6 3.4 %fusion.6 = f32[512,1152]{1,0:T(8,128)} fusion(f32[512,1152]{1,0:T(8,128)S(1)} %fusion.15, f32[512,1152]{1,0:T(8,128)S(1)} %fusion.68, bf16[1152,1152]{1,0:T(8,128)(2,1)S(1)} %copy-done.5, f32[512]{0:T(512)S(1)} %copy-done.20), kind=kOutput, calls=%fused_computation.10 | convolution fusion | flops 1363673088 | bytes 9734144 | tf_op jit(solution)/shard_map/dot_general | solution.py:44
  110.0 3.1 %copy.53 = f32[512,1152]{0,1:T(8,128)} copy(f32[512,1152]{1,0:T(8,128)} %fusion.6) | data formatting | bytes 4718592 | tf_op jit(solution)/shard_map/add | solution.py:134
  113.1 6.7 %all-to-all-start.1 = ((f32[512,16,72]{0,2,1:T(8,128)}), f32[512,16,72]{0,2,1:T(8,128)}, u32[]{:S(2)}, u32[]{:S(2)}) async-start(f32[512,16,72]{0,2,1:T(8,128)} %bitcast.35), calls=%async_computation.1 | async-start | bytes 4718592 | tf_op jit(solution)/shard_map/all_to_all | solution.py:154
  119.8 0.4 collective-permute-start.2
  120.2 2.1 %fusion.65 = f32[512,128]{1,0:T(8,128)S(1)} fusion(bf16[1152,128]{1,0:T(8,128)(2,1)S(1)} %copy-done.6, f32[512,1152]{1,0:T(8,128)} %copy-done.2), kind=kOutput, calls=%fused_computation.129 | convolution fusion | flops 151584768 | bytes 2916352 | tf_op jit(solution)/shard_map/dot_general | solution.py:46
  122.4 0.2 convolution_divide_fusion
  122.6 1.7 collective-permute-start.3
  124.3 51.5 %collective-permute-done.2 = f32[33,128]{1,0:T(8,128)S(1)} collective-permute-done((f32[33,128]{1,0:T(8,128)S(1)}, f32[33,128]{1,0:T(8,128)S(1)}, u32[]{:S(2)}, u32[]{:S(2)}) %collective-permute-start.2) | collective-permute-done | bytes 16928 | tf_op jit(solution)/shard_map/ppermute | solution.py:18
  175.9 0.1 reshape.124
  176.0 0.1 fusion.76
  176.2 0.3 fusion.23
  176.5 0.1 mul.306
  176.6 0.6 fusion.44
  177.2 2.5 %all-to-all-done.1 = f32[512,16,72]{0,2,1:T(8,128)} async-done(((f32[512,16,72]{0,2,1:T(8,128)}), f32[512,16,72]{0,2,1:T(8,128)}, u32[]{:S(2)}, u32[]{:S(2)}) %all-to-all-start.1) | async-done | bytes 2359328 | tf_op jit(solution)/shard_map/all_to_all | solution.py:154
  179.7 3.4 %copy.57 = f32[16,9,8,512]{3,2,0,1:T(8,128)} copy(f32[16,9,8,512]{3,2,1,0:T(8,128)} %bitcast.15) | data formatting | bytes 4718592 | tf_op jit(solution)/shard_map/all_to_all | solution.py:154
  (64 shorter events, 0.8 us)
Async XLA Ops:
  0.6 87.9 %copy-start = (bf16[1152,1152]{1,0:T(8,128)(2,1)S(1)}, bf16[1152,1152]{1,0:T(8,128)(2,1)}, u32[]{:S(2)}) copy-start(bf16[1152,1152]{1,0:T(8,128)(2,1)} %param.10) | copy-start | bytes 7962628
  4.1 9.4 %copy-start.8 = (f32[64,128]{1,0:T(8,128)S(1)}, f32[64,128]{1,0:T(8,128)}, u32[]{:S(2)}) copy-start(f32[64,128]{1,0:T(8,128)} %param.9) | copy-start | bytes 98308
  4.1 17.2 %copy-start.7 = (s32[131072]{0:T(1024)S(1)}, s32[131072]{0:T(1024)}, u32[]{:S(2)}) copy-start(s32[131072]{0:T(1024)} %param.14) | copy-start | bytes 1572868
  4.1 69.2 %all-to-all-start = ((f32[16,512,72]{1,2,0:T(8,128)}), f32[16,512,72]{1,2,0:T(8,128)}, u32[]{:S(2)}, u32[]{:S(2)}) async-start(f32[16,512,72]{1,2,0:T(8,128)} %bitcast.34), calls=%async_computation | async-start | bytes 4718592 | tf_op jit(solution)/shard_map/all_to_all | solution.py:115
  14.1 52.2 %collective-permute-start = (f32[33,128]{1,0:T(8,128)S(1)}, f32[33,128]{1,0:T(8,128)S(1)}, u32[]{:S(2)}, u32[]{:S(2)}) collective-permute-start(f32[33,128]{1,0:T(8,128)S(1)} %get-tuple-element.26), channel_id=1, source_target_pairs={{1,0},{2,1},{3,2},{4,3},{5,4},{6,5},{7,6},{8,7},{9,8},{10,9},{11,1... | collective-permute-start | bytes 50696 | tf_op jit(solution)/shard_map/ppermute | solution.py:18
  66.3 0.6 copy-start.12
  75.4 10.6 %collective-permute-start.1 = (f32[8,1152]{1,0:T(8,128)}, f32[8,1152]{1,0:T(8,128)S(1)}, u32[]{:S(2)}, u32[]{:S(2)}) collective-permute-start(f32[8,1152]{1,0:T(8,128)} %copy.55), channel_id=1, source_target_pairs={{0,1},{1,2},{2,3},{3,4},{4,5},{5,6},{6,7},{7,8},{8,9},{9,10},{10,1... | collective-permute-start | bytes 110600 | tf_op jit(solution)/shard_map/ppermute | solution.py:24
  81.7 4.3 %copy-start.9 = (f32[1152]{0:T(1024)S(1)}, f32[1152]{0:T(1024)}, u32[]{:S(2)}) copy-start(f32[1152]{0:T(1024)} %get-tuple-element.34) | copy-start | bytes 13828
  81.7 4.3 %copy-start.11 = (f32[1152]{0:T(1024)S(1)}, f32[1152]{0:T(1024)}, u32[]{:S(2)}) copy-start(f32[1152]{0:T(1024)} %param.13) | copy-start | bytes 13828
  81.7 4.3 %copy-start.23 = (f32[8]{0:T(128)S(1)}, f32[8]{0:T(128)}, u32[]{:S(2)}) copy-start(f32[8]{0:T(128)} %get-tuple-element.28) | copy-start | bytes 100
  86.1 2.9 %copy-start.3 = (f32[512,1152]{1,0:T(8,128)S(1)}, f32[512,1152]{1,0:T(8,128)}, u32[]{:S(2)}) copy-start(f32[512,1152]{1,0:T(8,128)} %copy.51) | copy-start | bytes 7077892
  86.1 3.2 %copy-start.4 = (f32[511,1152]{1,0:T(8,128)S(1)}, f32[511,1152]{1,0:T(8,128)}, u32[]{:S(2)}) copy-start(f32[511,1152]{1,0:T(8,128)} %copy.49) | copy-start | bytes 7064068
  86.2 3.2 %copy-start.14 = (f32[512]{0:T(512)S(1)}, f32[512]{0:T(512)}, u32[]{:S(2)}) copy-start(f32[512]{0:T(512)} %get-tuple-element.30) | copy-start | bytes 6148
  86.2 3.2 %copy-start.16 = (f32[512]{0:T(512)S(1)}, f32[512]{0:T(512)}, u32[]{:S(2)}) copy-start(f32[512]{0:T(512)} %get-tuple-element.4) | copy-start | bytes 6148
  86.2 3.1 %copy-start.17 = (f32[512]{0:T(512)S(1)}, f32[512]{0:T(512)}, u32[]{:S(2)}) copy-start(f32[512]{0:T(512)} %get-tuple-element.5) | copy-start | bytes 6148
  90.4 3.3 %copy-start.1 = (f32[512,1152]{1,0:T(8,128)}, f32[512,1152]{1,0:T(8,128)S(1)}, u32[]{:S(2)}) copy-start(f32[512,1152]{1,0:T(8,128)S(1)} %fusion.12) | copy-start | bytes 7077892
  90.4 3.3 %copy-start.6 = (bf16[1152,128]{1,0:T(8,128)(2,1)S(1)}, bf16[1152,128]{1,0:T(8,128)(2,1)}, u32[]{:S(2)}) copy-start(bf16[1152,128]{1,0:T(8,128)(2,1)} %param.12) | copy-start | bytes 884740
  93.7 0.7 copy-start.18
  93.7 0.9 copy-start.10
  93.7 0.9 copy-start.13
  93.7 0.9 copy-start.21
  93.8 0.9 copy-start.22
  93.8 1.3 copy-start.15
  93.8 2.3 %copy-start.19 = (pred[512]{0:T(512)(128)(4,1)S(1)}, pred[512]{0:T(512)(128)(4,1)}, u32[]{:S(2)}) copy-start(pred[512]{0:T(512)(128)(4,1)} %get-tuple-element.12) | copy-start | bytes 1540
  93.8 2.8 %copy-start.20 = (f32[512]{0:T(512)S(1)}, f32[512]{0:T(512)}, u32[]{:S(2)}) copy-start(f32[512]{0:T(512)} %get-tuple-element.29) | copy-start | bytes 6148
  104.0 1.9 %copy-start.2 = (f32[512,1152]{1,0:T(8,128)}, f32[512,1152]{1,0:T(8,128)S(1)}, u32[]{:S(2)}) copy-start(f32[512,1152]{1,0:T(8,128)S(1)} %fusion.15) | copy-start | bytes 7077892
  104.0 2.6 %copy-start.5 = (bf16[1152,1152]{1,0:T(8,128)(2,1)S(1)}, bf16[1152,1152]{1,0:T(8,128)(2,1)}, u32[]{:S(2)}) copy-start(bf16[1152,1152]{1,0:T(8,128)(2,1)} %param.11) | copy-start | bytes 7962628
  113.1 66.7 %all-to-all-start.1 = ((f32[512,16,72]{0,2,1:T(8,128)}), f32[512,16,72]{0,2,1:T(8,128)}, u32[]{:S(2)}, u32[]{:S(2)}) async-start(f32[512,16,72]{0,2,1:T(8,128)} %bitcast.35), calls=%async_computation.1 | async-start | bytes 4718592 | tf_op jit(solution)/shard_map/all_to_all | solution.py:154
  119.8 56.0 %collective-permute-start.2 = (f32[33,128]{1,0:T(8,128)S(1)}, f32[33,128]{1,0:T(8,128)S(1)}, u32[]{:S(2)}, u32[]{:S(2)}) collective-permute-start(f32[33,128]{1,0:T(8,128)S(1)} %get-tuple-element.23), channel_id=1, source_target_pairs={{255,0},{0,1},{1,2},{2,3},{3,4},{4,5},{5,6},{6,7},{7,8},{8,9},{9,1... | collective-permute-start | bytes 50696 | tf_op jit(solution)/shard_map/ppermute | solution.py:18
  122.6 53.9 %collective-permute-start.3 = (f32[32,128]{1,0:T(8,128)S(1)}, f32[32,128]{1,0:T(8,128)S(1)}, u32[]{:S(2)}, u32[]{:S(2)}) collective-permute-start(f32[32,128]{1,0:T(8,128)S(1)} %get-tuple-element.21), channel_id=1, source_target_pairs={{255,0},{0,1},{1,2},{2,3},{3,4},{4,5},{5,6},{6,7},{7,8},{8,9},{9,1... | collective-permute-start | bytes 49160 | tf_op jit(solution)/shard_map/ppermute | solution.py:18

commit v10 on v7

--- a/solution.py
+++ b/solution.py
@@ -3,6 +3,7 @@
 import jax
 import jax.numpy as jnp
 from jax import lax
+from jax.experimental.layout import Layout, with_layout_constraint
 from jax.sharding import PartitionSpec as P
 
 NDIR = 36
@@ -146,6 +147,7 @@
                 outside = ((device == 0) & (row == 0)) | (joint & (row == padded.shape[0] - 1))
                 padded = jnp.where(outside, 0.0, padded)
             velocity_out = ocean_rows(padded, jnp.concatenate([low_forcing, forcing[:half]], 0))
+    field = with_layout_constraint(field, Layout(major_to_minor=(1, 0)))
     spectrum_out = lax.all_to_all(field, "bin", split_axis=1, concat_axis=0, tiled=True)
     return (spectrum_out, velocity_out)
 

time: 180 us -> 182 us (1.011)
  local copies, waits for them, and re-layouts: 22.8 us -> 18.2 us
  other arithmetic: 12.9 us -> 17.1 us
    add x1 -> x0, local copies, waits for them, and re-layouts: 3.17 us -> none  [per_device(): field = moved + increment.astype(jnp.float32)]
    all_to_all x2 -> x1, local copies, waits for them, and re-layouts: 6.48 us -> 3.44 us  [per_device(): lax.all_to_all(spectrum, 'bin', split_axis=0, concat_axis=1, tiled=True)]
    convert_element_type x1, other arithmetic: 2.45 us -> 4.7 us  [per_device(): moved.astype(jnp.bfloat16)]
    ppermute x1, waiting for transfers between devices: 4.16 us -> 6.01 us  [from_behind(): return lax.ppermute(shard, axis, pairs)]
  transfers between devices with their start and end apart: 6 -> 6, of which waited for: 5 -> 4; matrix products, arithmetic and copies ran while one was open for 10% -> 9% of each run, Pallas kernels for 0% -> 0%
where the time goes in v10:
time: 182 us; the launch traced here: 180 us
  waiting for transfers between devices  102 us (56%)
  starting transfers between devices  25.7 us (14%)
  local copies, waits for them, and re-layouts  18.2 us (10%)
  other arithmetic  17.1 us (9%)
  matrix products  15.3 us (8%)
    ppermute x3, waiting for transfers between devices, shifted(): return lax.ppermute(block, axis, route)  92.3 us
    all_to_all x1, starting transfers between devices, per_device(): lax.all_to_all(spectrum, 'bin', split_axis=0, concat_axis=1, tiled=True)  9.41 us
    ppermute x3, starting transfers between devices, shifted(): return lax.ppermute(block, axis, route)  9.31 us
    ppermute x1, waiting for transfers between devices, from_behind(): return lax.ppermute(shard, axis, pairs)  6.01 us
    dot_general x2, matrix products, sources(): other = jnp.dot(rounded, source_b, preferred_element_type=jnp.float32)  5.98 us
    dot_general x2, matrix products, sources(): gain = jnp.dot(rounded, source_a, preferred_element_type=jnp.float32)  5.68 us
    all_to_all x1, starting transfers between devices, per_device(): lax.all_to_all(field, 'bin', split_axis=1, concat_axis=0, tiled=True)  4.91 us
    convert_element_type x1, other arithmetic, per_device(): moved.astype(jnp.bfloat16)  4.7 us
  transfers between devices with their start and end apart: 6, of which 4 were waited for; matrix products, arithmetic and copies ran while one was open for 9% of the time, Pallas kernels for 0%

profile of v10, /device:TPU:88, one launch (start us, length us, event | category | flops | bytes accessed | tf_op | source)
XLA Modules:
  0.0 179.7 jit_solution(10104825375127601861)
XLA Ops:
  0.6 0.0 copy-start
  0.6 3.4 %copy.61 = f32[9,16,8,512]{3,2,0,1:T(8,128)} copy(f32[9,16,8,512]{3,2,1,0:T(8,128)} %bitcast.31) | data formatting | bytes 4718592 | tf_op jit(solution)/shard_map/all_to_all | solution.py:116
  4.1 9.4 %all-to-all-start = ((f32[16,512,72]{1,2,0:T(8,128)}), f32[16,512,72]{1,2,0:T(8,128)}, u32[]{:S(2)}, u32[]{:S(2)}) async-start(f32[16,512,72]{1,2,0:T(8,128)} %bitcast.30), calls=%async_computation | async-start | bytes 4718592 | tf_op jit(solution)/shard_map/all_to_all | solution.py:116
  13.5 0.6 fusion.70
  14.1 7.2 %collective-permute-start.1 = (f32[33,128]{1,0:T(8,128)S(1)}, f32[33,128]{1,0:T(8,128)S(1)}, u32[]{:S(2)}, u32[]{:S(2)}) collective-permute-start(f32[33,128]{1,0:T(8,128)S(1)} %get-tuple-element.28), channel_id=1, source_target_pairs={{1,0},{2,1},{3,2},{4,3},{5,4},{6,5},{7,6},{8,7},{9,8},{10,9},{11,1... | collective-permute-start | bytes 50696 | tf_op jit(solution)/shard_map/ppermute | solution.py:19
  21.3 0.1 slice.132
  21.4 0.8 slice.128
  22.1 0.1 compare_and_fusion
  22.2 0.6 compare_and_fusion.3
  22.9 0.6 pad_clamp_fusion
  23.4 1.4 broadcast_multiply_fusion
  24.8 0.7 fusion.50
  25.5 0.7 convert_reduce_fusion
  26.2 0.7 broadcast_multiply_fusion.1
  26.9 0.6 compare_and_fusion.1
  27.5 38.9 %collective-permute-done.1 = f32[33,128]{1,0:T(8,128)S(1)} collective-permute-done((f32[33,128]{1,0:T(8,128)S(1)}, f32[33,128]{1,0:T(8,128)S(1)}, u32[]{:S(2)}, u32[]{:S(2)}) %collective-permute-start.1) | collective-permute-done | bytes 16928 | tf_op jit(solution)/shard_map/ppermute | solution.py:19
  66.3 0.2 maximum_reduce_fusion
  66.6 0.1 copy.46
  66.7 0.1 reshape.110
  66.8 1.6 gather_fusion
  68.4 0.1 fusion.67
  68.5 0.9 fusion.26
  69.4 0.1 select_bitcast_fusion
  69.6 3.8 %all-to-all-done = f32[16,512,72]{1,2,0:T(8,128)} async-done(((f32[16,512,72]{1,2,0:T(8,128)}), f32[16,512,72]{1,2,0:T(8,128)}, u32[]{:S(2)}, u32[]{:S(2)}) %all-to-all-start) | async-done | bytes 2359328 | tf_op jit(solution)/shard_map/all_to_all | solution.py:116
  73.3 1.3 slice.171
  74.6 0.8 copy.57
  75.4 2.1 %collective-permute-start = (f32[8,1152]{1,0:T(8,128)}, f32[8,1152]{1,0:T(8,128)S(1)}, u32[]{:S(2)}, u32[]{:S(2)}) collective-permute-start(f32[8,1152]{1,0:T(8,128)} %copy.57), channel_id=1, source_target_pairs={{0,1},{1,2},{2,3},{3,4},{4,5},{5,6},{6,7},{7,8},{8,9},{9,10},{10,1... | collective-permute-start | bytes 110600 | tf_op jit(solution)/shard_map/ppermute | solution.py:25
  77.5 0.9 fusion.18
  78.5 1.6 mul.233
  80.0 6.0 %collective-permute-done = f32[8,1152]{1,0:T(8,128)S(1)} collective-permute-done((f32[8,1152]{1,0:T(8,128)}, f32[8,1152]{1,0:T(8,128)S(1)}, u32[]{:S(2)}, u32[]{:S(2)}) %collective-permute-start) | collective-permute-done | bytes 36896 | tf_op jit(solution)/shard_map/ppermute | solution.py:25
  86.0 0.2 copy.45
  86.3 0.0 copy-start.21
  86.3 2.5 %fusion.10 = f32[519,1152]{0,1:T(8,128)S(1)} fusion(f32[512,1152]{0,1:T(8,128)} %bitcast.2, f32[8,1152]{0,1:T(8,128)S(1)} %copy.45), kind=kLoop, calls=%fused_computation.17 | loop fusion | flops 597888 | bytes 4787712 | tf_op jit(solution)/shard_map/concatenate | solution.py:118
  88.9 0.0 copy-start.6
  89.0 4.7 %fusion.64 = (bf16[520,1152]{0,1:T(8,128)(2,1)S(1)}, f32[520,1152]{0,1:T(8,128)}) fusion(f32[519,1152]{0,1:T(8,128)S(1)} %fusion.10, f32[1152]{0:T(1024)S(1)} %copy-done.12, f32[520]{0:T(1024)S(1)} %copy-done.26, f32[1152]{0:T(1024)S(1)} %copy-done.14, f32[520]{0:T(1024)S(1)} %copy-done.25, f32[1152]{0:T(1024)S(1)} %copy-done.21, f32[512,1152]{0,1:T(8,128)} %bitcast.2, ...), kind=kLoop, calls=%fused_computation.123 | loop fusion | flops 6589440 | bytes 8402016 | tf_op jit(solution)/shard_map/convert_element_type | solution.py:124
  93.7 1.1 copy-done.3
  94.8 1.0 fusion.14
  95.8 0.2 fusion.16
  96.1 0.1 fusion.38
  96.2 0.2 slice_reduce_fusion.1
  96.4 0.1 copy.50
  96.5 1.0 gather_fusion.1
  97.5 0.1 select_bitcast_fusion.1
  97.7 0.3 fusion.20
  98.0 0.0 copy-start.4
  98.0 0.0 copy-start.36
  98.0 3.9 %fusion.71 = f32[520,1152]{0,1:T(8,128)S(1)} fusion(bf16[520,1152]{0,1:T(8,128)(2,1)} %copy-done.3, bf16[1152,1152]{1,0:T(8,128)(2,1)S(1)} %copy-done), kind=kOutput, calls=%fused_computation.129 | convolution fusion | flops 1380188160 | bytes 6248448 | tf_op jit(solution)/shard_map/dot_general | solution.py:44
  102.1 2.7 %fusion.6 = f32[520,1152]{0,1:T(8,128)S(1)} fusion(f32[520,1152]{0,1:T(8,128)S(1)} %copy-done.2, f32[520,1152]{0,1:T(8,128)S(1)} %fusion.71, bf16[520,1152]{0,1:T(8,128)(2,1)S(1)} %copy-done.4, bf16[1152,1152]{1,0:T(8,128)(2,1)S(1)} %copy-done.36, f32[520]{0:T(1024)S(1)} %copy-done.31), kind=kOutput, calls=%fused_computation.12 | convolution fusion | flops 1384381440 | bytes 11042848 | tf_op jit(solution)/shard_map/dot_general | solution.py:45
  104.8 2.1 %fusion.13 = f32[512,1152]{0,1:T(8,128)S(1)} fusion(f32[520,1152]{0,1:T(8,128)S(1)} %fusion.6, f32[1152]{0:T(1024)S(1)} %copy-done.13, f32[512]{0:T(512)S(1)} %get-tuple-element.5, f32[1152]{0:T(1024)S(1)} %copy-done.15, f32[512]{0:T(512)S(1)} %get-tuple-element.4, f32[1152]{0:T(1024)S(1)} %copy-done.22, f32[512]{0:T(512)S(1)} %copy-done.28), kind=kLoop, calls=%fused_computation.23 | loop fusion | flops 5308416 | bytes 7097856 | tf_op jit(solution)/shard_map/mul | solution.py:40
  106.9 1.7 fusion.61
  108.7 3.3 %fusion.9 = f32[512,1152]{0,1:T(8,128)} fusion(f32[512,1152]{0,1:T(8,128)S(1)} %fusion.13, f32[512,1152]{0,1:T(8,128)S(1)} %fusion.61, bf16[1152,1152]{1,0:T(8,128)(2,1)S(1)} %copy-done.36, f32[512]{0:T(512)S(1)} %copy-done.33), kind=kOutput, calls=%fused_computation.16 | convolution fusion | flops 1363673088 | bytes 9734144 | tf_op jit(solution)/shard_map/dot_general | solution.py:45
  112.0 4.9 %all-to-all-start.1 = ((f32[512,16,72]{0,2,1:T(8,128)}), f32[512,16,72]{0,2,1:T(8,128)}, u32[]{:S(2)}, u32[]{:S(2)}) async-start(f32[512,16,72]{0,2,1:T(8,128)} %bitcast.32), calls=%async_computation.1 | async-start | bytes 4718592 | tf_op jit(solution)/shard_map/all_to_all | solution.py:151
  117.0 0.4 collective-permute-start.2
  117.4 2.2 %fusion.58 = f32[512,128]{1,0:T(8,128)S(1)} fusion(bf16[1152,128]{1,0:T(8,128)(2,1)S(1)} %copy-done.6, f32[512,1152]{0,1:T(8,128)} %copy-done.1), kind=kOutput, calls=%fused_computation.118 | convolution fusion | flops 151584768 | bytes 2916352 | tf_op jit(solution)/shard_map/dot_general | solution.py:47
  119.6 0.2 convolution_divide_fusion
  119.9 1.7 collective-permute-start.3
  121.6 53.5 %collective-permute-done.2 = f32[33,128]{1,0:T(8,128)S(1)} collective-permute-done((f32[33,128]{1,0:T(8,128)S(1)}, f32[33,128]{1,0:T(8,128)S(1)}, u32[]{:S(2)}, u32[]{:S(2)}) %collective-permute-start.2) | collective-permute-done | bytes 16928 | tf_op jit(solution)/shard_map/ppermute | solution.py:19
  175.0 0.1 maximum_select_fusion
  175.1 0.1 reshape.111
  175.2 0.1 fusion.66
  175.4 0.3 fusion.23
  175.6 0.1 mul.257
  175.8 0.6 fusion.44
  176.4 3.4 %copy.59 = f32[16,9,8,512]{3,2,0,1:T(8,128)} copy(f32[16,9,8,512]{3,2,1,0:T(8,128)} %bitcast.14) | data formatting | bytes 4718592 | tf_op jit(solution)/shard_map/all_to_all | solution.py:151
  (81 shorter events, 0.2 us)
Async XLA Ops:
  0.6 97.3 %copy-start = (bf16[1152,1152]{1,0:T(8,128)(2,1)S(1)}, bf16[1152,1152]{1,0:T(8,128)(2,1)}, u32[]{:S(2)}) copy-start(bf16[1152,1152]{1,0:T(8,128)(2,1)} %param.10) | copy-start | bytes 7962628
  4.1 9.4 %copy-start.7 = (f32[64,128]{1,0:T(8,128)S(1)}, f32[64,128]{1,0:T(8,128)}, u32[]{:S(2)}) copy-start(f32[64,128]{1,0:T(8,128)} %param.9) | copy-start | bytes 98308
  4.1 17.2 %copy-start.5 = (s32[131072]{0:T(1024)S(1)}, s32[131072]{0:T(1024)}, u32[]{:S(2)}) copy-start(s32[131072]{0:T(1024)} %param.14) | copy-start | bytes 1572868
  4.1 69.2 %all-to-all-start = ((f32[16,512,72]{1,2,0:T(8,128)}), f32[16,512,72]{1,2,0:T(8,128)}, u32[]{:S(2)}, u32[]{:S(2)}) async-start(f32[16,512,72]{1,2,0:T(8,128)} %bitcast.30), calls=%async_computation | async-start | bytes 4718592 | tf_op jit(solution)/shard_map/all_to_all | solution.py:116
  14.1 52.2 %collective-permute-start.1 = (f32[33,128]{1,0:T(8,128)S(1)}, f32[33,128]{1,0:T(8,128)S(1)}, u32[]{:S(2)}, u32[]{:S(2)}) collective-permute-start(f32[33,128]{1,0:T(8,128)S(1)} %get-tuple-element.28), channel_id=1, source_target_pairs={{1,0},{2,1},{3,2},{4,3},{5,4},{6,5},{7,6},{8,7},{9,8},{10,9},{11,1... | collective-permute-start | bytes 50696 | tf_op jit(solution)/shard_map/ppermute | solution.py:19
  22.8 43.7 %copy-start.18 = (s32[512]{0:T(512)}, s32[512]{0:T(512)S(1)}, u32[]{:S(2)}) copy-start(s32[512]{0:T(512)S(1)} %get-tuple-element.11) | copy-start | bytes 6148
  24.8 41.7 %copy-start.23 = (f32[520]{0:T(1024)}, f32[520]{0:T(1024)S(1)}, u32[]{:S(2)}) copy-start(f32[520]{0:T(1024)S(1)} %get-tuple-element.13) | copy-start | bytes 6244
  27.5 39.2 %copy-start.8 = (f32[32,128]{1,0:T(8,128)}, f32[32,128]{1,0:T(8,128)S(1)}, u32[]{:S(2)}) copy-start(f32[32,128]{1,0:T(8,128)S(1)} %slice.142) | copy-start | bytes 49156
  66.3 7.0 %copy-start.16 = (f32[33,128]{1,0:T(8,128)}, f32[33,128]{1,0:T(8,128)S(1)}, u32[]{:S(2)}) copy-start(f32[33,128]{1,0:T(8,128)S(1)} %collective-permute-done.1) | copy-start | bytes 50692
  75.4 10.6 %collective-permute-start = (f32[8,1152]{1,0:T(8,128)}, f32[8,1152]{1,0:T(8,128)S(1)}, u32[]{:S(2)}, u32[]{:S(2)}) collective-permute-start(f32[8,1152]{1,0:T(8,128)} %copy.57), channel_id=1, source_target_pairs={{0,1},{1,2},{2,3},{3,4},{4,5},{5,6},{6,7},{7,8},{8,9},{9,10},{10,1... | collective-permute-start | bytes 110600 | tf_op jit(solution)/shard_map/ppermute | solution.py:25
  86.3 2.6 %copy-start.12 = (f32[1152]{0:T(1024)S(1)}, f32[1152]{0:T(1024)}, u32[]{:S(2)}) copy-start(f32[1152]{0:T(1024)} %get-tuple-element.31) | copy-start | bytes 13828
  86.3 2.6 %copy-start.14 = (f32[1152]{0:T(1024)S(1)}, f32[1152]{0:T(1024)}, u32[]{:S(2)}) copy-start(f32[1152]{0:T(1024)} %get-tuple-element.32) | copy-start | bytes 13828
  86.3 2.6 %copy-start.21 = (f32[1152]{0:T(1024)S(1)}, f32[1152]{0:T(1024)}, u32[]{:S(2)}) copy-start(f32[1152]{0:T(1024)} %param.13) | copy-start | bytes 13828
  86.3 2.6 %copy-start.24 = (f32[520]{0:T(1024)S(1)}, f32[520]{0:T(1024)}, u32[]{:S(2)}) copy-start(f32[520]{0:T(1024)} %copy-done.23) | copy-start | bytes 6244
  86.3 2.6 %copy-start.25 = (f32[520]{0:T(1024)S(1)}, f32[520]{0:T(1024)}, u32[]{:S(2)}) copy-start(f32[520]{0:T(1024)} %get-tuple-element.2) | copy-start | bytes 6244
  86.3 2.6 %copy-start.26 = (f32[520]{0:T(1024)S(1)}, f32[520]{0:T(1024)}, u32[]{:S(2)}) copy-start(f32[520]{0:T(1024)} %get-tuple-element.3) | copy-start | bytes 6244
  88.9 5.9 %copy-start.6 = (bf16[1152,128]{1,0:T(8,128)(2,1)S(1)}, bf16[1152,128]{1,0:T(8,128)(2,1)}, u32[]{:S(2)}) copy-start(bf16[1152,128]{1,0:T(8,128)(2,1)} %param.12) | copy-start | bytes 884740
  88.9 6.9 %copy-start.19 = (s32[512]{0:T(512)S(1)}, s32[512]{0:T(512)}, u32[]{:S(2)}) copy-start(s32[512]{0:T(512)} %copy-done.18) | copy-start | bytes 6148
  88.9 6.9 %copy-start.29 = (f32[64]{0:T(128)S(1)}, f32[64]{0:T(128)}, u32[]{:S(2)}) copy-start(f32[64]{0:T(128)} %convert_reduce_fusion) | copy-start | bytes 772
  88.9 7.1 %copy-start.9 = (f32[32,128]{1,0:T(8,128)S(1)}, f32[32,128]{1,0:T(8,128)}, u32[]{:S(2)}) copy-start(f32[32,128]{1,0:T(8,128)} %copy-done.8) | copy-start | bytes 49156
  88.9 7.1 %copy-start.11 = (f32[33,128]{1,0:T(8,128)S(1)}, f32[33,128]{1,0:T(8,128)}, u32[]{:S(2)}) copy-start(f32[33,128]{1,0:T(8,128)} %get-tuple-element.27) | copy-start | bytes 50692
  88.9 7.1 %copy-start.17 = (f32[33,128]{1,0:T(8,128)S(1)}, f32[33,128]{1,0:T(8,128)}, u32[]{:S(2)}) copy-start(f32[33,128]{1,0:T(8,128)} %copy-done.16) | copy-start | bytes 50692
  88.9 7.1 %copy-start.34 = (pred[64]{0:T(512)(128)(4,1)S(1)}, pred[64]{0:T(512)(128)(4,1)}, u32[]{:S(2)}) copy-start(pred[64]{0:T(512)(128)(4,1)} %get-tuple-element.33) | copy-start | bytes 196
  89.0 7.1 %copy-start.35 = (pred[64]{0:T(512)(128)(4,1)S(1)}, pred[64]{0:T(512)(128)(4,1)}, u32[]{:S(2)}) copy-start(pred[64]{0:T(512)(128)(4,1)} %get-tuple-element.34) | copy-start | bytes 196
  93.7 1.1 copy-start.3
  93.7 2.4 %copy-start.10 = (f32[64,128]{1,0:T(8,128)S(1)}, f32[64,128]{1,0:T(8,128)}, u32[]{:S(2)}) copy-start(f32[64,128]{1,0:T(8,128)} %mul.233) | copy-start | bytes 98308
  93.7 2.8 %copy-start.27 = (s32[1024]{0:T(1024)S(1)}, s32[1024]{0:T(1024)}, u32[]{:S(2)}) copy-start(s32[1024]{0:T(1024)} %pad_clamp_fusion) | copy-start | bytes 12292
  93.7 3.8 %copy-start.32 = (pred[512]{0:T(512)(128)(4,1)S(1)}, pred[512]{0:T(512)(128)(4,1)}, u32[]{:S(2)}) copy-start(pred[512]{0:T(512)(128)(4,1)} %get-tuple-element.10) | copy-start | bytes 1540
  98.0 4.0 %copy-start.2 = (f32[520,1152]{0,1:T(8,128)S(1)}, f32[520,1152]{0,1:T(8,128)}, u32[]{:S(2)}) copy-start(f32[520,1152]{0,1:T(8,128)} %get-tuple-element.15) | copy-start | bytes 7188484
  98.0 4.0 %copy-start.4 = (bf16[520,1152]{0,1:T(8,128)(2,1)S(1)}, bf16[520,1152]{0,1:T(8,128)(2,1)}, u32[]{:S(2)}) copy-start(bf16[520,1152]{0,1:T(8,128)(2,1)} %copy-done.3) | copy-start | bytes 3594244
  98.0 4.0 %copy-start.31 = (f32[520]{0:T(1024)S(1)}, f32[520]{0:T(1024)}, u32[]{:S(2)}) copy-start(f32[520]{0:T(1024)} %get-tuple-element.12) | copy-start | bytes 6244
  98.0 4.0 %copy-start.36 = (bf16[1152,1152]{1,0:T(8,128)(2,1)S(1)}, bf16[1152,1152]{1,0:T(8,128)(2,1)}, u32[]{:S(2)}) copy-start(bf16[1152,1152]{1,0:T(8,128)(2,1)} %param.11) | copy-start | bytes 7962628
  102.0 2.7 %copy-start.13 = (f32[1152]{0:T(1024)S(1)}, f32[1152]{0:T(1024)}, u32[]{:S(2)}) copy-start(f32[1152]{0:T(1024)} %get-tuple-element.31) | copy-start | bytes 13828
  102.0 2.7 %copy-start.15 = (f32[1152]{0:T(1024)S(1)}, f32[1152]{0:T(1024)}, u32[]{:S(2)}) copy-start(f32[1152]{0:T(1024)} %get-tuple-element.32) | copy-start | bytes 13828
  102.0 2.7 %copy-start.22 = (f32[1152]{0:T(1024)S(1)}, f32[1152]{0:T(1024)}, u32[]{:S(2)}) copy-start(f32[1152]{0:T(1024)} %param.13) | copy-start | bytes 13828
  102.1 2.7 %copy-start.28 = (f32[512]{0:T(512)S(1)}, f32[512]{0:T(512)}, u32[]{:S(2)}) copy-start(f32[512]{0:T(512)} %get-tuple-element.30) | copy-start | bytes 6148
  106.9 1.8 copy-start.1
  106.9 1.8 copy-start.33
  112.0 64.4 %all-to-all-start.1 = ((f32[512,16,72]{0,2,1:T(8,128)}), f32[512,16,72]{0,2,1:T(8,128)}, u32[]{:S(2)}, u32[]{:S(2)}) async-start(f32[512,16,72]{0,2,1:T(8,128)} %bitcast.32), calls=%async_computation.1 | async-start | bytes 4718592 | tf_op jit(solution)/shard_map/all_to_all | solution.py:151
  116.9 2.7 %copy-start.20 = (s32[512]{0:T(512)S(1)}, s32[512]{0:T(512)}, u32[]{:S(2)}) copy-start(s32[512]{0:T(512)} %copy-done.18) | copy-start | bytes 6148
  116.9 2.7 %copy-start.30 = (f32[64]{0:T(128)S(1)}, f32[64]{0:T(128)}, u32[]{:S(2)}) copy-start(f32[64]{0:T(128)} %convert_reduce_fusion) | copy-start | bytes 772
  117.0 58.0 %collective-permute-start.2 = (f32[33,128]{1,0:T(8,128)S(1)}, f32[33,128]{1,0:T(8,128)S(1)}, u32[]{:S(2)}, u32[]{:S(2)}) collective-permute-start(f32[33,128]{1,0:T(8,128)S(1)} %get-tuple-element.25), channel_id=1, source_target_pairs={{255,0},{0,1},{1,2},{2,3},{3,4},{4,5},{5,6},{6,7},{7,8},{8,9},{9,1... | collective-permute-start | bytes 50696 | tf_op jit(solution)/shard_map/ppermute | solution.py:19
  119.9 55.9 %collective-permute-start.3 = (f32[32,128]{1,0:T(8,128)S(1)}, f32[32,128]{1,0:T(8,128)S(1)}, u32[]{:S(2)}, u32[]{:S(2)}) collective-permute-start(f32[32,128]{1,0:T(8,128)S(1)} %get-tuple-element.23), channel_id=1, source_target_pairs={{255,0},{0,1},{1,2},{2,3},{3,4},{4,5},{5,6},{6,7},{7,8},{8,9},{9,1... | collective-permute-start | bytes 49160 | tf_op jit(solution)/shard_map/ppermute | solution.py:19

commit v11 on v9

--- a/solution.py
+++ b/solution.py
@@ -112,27 +112,15 @@
     table = jnp.stack([own[:, 0], own[:, LEVELS]])
     current = jnp.take(table, ext_where, axis=1)
 
-    body = lax.all_to_all(spectrum, "bin", split_axis=0, concat_axis=1, tiled=True)
-    head = from_behind(body[-EXTRA:], ALL, 1)
-    head_current = current[:, :EXTRA]
+    field = lax.all_to_all(spectrum, "bin", split_axis=0, concat_axis=1, tiled=True)
     current = current[:, EXTRA:]
-    head_mask = ext_mask[:EXTRA]
-    head_moved = propagate(
-        head, jnp.zeros((1, bins), jnp.float32), head_current, group_speed, cos_b, sin_b, head_mask
-    )
-    head_increment, _ = sources(
-        head_moved.astype(jnp.bfloat16), head_mask, source_a, source_b, stokes_kernel
-    )
-    later_prev = (head_moved + head_increment.astype(jnp.float32))[-1:]
-    field = body
-    prev = head[-1:]
     for step in range(STEPS):
+        prev = from_behind(field[-1:], ALL, 1)
         moved = propagate(field, prev, current, group_speed, cos_b, sin_b, local_mask)
         increment, stokes = sources(
             moved.astype(jnp.bfloat16), local_mask, source_a, source_b, stokes_kernel
         )
         field = moved + increment.astype(jnp.float32)
-        prev = later_prev
         sums = jnp.dot(onehot, stokes, precision=lax.Precision.HIGHEST)
         forcing = sums / counts[:, None]
         if step + 1 < STEPS:

time: 186 us -> 186 us (level)
  waiting for transfers between devices: 96.2 us -> 109 us
  matrix products: 20.1 us -> 12.1 us
  local copies, waits for them, and re-layouts: 27.6 us -> 24.9 us
    ppermute x3, waiting for transfers between devices: 89.8 us -> 97.4 us  [shifted(): return lax.ppermute(block, axis, route)]
    dot_general x3 -> x2, matrix products: 11.4 us -> 5.3 us  [sources(): other = jnp.dot(rounded, source_b, preferred_element_type=jnp.float32)]
    ppermute x1 -> x2, waiting for transfers between devices: 1.23 us -> 6.92 us  [from_behind(): return lax.ppermute(shard, axis, pairs)]
    mul x3 -> x2, other arithmetic: 2.24 us -> 6.67 us  [propagate(): return mask_cells[:, None] * (field - speed * (field - behind))]
    all_to_all x1, waiting for transfers between devices: 2.52 us -> 0.01 us  [per_device(): lax.all_to_all(field, 'bin', split_axis=1, concat_axis=0, tiled=True)]
    ppermute x1 -> x2, starting transfers between devices: 2.09 us -> 4.01 us  [from_behind(): return lax.ppermute(shard, axis, pairs)]
    dot_general x3 -> x2, matrix products: 5.61 us -> 3.7 us  [sources(): gain = jnp.dot(rounded, source_a, preferred_element_type=jnp.float32)]
  transfers between devices with their start and end apart: 6 -> 7, of which waited for: 5 -> 5; matrix products, arithmetic and copies ran while one was open for 12% -> 9% of each run, Pallas kernels for 0% -> 0%
where the time goes in v11:
time: 186 us; the launch traced here: 184 us
  waiting for transfers between devices  109 us (59%)
  starting transfers between devices  28 us (15%)
  local copies, waits for them, and re-layouts  24.9 us (13%)
  matrix products  12.1 us (7%)
  other arithmetic  9.75 us (5%)
    ppermute x3, waiting for transfers between devices, shifted(): return lax.ppermute(block, axis, route)  97.4 us
    all_to_all x1, starting transfers between devices, per_device(): lax.all_to_all(spectrum, 'bin', split_axis=0, concat_axis=1, tiled=True)  9.41 us
    ppermute x3, starting transfers between devices, shifted(): return lax.ppermute(block, axis, route)  9.39 us
    ppermute x2, waiting for transfers between devices, from_behind(): return lax.ppermute(shard, axis, pairs)  6.92 us
    mul x2, other arithmetic, propagate(): return mask_cells[:, None] * (field - speed * (field - behind))  6.67 us
    all_to_all x2, local copies, waits for them, and re-layouts, per_device(): lax.all_to_all(spectrum, 'bin', split_axis=0, concat_axis=1, tiled=True)  6.49 us
    dot_general x2, matrix products, sources(): other = jnp.dot(rounded, source_b, preferred_element_type=jnp.float32)  5.3 us
    all_to_all x1, starting transfers between devices, per_device(): lax.all_to_all(field, 'bin', split_axis=1, concat_axis=0, tiled=True)  5.18 us
  transfers between devices with their start and end apart: 7, of which 5 were waited for; matrix products, arithmetic and copies ran while one was open for 9% of the time, Pallas kernels for 0%

profile of v11, /device:TPU:88, one launch (start us, length us, event | category | flops | bytes accessed | tf_op | source)
XLA Modules:
  0.0 184.4 jit_solution(6127564838876779054)
XLA Ops:
  0.6 0.0 copy-start
  0.6 3.4 %copy.55 = f32[9,16,8,512]{3,2,0,1:T(8,128)} copy(f32[9,16,8,512]{3,2,1,0:T(8,128)} %bitcast.33) | data formatting | bytes 4718592 | tf_op jit(solution)/shard_map/all_to_all | solution.py:115
  4.1 9.4 %all-to-all-start = ((f32[16,512,72]{1,2,0:T(8,128)}), f32[16,512,72]{1,2,0:T(8,128)}, u32[]{:S(2)}, u32[]{:S(2)}) async-start(f32[16,512,72]{1,2,0:T(8,128)} %bitcast.31), calls=%async_computation | async-start | bytes 4718592 | tf_op jit(solution)/shard_map/all_to_all | solution.py:115
  13.5 7.2 %collective-permute-start = (f32[33,128]{1,0:T(8,128)S(1)}, f32[33,128]{1,0:T(8,128)S(1)}, u32[]{:S(2)}, u32[]{:S(2)}) collective-permute-start(f32[33,128]{1,0:T(8,128)S(1)} %get-tuple-element.24), channel_id=1, source_target_pairs={{1,0},{2,1},{3,2},{4,3},{5,4},{6,5},{7,6},{8,7},{9,8},{10,9},{11,1... | collective-permute-start | bytes 50696 | tf_op jit(solution)/shard_map/ppermute | solution.py:18
  20.8 0.1 slice.132
  20.8 0.8 slice.130
  21.6 0.1 compare_and_fusion
  21.7 0.8 fusion.56
  22.5 0.1 compare_and_fusion.3
  22.6 0.1 fusion.50
  22.7 0.1 convert_reduce_fusion
  22.8 0.1 broadcast_multiply_fusion
  22.9 43.6 %collective-permute-done = f32[33,128]{1,0:T(8,128)S(1)} collective-permute-done((f32[33,128]{1,0:T(8,128)S(1)}, f32[33,128]{1,0:T(8,128)S(1)}, u32[]{:S(2)}, u32[]{:S(2)}) %collective-permute-start) | collective-permute-done | bytes 16928 | tf_op jit(solution)/shard_map/ppermute | solution.py:18
  66.4 0.2 maximum_reduce_fusion
  66.6 0.1 copy.45
  66.8 0.1 reshape.108
  66.9 1.6 gather_fusion
  68.5 0.1 fusion.70
  68.6 0.3 fusion.26
  68.9 0.1 select_bitcast_fusion
  69.0 4.3 %all-to-all-done = f32[16,512,72]{1,2,0:T(8,128)} async-done(((f32[16,512,72]{1,2,0:T(8,128)}), f32[16,512,72]{1,2,0:T(8,128)}, u32[]{:S(2)}, u32[]{:S(2)}) %all-to-all-start) | async-done | bytes 2359328 | tf_op jit(solution)/shard_map/all_to_all | solution.py:115
  73.3 1.6 slice_reduce_fusion
  74.9 0.1 slice.140
  75.0 1.9 %collective-permute-start.1 = (f32[1,1152]{1,0:T(1,128)S(1)}, f32[1,1152]{1,0:T(1,128)S(1)}, u32[]{:S(2)}, u32[]{:S(2)}) collective-permute-start(f32[1,1152]{1,0:T(1,128)S(1)} %slice.140), channel_id=1, source_target_pairs={{0,1},{1,2},{2,3},{3,4},{4,5},{5,6},{6,7},{7,8},{8,9},{9,10},{10,1... | collective-permute-start | bytes 13832 | tf_op jit(solution)/shard_map/ppermute | solution.py:24
  76.9 0.3 fusion.20
  77.2 0.1 mul.204
  77.3 3.0 %copy.48 = f32[512,1152]{1,0:T(8,128)} copy(f32[512,1152]{0,1:T(8,128)} %bitcast.1) | data formatting | bytes 4718592 | tf_op jit(solution)/shard_map/all_to_all | solution.py:115
  80.4 3.1 %copy.46 = f32[511,1152]{1,0:T(8,128)} copy(f32[511,1152]{0,1:T(8,128)} %bitcast.4) | data formatting | bytes 4709376 | tf_op jit(solution)/shard_map/slice | solution.py:38
  83.4 1.6 collective-permute-done.1
  85.0 3.3 %fusion.12 = f32[512,1152]{1,0:T(8,128)S(1)} fusion(f32[512,1152]{1,0:T(8,128)} %copy.48, f32[511,1152]{1,0:T(8,128)} %copy.46, f32[1,1152]{1,0:T(1,128)S(1)} %collective-permute-done.1, f32[1152]{0:T(1024)S(1)} %get-tuple-element.27, f32[512]{0:T(512)S(1)} %get-tuple-element.3, f32[1152]{0:T(1024)S(1)} %get-tuple-element.28, f32[512]{0:T(512)S(1)} %get-tuple-element.2, ...), kind=kLoop, calls=%fused_computation.18 | loop fusion | flops 5898240 | bytes 7097856 | tf_op jit(solution)/shard_map/mul | solution.py:39
  88.4 0.0 copy-start.7
  88.4 1.8 %fusion.66 = f32[512,1152]{1,0:T(8,128)S(1)} fusion(bf16[1152,1152]{1,0:T(8,128)(2,1)S(1)} %copy-done, f32[512,1152]{1,0:T(8,128)S(1)} %fusion.12), kind=kOutput, calls=%fused_computation.123 | convolution fusion | flops 1359544320 | bytes 7372800 | tf_op jit(solution)/shard_map/dot_general | solution.py:43
  90.3 0.0 copy-start.3
  90.3 1.9 %fusion.9 = f32[512,1152]{1,0:T(8,128)S(1)} fusion(f32[512,1152]{1,0:T(8,128)S(1)} %fusion.12, f32[512,1152]{1,0:T(8,128)S(1)} %fusion.66, bf16[1152,1152]{1,0:T(8,128)(2,1)S(1)} %copy-done.7, f32[512]{0:T(512)S(1)} %get-tuple-element.25), kind=kOutput, calls=%fused_computation.13 | convolution fusion | flops 1363673088 | bytes 9734144 | tf_op jit(solution)/shard_map/dot_general | solution.py:44
  92.2 1.4 copy-done.1
  93.6 2.1 %collective-permute-start.2 = (f32[1,1152]{1,0:T(1,128)S(1)}, f32[1,1152]{1,0:T(1,128)S(1)}, u32[]{:S(2)}, u32[]{:S(2)}) collective-permute-start(f32[1,1152]{1,0:T(1,128)S(1)} %slice.188), channel_id=1, source_target_pairs={{0,1},{1,2},{2,3},{3,4},{4,5},{5,6},{6,7},{7,8},{8,9},{9,10},{10,1... | collective-permute-start | bytes 13832 | tf_op jit(solution)/shard_map/ppermute | solution.py:24
  95.7 0.5 fusion.63
  96.2 0.2 fusion.16
  96.5 0.1 fusion.38
  96.6 0.2 slice_reduce_fusion.2
  96.8 0.1 copy.49
  96.9 1.0 gather_fusion.1
  97.9 0.1 select_bitcast_fusion.1
  98.0 0.3 fusion.18
  98.4 5.3 %collective-permute-done.2 = f32[1,1152]{1,0:T(1,128)S(1)} collective-permute-done((f32[1,1152]{1,0:T(1,128)S(1)}, f32[1,1152]{1,0:T(1,128)S(1)}, u32[]{:S(2)}, u32[]{:S(2)}) %collective-permute-start.2) | collective-permute-done | bytes 4640 | tf_op jit(solution)/shard_map/ppermute | solution.py:24
  103.7 3.3 %fusion.15 = f32[512,1152]{1,0:T(8,128)S(1)} fusion(f32[512,1152]{1,0:T(8,128)} %copy-done.1, f32[511,1152]{1,0:T(8,128)} %bitcast.30, f32[1,1152]{1,0:T(1,128)S(1)} %collective-permute-done.2, f32[512]{0:T(512)S(1)} %get-tuple-element.5, f32[512]{0:T(512)S(1)} %get-tuple-element.4, f32[1152]{0:T(1024)S(1)} %get-tuple-element.27, ...), kind=kLoop, calls=%fused_computation.22 | loop fusion | flops 5898240 | bytes 7097856 | tf_op jit(solution)/shard_map/mul | solution.py:39
  107.0 0.0 copy-start.8
  107.0 1.9 %fusion.61 = f32[512,1152]{1,0:T(8,128)S(1)} fusion(bf16[1152,1152]{1,0:T(8,128)(2,1)S(1)} %copy-done, f32[512,1152]{1,0:T(8,128)S(1)} %fusion.15), kind=kOutput, calls=%fused_computation.118 | convolution fusion | flops 1359544320 | bytes 7372800 | tf_op jit(solution)/shard_map/dot_general | solution.py:43
  108.9 0.7 copy-done.8
  109.6 3.4 %fusion.6 = f32[512,1152]{1,0:T(8,128)} fusion(f32[512,1152]{1,0:T(8,128)S(1)} %fusion.15, f32[512,1152]{1,0:T(8,128)S(1)} %fusion.61, bf16[1152,1152]{1,0:T(8,128)(2,1)S(1)} %copy-done.8, f32[512]{0:T(512)S(1)} %get-tuple-element.25), kind=kOutput, calls=%fused_computation.10 | convolution fusion | flops 1363673088 | bytes 9734144 | tf_op jit(solution)/shard_map/dot_general | solution.py:44
  113.0 3.1 %copy.50 = f32[512,1152]{0,1:T(8,128)} copy(f32[512,1152]{1,0:T(8,128)} %fusion.6) | data formatting | bytes 4718592 | tf_op jit(solution)/shard_map/add | solution.py:123
  116.1 5.2 %all-to-all-start.1 = ((f32[512,16,72]{0,2,1:T(8,128)}), f32[512,16,72]{0,2,1:T(8,128)}, u32[]{:S(2)}, u32[]{:S(2)}) async-start(f32[512,16,72]{0,2,1:T(8,128)} %bitcast.32), calls=%async_computation.1 | async-start | bytes 4718592 | tf_op jit(solution)/shard_map/all_to_all | solution.py:142
  121.3 0.4 collective-permute-start.3
  121.7 2.1 %fusion.58 = f32[512,128]{1,0:T(8,128)S(1)} fusion(bf16[1152,128]{1,0:T(8,128)(2,1)S(1)} %copy-done.3, f32[512,1152]{1,0:T(8,128)} %copy-done.2), kind=kOutput, calls=%fused_computation.115 | convolution fusion | flops 151584768 | bytes 2916352 | tf_op jit(solution)/shard_map/dot_general | solution.py:46
  123.9 0.2 convolution_divide_fusion
  124.1 1.7 collective-permute-start.4
  125.8 53.8 %collective-permute-done.3 = f32[33,128]{1,0:T(8,128)S(1)} collective-permute-done((f32[33,128]{1,0:T(8,128)S(1)}, f32[33,128]{1,0:T(8,128)S(1)}, u32[]{:S(2)}, u32[]{:S(2)}) %collective-permute-start.3) | collective-permute-done | bytes 16928 | tf_op jit(solution)/shard_map/ppermute | solution.py:18
  179.7 0.1 maximum_select_fusion
  179.8 0.1 reshape.109
  179.9 0.1 fusion.69
  180.0 0.3 fusion.23
  180.3 0.1 mul.221
  180.4 0.6 fusion.44
  181.0 3.4 %copy.53 = f32[16,9,8,512]{3,2,0,1:T(8,128)} copy(f32[16,9,8,512]{3,2,1,0:T(8,128)} %bitcast.14) | data formatting | bytes 4718592 | tf_op jit(solution)/shard_map/all_to_all | solution.py:142
  (29 shorter events, 0.1 us)
Async XLA Ops:
  0.6 87.8 %copy-start = (bf16[1152,1152]{1,0:T(8,128)(2,1)S(1)}, bf16[1152,1152]{1,0:T(8,128)(2,1)}, u32[]{:S(2)}) copy-start(bf16[1152,1152]{1,0:T(8,128)(2,1)} %param.10) | copy-start | bytes 7962628
  4.1 9.4 %copy-start.5 = (f32[64,128]{1,0:T(8,128)S(1)}, f32[64,128]{1,0:T(8,128)}, u32[]{:S(2)}) copy-start(f32[64,128]{1,0:T(8,128)} %param.9) | copy-start | bytes 98308
  4.1 16.7 %copy-start.4 = (s32[131072]{0:T(1024)S(1)}, s32[131072]{0:T(1024)}, u32[]{:S(2)}) copy-start(s32[131072]{0:T(1024)} %param.14) | copy-start | bytes 1572868
  4.1 69.2 %all-to-all-start = ((f32[16,512,72]{1,2,0:T(8,128)}), f32[16,512,72]{1,2,0:T(8,128)}, u32[]{:S(2)}, u32[]{:S(2)}) async-start(f32[16,512,72]{1,2,0:T(8,128)} %bitcast.31), calls=%async_computation | async-start | bytes 4718592 | tf_op jit(solution)/shard_map/all_to_all | solution.py:115
  13.5 52.9 %collective-permute-start = (f32[33,128]{1,0:T(8,128)S(1)}, f32[33,128]{1,0:T(8,128)S(1)}, u32[]{:S(2)}, u32[]{:S(2)}) collective-permute-start(f32[33,128]{1,0:T(8,128)S(1)} %get-tuple-element.24), channel_id=1, source_target_pairs={{1,0},{2,1},{3,2},{4,3},{5,4},{6,5},{7,6},{8,7},{9,8},{10,9},{11,1... | collective-permute-start | bytes 50696 | tf_op jit(solution)/shard_map/ppermute | solution.py:18
  75.0 10.0 %collective-permute-start.1 = (f32[1,1152]{1,0:T(1,128)S(1)}, f32[1,1152]{1,0:T(1,128)S(1)}, u32[]{:S(2)}, u32[]{:S(2)}) collective-permute-start(f32[1,1152]{1,0:T(1,128)S(1)} %slice.140), channel_id=1, source_target_pairs={{0,1},{1,2},{2,3},{3,4},{4,5},{5,6},{6,7},{7,8},{8,9},{9,10},{10,1... | collective-permute-start | bytes 13832 | tf_op jit(solution)/shard_map/ppermute | solution.py:24
  80.4 4.7 %copy-start.6 = (f32[1152]{0:T(1024)S(1)}, f32[1152]{0:T(1024)}, u32[]{:S(2)}) copy-start(f32[1152]{0:T(1024)} %param.13) | copy-start | bytes 13828
  88.4 1.9 %copy-start.7 = (bf16[1152,1152]{1,0:T(8,128)(2,1)S(1)}, bf16[1152,1152]{1,0:T(8,128)(2,1)}, u32[]{:S(2)}) copy-start(bf16[1152,1152]{1,0:T(8,128)(2,1)} %param.11) | copy-start | bytes 7962628
  90.3 5.5 %copy-start.3 = (bf16[1152,128]{1,0:T(8,128)(2,1)S(1)}, bf16[1152,128]{1,0:T(8,128)(2,1)}, u32[]{:S(2)}) copy-start(bf16[1152,128]{1,0:T(8,128)(2,1)} %param.12) | copy-start | bytes 884740
  92.2 1.4 copy-start.1
  93.6 10.0 %collective-permute-start.2 = (f32[1,1152]{1,0:T(1,128)S(1)}, f32[1,1152]{1,0:T(1,128)S(1)}, u32[]{:S(2)}, u32[]{:S(2)}) collective-permute-start(f32[1,1152]{1,0:T(1,128)S(1)} %slice.188), channel_id=1, source_target_pairs={{0,1},{1,2},{2,3},{3,4},{4,5},{5,6},{6,7},{7,8},{8,9},{9,10},{10,1... | collective-permute-start | bytes 13832 | tf_op jit(solution)/shard_map/ppermute | solution.py:24
  107.0 1.9 %copy-start.2 = (f32[512,1152]{1,0:T(8,128)}, f32[512,1152]{1,0:T(8,128)S(1)}, u32[]{:S(2)}) copy-start(f32[512,1152]{1,0:T(8,128)S(1)} %fusion.15) | copy-start | bytes 7077892
  107.0 2.6 %copy-start.8 = (bf16[1152,1152]{1,0:T(8,128)(2,1)S(1)}, bf16[1152,1152]{1,0:T(8,128)(2,1)}, u32[]{:S(2)}) copy-start(bf16[1152,1152]{1,0:T(8,128)(2,1)} %param.11) | copy-start | bytes 7962628
  116.1 65.0 %all-to-all-start.1 = ((f32[512,16,72]{0,2,1:T(8,128)}), f32[512,16,72]{0,2,1:T(8,128)}, u32[]{:S(2)}, u32[]{:S(2)}) async-start(f32[512,16,72]{0,2,1:T(8,128)} %bitcast.32), calls=%async_computation.1 | async-start | bytes 4718592 | tf_op jit(solution)/shard_map/all_to_all | solution.py:142
  121.3 58.4 %collective-permute-start.3 = (f32[33,128]{1,0:T(8,128)S(1)}, f32[33,128]{1,0:T(8,128)S(1)}, u32[]{:S(2)}, u32[]{:S(2)}) collective-permute-start(f32[33,128]{1,0:T(8,128)S(1)} %get-tuple-element.21), channel_id=1, source_target_pairs={{255,0},{0,1},{1,2},{2,3},{3,4},{4,5},{5,6},{6,7},{7,8},{8,9},{9,1... | collective-permute-start | bytes 50696 | tf_op jit(solution)/shard_map/ppermute | solution.py:18
  124.1 56.3 %collective-permute-start.4 = (f32[32,128]{1,0:T(8,128)S(1)}, f32[32,128]{1,0:T(8,128)S(1)}, u32[]{:S(2)}, u32[]{:S(2)}) collective-permute-start(f32[32,128]{1,0:T(8,128)S(1)} %get-tuple-element.19), channel_id=1, source_target_pairs={{255,0},{0,1},{1,2},{2,3},{3,4},{4,5},{5,6},{6,7},{7,8},{8,9},{9,1... | collective-permute-start | bytes 49160 | tf_op jit(solution)/shard_map/ppermute | solution.py:18

commit v12 on v7

--- a/solution.py
+++ b/solution.py
@@ -9,7 +9,7 @@
 LEVELS = 64
 STEPS = 2
 ALL = ("band", "bin")
-EXTRA = 8
+EXTRA = 16
 
 
 def shifted(block, axis, distance):

time: 180 us -> 180 us (level)
  no operation moved by 1% of the time
where the time goes in v12:
time: 180 us; the launch traced here: 178 us
  waiting for transfers between devices  101 us (56%)
  starting transfers between devices  26.1 us (14%)
  local copies, waits for them, and re-layouts  23 us (13%)
  matrix products  13.8 us (8%)
  other arithmetic  12.4 us (7%)
    ppermute x3, waiting for transfers between devices, shifted(): return lax.ppermute(block, axis, route)  91.9 us
    all_to_all x1, starting transfers between devices, per_device(): lax.all_to_all(spectrum, 'bin', split_axis=0, concat_axis=1, tiled=True)  9.41 us
    ppermute x3, starting transfers between devices, shifted(): return lax.ppermute(block, axis, route)  9.31 us
    all_to_all x2, local copies, waits for them, and re-layouts, per_device(): lax.all_to_all(spectrum, 'bin', split_axis=0, concat_axis=1, tiled=True)  6.49 us
    ppermute x1, waiting for transfers between devices, from_behind(): return lax.ppermute(shard, axis, pairs)  5.59 us
    dot_general x2, matrix products, sources(): other = jnp.dot(rounded, source_b, preferred_element_type=jnp.float32)  5.53 us
    all_to_all x1, starting transfers between devices, per_device(): lax.all_to_all(field, 'bin', split_axis=1, concat_axis=0, tiled=True)  5.28 us
    dot_general x2, matrix products, sources(): gain = jnp.dot(rounded, source_a, preferred_element_type=jnp.float32)  5.2 us
  transfers between devices with their start and end apart: 6, of which 5 were waited for; matrix products, arithmetic and copies ran while one was open for 10% of the time, Pallas kernels for 0%

profile of v12, /device:TPU:88, one launch (start us, length us, event | category | flops | bytes accessed | tf_op | source)
XLA Modules:
  0.0 177.8 jit_solution(1831206313123911604)
XLA Ops:
  0.6 0.0 copy-start
  0.6 3.4 %copy.50 = f32[9,16,8,512]{3,2,0,1:T(8,128)} copy(f32[9,16,8,512]{3,2,1,0:T(8,128)} %bitcast.32) | data formatting | bytes 4718592 | tf_op jit(solution)/shard_map/all_to_all | solution.py:115
  4.1 9.4 %all-to-all-start = ((f32[16,512,72]{1,2,0:T(8,128)}), f32[16,512,72]{1,2,0:T(8,128)}, u32[]{:S(2)}, u32[]{:S(2)}) async-start(f32[16,512,72]{1,2,0:T(8,128)} %bitcast.30), calls=%async_computation | async-start | bytes 4718592 | tf_op jit(solution)/shard_map/all_to_all | solution.py:115
  13.5 0.6 fusion.70
  14.1 7.2 %collective-permute-start.1 = (f32[33,128]{1,0:T(8,128)S(1)}, f32[33,128]{1,0:T(8,128)S(1)}, u32[]{:S(2)}, u32[]{:S(2)}) collective-permute-start(f32[33,128]{1,0:T(8,128)S(1)} %get-tuple-element.28), channel_id=1, source_target_pairs={{1,0},{2,1},{3,2},{4,3},{5,4},{6,5},{7,6},{8,7},{9,8},{10,9},{11,1... | collective-permute-start | bytes 50696 | tf_op jit(solution)/shard_map/ppermute | solution.py:18
  21.3 0.1 slice.132
  21.4 0.8 slice.128
  22.1 0.1 compare_and_fusion
  22.2 0.6 compare_and_fusion.3
  22.8 0.6 pad_clamp_fusion
  23.4 1.4 broadcast_multiply_fusion
  24.8 0.7 fusion.50
  25.4 0.7 convert_reduce_fusion
  26.1 0.7 broadcast_multiply_fusion.1
  26.8 0.6 compare_and_fusion.1
  27.4 38.9 %collective-permute-done.1 = f32[33,128]{1,0:T(8,128)S(1)} collective-permute-done((f32[33,128]{1,0:T(8,128)S(1)}, f32[33,128]{1,0:T(8,128)S(1)}, u32[]{:S(2)}, u32[]{:S(2)}) %collective-permute-start.1) | collective-permute-done | bytes 16928 | tf_op jit(solution)/shard_map/ppermute | solution.py:18
  66.3 0.2 maximum_reduce_fusion
  66.5 0.4 copy-done.12
  66.9 0.1 copy.42
  67.1 0.1 reshape.110
  67.2 0.1 fusion.67
  67.3 0.3 fusion.26
  67.6 0.7 mul.233
  68.3 1.6 gather_fusion
  69.9 0.1 select_bitcast_fusion
  70.0 3.3 %all-to-all-done = f32[16,512,72]{1,2,0:T(8,128)} async-done(((f32[16,512,72]{1,2,0:T(8,128)}), f32[16,512,72]{1,2,0:T(8,128)}, u32[]{:S(2)}, u32[]{:S(2)}) %all-to-all-start) | async-done | bytes 2359328 | tf_op jit(solution)/shard_map/all_to_all | solution.py:115
  73.3 1.3 slice.171
  74.6 0.8 copy.46
  75.5 2.1 %collective-permute-start = (f32[16,1152]{1,0:T(8,128)}, f32[16,1152]{1,0:T(8,128)S(1)}, u32[]{:S(2)}, u32[]{:S(2)}) collective-permute-start(f32[16,1152]{1,0:T(8,128)} %copy.46), channel_id=1, source_target_pairs={{0,1},{1,2},{2,3},{3,4},{4,5},{5,6},{6,7},{7,8},{8,9},{9,10},{10,1... | collective-permute-start | bytes 221192 | tf_op jit(solution)/shard_map/ppermute | solution.py:24
  77.6 0.3 fusion.18
  77.9 3.0 %copy.41 = f32[512,1152]{1,0:T(8,128)} copy(f32[512,1152]{0,1:T(8,128)} %bitcast.2) | data formatting | bytes 4718592 | tf_op jit(solution)/shard_map/all_to_all | solution.py:115
  81.0 5.6 %collective-permute-done = f32[16,1152]{1,0:T(8,128)S(1)} collective-permute-done((f32[16,1152]{1,0:T(8,128)}, f32[16,1152]{1,0:T(8,128)S(1)}, u32[]{:S(2)}, u32[]{:S(2)}) %collective-permute-start) | collective-permute-done | bytes 73760 | tf_op jit(solution)/shard_map/ppermute | solution.py:24
  86.5 1.8 %fusion.10 = f32[527,1152]{1,0:T(8,128)S(1)} fusion(f32[16,1152]{1,0:T(8,128)S(1)} %collective-permute-done, f32[512,1152]{1,0:T(8,128)} %copy.41), kind=kLoop, calls=%fused_computation.16 | loop fusion | flops 607104 | bytes 4861440 | tf_op jit(solution)/shard_map/concatenate | solution.py:117
  88.4 0.0 copy-start.7
  88.5 2.5 %fusion.64 = (bf16[528,1152]{1,0:T(8,128)(2,1)S(1)}, f32[528,1152]{1,0:T(8,128)}) fusion(f32[527,1152]{1,0:T(8,128)S(1)} %fusion.10, f32[1152]{0:T(1024)S(1)} %get-tuple-element.31, f32[528]{0:T(1024)S(1)} %get-tuple-element.3, f32[1152]{0:T(1024)S(1)} %copy-done.11, f32[528]{0:T(1024)S(1)} %get-tuple-element.2, f32[1152]{0:T(1024)S(1)} %copy-done.16, ...), kind=kLoop, calls=%fused_computation.122 | loop fusion | flops 6690816 | bytes 8531136 | tf_op jit(solution)/shard_map/convert_element_type | solution.py:123
  91.0 1.0 copy-done.4
  92.0 0.5 fusion.14
  92.5 0.2 fusion.16
  92.8 0.1 fusion.38
  92.9 0.2 slice_reduce_fusion.1
  93.1 0.1 copy.43
  93.2 1.0 gather_fusion.1
  94.2 0.1 select_bitcast_fusion.1
  94.4 0.3 fusion.20
  94.7 3.3 %fusion.71 = f32[528,1152]{1,0:T(8,128)S(1)} fusion(bf16[528,1152]{1,0:T(8,128)(2,1)} %copy-done.4, bf16[1152,1152]{1,0:T(8,128)(2,1)S(1)} %copy-done), kind=kOutput, calls=%fused_computation.128 | convolution fusion | flops 1401421824 | bytes 6303744 | tf_op jit(solution)/shard_map/dot_general | solution.py:43
  98.1 2.1 %fusion.6 = f32[528,1152]{1,0:T(8,128)S(1)} fusion(f32[528,1152]{1,0:T(8,128)S(1)} %copy-done.3, f32[528,1152]{1,0:T(8,128)S(1)} %fusion.71, bf16[528,1152]{1,0:T(8,128)(2,1)S(1)} %copy-done.5, bf16[1152,1152]{1,0:T(8,128)(2,1)S(1)} %copy-done.27, f32[528]{0:T(1024)S(1)} %copy-done.22), kind=kOutput, calls=%fused_computation.12 | convolution fusion | flops 1405679616 | bytes 11171904 | tf_op jit(solution)/shard_map/dot_general | solution.py:44
  100.3 1.0 fusion.13
  101.3 1.8 %fusion.61 = f32[512,1152]{1,0:T(8,128)S(1)} fusion(bf16[1152,1152]{1,0:T(8,128)(2,1)S(1)} %copy-done, f32[512,1152]{1,0:T(8,128)S(1)} %fusion.13), kind=kOutput, calls=%fused_computation.120 | convolution fusion | flops 1359544320 | bytes 7372800 | tf_op jit(solution)/shard_map/dot_general | solution.py:43
  103.2 3.4 %fusion.9 = f32[512,1152]{1,0:T(8,128)} fusion(f32[512,1152]{1,0:T(8,128)S(1)} %fusion.13, f32[512,1152]{1,0:T(8,128)S(1)} %fusion.61, bf16[1152,1152]{1,0:T(8,128)(2,1)S(1)} %copy-done.27, f32[512]{0:T(512)S(1)} %copy-done.24), kind=kOutput, calls=%fused_computation.15 | convolution fusion | flops 1363673088 | bytes 9734144 | tf_op jit(solution)/shard_map/dot_general | solution.py:44
  106.6 3.2 %copy.44 = f32[512,1152]{0,1:T(8,128)} copy(f32[512,1152]{1,0:T(8,128)} %fusion.9) | data formatting | bytes 4718592 | tf_op jit(solution)/shard_map/add | solution.py:125
  109.8 5.3 %all-to-all-start.1 = ((f32[512,16,72]{0,2,1:T(8,128)}), f32[512,16,72]{0,2,1:T(8,128)}, u32[]{:S(2)}, u32[]{:S(2)}) async-start(f32[512,16,72]{0,2,1:T(8,128)} %bitcast.31), calls=%async_computation.1 | async-start | bytes 4718592 | tf_op jit(solution)/shard_map/all_to_all | solution.py:149
  115.1 0.4 collective-permute-start.2
  115.5 2.1 %fusion.58 = f32[512,128]{1,0:T(8,128)S(1)} fusion(bf16[1152,128]{1,0:T(8,128)(2,1)S(1)} %copy-done.7, f32[512,1152]{1,0:T(8,128)} %copy-done.2), kind=kOutput, calls=%fused_computation.117 | convolution fusion | flops 151584768 | bytes 2916352 | tf_op jit(solution)/shard_map/dot_general | solution.py:46
  117.7 0.2 convolution_divide_fusion
  117.9 1.7 collective-permute-start.3
  119.6 53.0 %collective-permute-done.2 = f32[33,128]{1,0:T(8,128)S(1)} collective-permute-done((f32[33,128]{1,0:T(8,128)S(1)}, f32[33,128]{1,0:T(8,128)S(1)}, u32[]{:S(2)}, u32[]{:S(2)}) %collective-permute-start.2) | collective-permute-done | bytes 16928 | tf_op jit(solution)/shard_map/ppermute | solution.py:18
  172.6 0.1 maximum_select_fusion
  172.7 0.1 reshape.111
  172.8 0.1 fusion.66
  173.0 0.3 fusion.23
  173.3 0.1 mul.257
  173.4 0.6 fusion.44
  174.0 0.5 all-to-all-done.1
  174.5 3.4 %copy.48 = f32[16,9,8,512]{3,2,0,1:T(8,128)} copy(f32[16,9,8,512]{3,2,1,0:T(8,128)} %bitcast.14) | data formatting | bytes 4718592 | tf_op jit(solution)/shard_map/all_to_all | solution.py:149
  (64 shorter events, 0.2 us)
Async XLA Ops:
  0.6 94.1 %copy-start = (bf16[1152,1152]{1,0:T(8,128)(2,1)S(1)}, bf16[1152,1152]{1,0:T(8,128)(2,1)}, u32[]{:S(2)}) copy-start(bf16[1152,1152]{1,0:T(8,128)(2,1)} %param.10) | copy-start | bytes 7962628
  4.1 9.4 %copy-start.8 = (f32[64,128]{1,0:T(8,128)S(1)}, f32[64,128]{1,0:T(8,128)}, u32[]{:S(2)}) copy-start(f32[64,128]{1,0:T(8,128)} %param.9) | copy-start | bytes 98308
  4.1 17.2 %copy-start.6 = (s32[131072]{0:T(1024)S(1)}, s32[131072]{0:T(1024)}, u32[]{:S(2)}) copy-start(s32[131072]{0:T(1024)} %param.14) | copy-start | bytes 1572868
  4.1 69.2 %all-to-all-start = ((f32[16,512,72]{1,2,0:T(8,128)}), f32[16,512,72]{1,2,0:T(8,128)}, u32[]{:S(2)}, u32[]{:S(2)}) async-start(f32[16,512,72]{1,2,0:T(8,128)} %bitcast.30), calls=%async_computation | async-start | bytes 4718592 | tf_op jit(solution)/shard_map/all_to_all | solution.py:115
  14.1 52.2 %collective-permute-start.1 = (f32[33,128]{1,0:T(8,128)S(1)}, f32[33,128]{1,0:T(8,128)S(1)}, u32[]{:S(2)}, u32[]{:S(2)}) collective-permute-start(f32[33,128]{1,0:T(8,128)S(1)} %get-tuple-element.28), channel_id=1, source_target_pairs={{1,0},{2,1},{3,2},{4,3},{5,4},{6,5},{7,6},{8,7},{9,8},{10,9},{11,1... | collective-permute-start | bytes 50696 | tf_op jit(solution)/shard_map/ppermute | solution.py:18
  22.8 43.7 %copy-start.14 = (s32[512]{0:T(512)}, s32[512]{0:T(512)S(1)}, u32[]{:S(2)}) copy-start(s32[512]{0:T(512)S(1)} %get-tuple-element.11) | copy-start | bytes 6148
  24.8 41.7 %copy-start.17 = (f32[528]{0:T(1024)}, f32[528]{0:T(1024)S(1)}, u32[]{:S(2)}) copy-start(f32[528]{0:T(1024)S(1)} %get-tuple-element.13) | copy-start | bytes 6340
  66.3 0.6 copy-start.12
  75.5 11.1 %collective-permute-start = (f32[16,1152]{1,0:T(8,128)}, f32[16,1152]{1,0:T(8,128)S(1)}, u32[]{:S(2)}, u32[]{:S(2)}) collective-permute-start(f32[16,1152]{1,0:T(8,128)} %copy.46), channel_id=1, source_target_pairs={{0,1},{1,2},{2,3},{3,4},{4,5},{5,6},{6,7},{7,8},{8,9},{9,10},{10,1... | collective-permute-start | bytes 221192 | tf_op jit(solution)/shard_map/ppermute | solution.py:24
  80.9 7.4 %copy-start.1 = (f32[512,1152]{1,0:T(8,128)S(1)}, f32[512,1152]{1,0:T(8,128)}, u32[]{:S(2)}) copy-start(f32[512,1152]{1,0:T(8,128)} %copy.41) | copy-start | bytes 7077892
  80.9 7.4 %copy-start.11 = (f32[1152]{0:T(1024)S(1)}, f32[1152]{0:T(1024)}, u32[]{:S(2)}) copy-start(f32[1152]{0:T(1024)} %get-tuple-element.32) | copy-start | bytes 13828
  80.9 7.4 %copy-start.16 = (f32[1152]{0:T(1024)S(1)}, f32[1152]{0:T(1024)}, u32[]{:S(2)}) copy-start(f32[1152]{0:T(1024)} %param.13) | copy-start | bytes 13828
  80.9 7.5 %copy-start.18 = (f32[528]{0:T(1024)S(1)}, f32[528]{0:T(1024)}, u32[]{:S(2)}) copy-start(f32[528]{0:T(1024)} %copy-done.17) | copy-start | bytes 6340
  88.4 3.6 %copy-start.7 = (bf16[1152,128]{1,0:T(8,128)(2,1)S(1)}, bf16[1152,128]{1,0:T(8,128)(2,1)}, u32[]{:S(2)}) copy-start(bf16[1152,128]{1,0:T(8,128)(2,1)} %param.12) | copy-start | bytes 884740
  88.4 4.1 %copy-start.15 = (s32[512]{0:T(512)S(1)}, s32[512]{0:T(512)}, u32[]{:S(2)}) copy-start(s32[512]{0:T(512)} %copy-done.14) | copy-start | bytes 6148
  88.4 4.1 %copy-start.21 = (f32[64]{0:T(128)S(1)}, f32[64]{0:T(128)}, u32[]{:S(2)}) copy-start(f32[64]{0:T(128)} %convert_reduce_fusion) | copy-start | bytes 772
  88.4 4.3 %copy-start.10 = (f32[33,128]{1,0:T(8,128)S(1)}, f32[33,128]{1,0:T(8,128)}, u32[]{:S(2)}) copy-start(f32[33,128]{1,0:T(8,128)} %get-tuple-element.27) | copy-start | bytes 50692
  88.5 4.3 %copy-start.13 = (f32[33,128]{1,0:T(8,128)S(1)}, f32[33,128]{1,0:T(8,128)}, u32[]{:S(2)}) copy-start(f32[33,128]{1,0:T(8,128)} %copy-done.12) | copy-start | bytes 50692
  88.5 4.3 %copy-start.25 = (pred[64]{0:T(512)(128)(4,1)S(1)}, pred[64]{0:T(512)(128)(4,1)}, u32[]{:S(2)}) copy-start(pred[64]{0:T(512)(128)(4,1)} %get-tuple-element.33) | copy-start | bytes 196
  88.5 4.3 %copy-start.26 = (pred[64]{0:T(512)(128)(4,1)S(1)}, pred[64]{0:T(512)(128)(4,1)}, u32[]{:S(2)}) copy-start(pred[64]{0:T(512)(128)(4,1)} %get-tuple-element.34) | copy-start | bytes 196
  91.0 1.0 copy-start.4
  91.0 1.8 %copy-start.9 = (f32[64,128]{1,0:T(8,128)S(1)}, f32[64,128]{1,0:T(8,128)}, u32[]{:S(2)}) copy-start(f32[64,128]{1,0:T(8,128)} %mul.233) | copy-start | bytes 98308
  91.0 2.2 %copy-start.19 = (s32[1024]{0:T(1024)S(1)}, s32[1024]{0:T(1024)}, u32[]{:S(2)}) copy-start(s32[1024]{0:T(1024)} %pad_clamp_fusion) | copy-start | bytes 12292
  91.0 3.3 %copy-start.23 = (pred[512]{0:T(512)(128)(4,1)S(1)}, pred[512]{0:T(512)(128)(4,1)}, u32[]{:S(2)}) copy-start(pred[512]{0:T(512)(128)(4,1)} %get-tuple-element.10) | copy-start | bytes 1540
  94.7 3.4 %copy-start.3 = (f32[528,1152]{1,0:T(8,128)S(1)}, f32[528,1152]{1,0:T(8,128)}, u32[]{:S(2)}) copy-start(f32[528,1152]{1,0:T(8,128)} %get-tuple-element.15) | copy-start | bytes 7299076
  94.7 3.4 %copy-start.5 = (bf16[528,1152]{1,0:T(8,128)(2,1)S(1)}, bf16[528,1152]{1,0:T(8,128)(2,1)}, u32[]{:S(2)}) copy-start(bf16[528,1152]{1,0:T(8,128)(2,1)} %copy-done.4) | copy-start | bytes 3649540
  94.7 3.4 %copy-start.22 = (f32[528]{0:T(1024)S(1)}, f32[528]{0:T(1024)}, u32[]{:S(2)}) copy-start(f32[528]{0:T(1024)} %get-tuple-element.12) | copy-start | bytes 6340
  94.7 3.4 %copy-start.27 = (bf16[1152,1152]{1,0:T(8,128)(2,1)S(1)}, bf16[1152,1152]{1,0:T(8,128)(2,1)}, u32[]{:S(2)}) copy-start(bf16[1152,1152]{1,0:T(8,128)(2,1)} %param.11) | copy-start | bytes 7962628
  98.1 2.1 %copy-start.20 = (f32[512]{0:T(512)S(1)}, f32[512]{0:T(512)}, u32[]{:S(2)}) copy-start(f32[512]{0:T(512)} %get-tuple-element.30) | copy-start | bytes 6148
  101.3 1.9 %copy-start.2 = (f32[512,1152]{1,0:T(8,128)}, f32[512,1152]{1,0:T(8,128)S(1)}, u32[]{:S(2)}) copy-start(f32[512,1152]{1,0:T(8,128)S(1)} %fusion.13) | copy-start | bytes 7077892
  101.3 1.9 %copy-start.24 = (f32[512]{0:T(512)S(1)}, f32[512]{0:T(512)}, u32[]{:S(2)}) copy-start(f32[512]{0:T(512)} %get-tuple-element.29) | copy-start | bytes 6148
  109.8 64.7 %all-to-all-start.1 = ((f32[512,16,72]{0,2,1:T(8,128)}), f32[512,16,72]{0,2,1:T(8,128)}, u32[]{:S(2)}, u32[]{:S(2)}) async-start(f32[512,16,72]{0,2,1:T(8,128)} %bitcast.31), calls=%async_computation.1 | async-start | bytes 4718592 | tf_op jit(solution)/shard_map/all_to_all | solution.py:149
  115.1 57.6 %collective-permute-start.2 = (f32[33,128]{1,0:T(8,128)S(1)}, f32[33,128]{1,0:T(8,128)S(1)}, u32[]{:S(2)}, u32[]{:S(2)}) collective-permute-start(f32[33,128]{1,0:T(8,128)S(1)} %get-tuple-element.25), channel_id=1, source_target_pairs={{255,0},{0,1},{1,2},{2,3},{3,4},{4,5},{5,6},{6,7},{7,8},{8,9},{9,1... | collective-permute-start | bytes 50696 | tf_op jit(solution)/shard_map/ppermute | solution.py:18
  117.9 55.4 %collective-permute-start.3 = (f32[32,128]{1,0:T(8,128)S(1)}, f32[32,128]{1,0:T(8,128)S(1)}, u32[]{:S(2)}, u32[]{:S(2)}) collective-permute-start(f32[32,128]{1,0:T(8,128)S(1)} %get-tuple-element.23), channel_id=1, source_target_pairs={{255,0},{0,1},{1,2},{2,3},{3,4},{4,5},{5,6},{6,7},{7,8},{8,9},{9,1... | collective-permute-start | bytes 49160 | tf_op jit(solution)/shard_map/ppermute | solution.py:18

commit v13 on v7

--- a/solution.py
+++ b/solution.py
@@ -39,11 +39,12 @@
     return mask_cells[:, None] * (field - speed * (field - behind))
 
 
-def sources(rounded, mask_cells, source_a, source_b, stokes_kernel):
-    gain = jnp.dot(rounded, source_a, preferred_element_type=jnp.float32)
+def sources(rounded, mask_cells, joined, source_b, stokes_kernel):
+    both = jnp.dot(rounded, joined, preferred_element_type=jnp.float32)
+    gain = both[:, : source_b.shape[1]]
+    stokes = both[:, source_b.shape[1] :]
     other = jnp.dot(rounded, source_b, preferred_element_type=jnp.float32)
     increment = (0.1 * mask_cells[:, None] * (gain + 0.5 * gain * other)).astype(jnp.bfloat16)
-    stokes = jnp.dot(rounded, stokes_kernel, preferred_element_type=jnp.float32)
     return (increment, stokes)
 
 
@@ -95,6 +96,7 @@
     local_map = ext_map[EXTRA:]
     local_mask = ext_mask[EXTRA:]
     cos_b, sin_b = bin_angles(bins)
+    joined = jnp.concatenate([source_a, stokes_kernel], 1)
 
     first = device * columns + half
     where = jnp.mod(local_map - first, total)
@@ -120,7 +122,7 @@
     for step in range(STEPS):
         moved = propagate(field, prev, current, group_speed, cos_b, sin_b, mask)
         increment, stokes = sources(
-            moved.astype(jnp.bfloat16), mask, source_a, source_b, stokes_kernel
+            moved.astype(jnp.bfloat16), mask, joined, source_b, stokes_kernel
         )
         field = moved + increment.astype(jnp.float32)
         if step == 0:

time: 180 us -> 189 us (1.050)
  matrix products: 13.7 us -> 23.8 us
  local copies, waits for them, and re-layouts: 22.8 us -> 28.5 us
  other arithmetic: 12.9 us -> 8.92 us
  waiting for transfers between devices: 101 us -> 98.6 us
    dot_general x2, matrix products: 5.44 us -> 12.6 us  [sources(): other = jnp.dot(rounded, source_b, preferred_element_type=jnp.float32)]
    unnamed x50 -> x43, local copies, waits for them, and re-layouts: 1.12 us -> 6.06 us
    ppermute x3, waiting for transfers between devices: 92.6 us -> 90 us  [shifted(): return lax.ppermute(block, axis, route)]
    convert_element_type x1 -> x0, other arithmetic: 2.45 us -> none  [per_device(): moved.astype(jnp.bfloat16)]
    dot_general x4 -> x2, matrix products: 7.79 us -> 9.73 us  [sources(): both = jnp.dot(rounded, joined, preferred_element_type=jnp.float32)]
  transfers between devices with their start and end apart: 6 -> 6, of which waited for: 5 -> 5; matrix products, arithmetic and copies ran while one was open for 10% -> 11% of each run, Pallas kernels for 0% -> 0%
where the time goes in v13:
time: 189 us; the launch traced here: 187 us
  waiting for transfers between devices  98.6 us (52%)
  local copies, waits for them, and re-layouts  28.5 us (15%)
  starting transfers between devices  25.7 us (14%)
  matrix products  23.8 us (13%)
  other arithmetic  8.92 us (5%)
    ppermute x3, waiting for transfers between devices, shifted(): return lax.ppermute(block, axis, route)  90 us
    dot_general x2, matrix products, sources(): other = jnp.dot(rounded, source_b, preferred_element_type=jnp.float32)  12.6 us
    dot_general x2, matrix products, sources(): both = jnp.dot(rounded, joined, preferred_element_type=jnp.float32)  9.73 us
    all_to_all x1, starting transfers between devices, per_device(): lax.all_to_all(spectrum, 'bin', split_axis=0, concat_axis=1, tiled=True)  9.41 us
    ppermute x3, starting transfers between devices, shifted(): return lax.ppermute(block, axis, route)  9.31 us
    all_to_all x2, local copies, waits for them, and re-layouts, per_device(): lax.all_to_all(spectrum, 'bin', split_axis=0, concat_axis=1, tiled=True)  6.48 us
    unnamed x43, local copies, waits for them, and re-layouts  6.06 us
    all_to_all x1, starting transfers between devices, per_device(): lax.all_to_all(field, 'bin', split_axis=1, concat_axis=0, tiled=True)  4.88 us
  transfers between devices with their start and end apart: 6, of which 5 were waited for; matrix products, arithmetic and copies ran while one was open for 11% of the time, Pallas kernels for 0%

profile of v13, /device:TPU:88, one launch (start us, length us, event | category | flops | bytes accessed | tf_op | source)
XLA Modules:
  0.0 186.6 jit_solution(15876296646421605929)
XLA Ops:
  0.6 0.0 copy-start
  0.6 3.4 %copy.50 = f32[9,16,8,512]{3,2,0,1:T(8,128)} copy(f32[9,16,8,512]{3,2,1,0:T(8,128)} %bitcast.26) | data formatting | bytes 4718592 | tf_op jit(solution)/shard_map/all_to_all | solution.py:117
  4.1 9.4 %all-to-all-start = ((f32[16,512,72]{1,2,0:T(8,128)}), f32[16,512,72]{1,2,0:T(8,128)}, u32[]{:S(2)}, u32[]{:S(2)}) async-start(f32[16,512,72]{1,2,0:T(8,128)} %bitcast.24), calls=%async_computation | async-start | bytes 4718592 | tf_op jit(solution)/shard_map/all_to_all | solution.py:117
  13.5 0.6 fusion.72
  14.1 7.2 %collective-permute-start.1 = (f32[33,128]{1,0:T(8,128)S(1)}, f32[33,128]{1,0:T(8,128)S(1)}, u32[]{:S(2)}, u32[]{:S(2)}) collective-permute-start(f32[33,128]{1,0:T(8,128)S(1)} %get-tuple-element.26), channel_id=1, source_target_pairs={{1,0},{2,1},{3,2},{4,3},{5,4},{6,5},{7,6},{8,7},{9,8},{10,9},{11,1... | collective-permute-start | bytes 50696 | tf_op jit(solution)/shard_map/ppermute | solution.py:18
  21.3 0.1 slice.143
  21.4 0.8 slice.139
  22.1 1.4 broadcast_multiply_fusion
  23.5 0.1 compare_and_fusion
  23.6 0.6 compare_and_fusion.3
  24.2 0.7 fusion.56
  24.9 0.7 convert_reduce_fusion
  25.6 0.7 broadcast_multiply_fusion.1
  26.2 3.5 %constant_dynamic-update-slice_fusion.1 = bf16[1152,1280]{1,0:T(8,128)(2,1)} fusion(bf16[1152,1152]{1,0:T(8,128)(2,1)} %param.10), kind=kLoop, calls=%fused_computation.110 | loop fusion | bytes 5308416
  29.7 0.8 constant_dynamic-update-slice_fusion
  30.5 0.5 compare_and_fusion.1
  31.0 35.3 %collective-permute-done.1 = f32[33,128]{1,0:T(8,128)S(1)} collective-permute-done((f32[33,128]{1,0:T(8,128)S(1)}, f32[33,128]{1,0:T(8,128)S(1)}, u32[]{:S(2)}, u32[]{:S(2)}) %collective-permute-start.1) | collective-permute-done | bytes 16928 | tf_op jit(solution)/shard_map/ppermute | solution.py:18
  66.3 0.2 maximum_reduce_fusion
  66.5 0.1 copy.42
  66.6 0.1 reshape.110
  66.8 1.6 gather_fusion
  68.3 0.1 fusion.69
  68.5 0.9 fusion.32
  69.4 0.1 select_bitcast_fusion
  69.5 3.8 %all-to-all-done = f32[16,512,72]{1,2,0:T(8,128)} async-done(((f32[16,512,72]{1,2,0:T(8,128)}), f32[16,512,72]{1,2,0:T(8,128)}, u32[]{:S(2)}, u32[]{:S(2)}) %all-to-all-start) | async-done | bytes 2359328 | tf_op jit(solution)/shard_map/all_to_all | solution.py:117
  73.3 1.3 slice.184
  74.6 0.8 copy.46
  75.4 2.1 %collective-permute-start = (f32[8,1152]{1,0:T(8,128)}, f32[8,1152]{1,0:T(8,128)S(1)}, u32[]{:S(2)}, u32[]{:S(2)}) collective-permute-start(f32[8,1152]{1,0:T(8,128)} %copy.46), channel_id=1, source_target_pairs={{0,1},{1,2},{2,3},{3,4},{4,5},{5,6},{6,7},{7,8},{8,9},{9,10},{10,1... | collective-permute-start | bytes 110600 | tf_op jit(solution)/shard_map/ppermute | solution.py:24
  77.5 0.3 fusion.22
  77.9 0.9 mul.233
  78.8 3.0 %copy.41 = f32[512,1152]{1,0:T(8,128)} copy(f32[512,1152]{0,1:T(8,128)} %bitcast.2) | data formatting | bytes 4718592 | tf_op jit(solution)/shard_map/all_to_all | solution.py:117
  81.9 4.2 %collective-permute-done = f32[8,1152]{1,0:T(8,128)S(1)} collective-permute-done((f32[8,1152]{1,0:T(8,128)}, f32[8,1152]{1,0:T(8,128)S(1)}, u32[]{:S(2)}, u32[]{:S(2)}) %collective-permute-start) | collective-permute-done | bytes 36896 | tf_op jit(solution)/shard_map/ppermute | solution.py:24
  86.0 1.8 fusion.10
  87.9 0.0 copy-start.6
  88.0 5.4 %fusion.16 = f32[520,1280]{1,0:T(8,128)S(1)} fusion(bf16[1152,1280]{1,0:T(8,128)(2,1)} %constant_dynamic-update-slice_fusion, f32[8,1152]{1,0:T(8,128)S(1)} %collective-permute-done, f32[519,1152]{1,0:T(8,128)S(1)} %fusion.10, f32[512,1152]{1,0:T(8,128)S(1)} %copy-done.1, f32[1152]{0:T(1024)S(1)} %copy-done.11, f32[520]{0:T(1024)S(1)} %get-tuple-element.3, ...), kind=kOutput, calls=%fused_computation.27 | convolution fusion | flops 1540131840 | bytes 10419296 | tf_op jit(solution)/shard_map/dot_general | solution.py:43
  93.4 0.2 fusion.14
  93.7 0.1 fusion.44
  93.8 0.2 slice_reduce_fusion.1
  94.0 1.0 copy-done.10
  95.0 0.1 copy.43
  95.1 1.0 gather_fusion.1
  96.1 0.0 copy-done.15
  96.1 0.1 select_bitcast_fusion.1
  96.3 0.3 fusion.25
  96.6 8.3 %fusion.6 = f32[520,1152]{1,0:T(8,128)S(1)} fusion(bf16[1152,1152]{1,0:T(8,128)(2,1)S(1)} %copy-done, f32[520,1280]{1,0:T(8,128)} %copy-done.10, f32[520]{0:T(1024)S(1)} %copy-done.14, f32[519,1152]{1,0:T(8,128)} %copy-done.2, f32[1152]{0:T(1024)S(1)} %copy-done.11, f32[520]{0:T(1024)S(1)} %get-tuple-element.3, f32[1152]{0:T(1024)S(1)} %copy-done.12, ...), kind=kOutput, calls=%fused_computation.12 | convolution fusion | flops 1396961280 | bytes 17108992 | tf_op jit(solution)/shard_map/dot_general | solution.py:46
  104.9 0.0 copy-done.17
  105.0 4.3 %fusion.19 = f32[512,1280]{1,0:T(8,128)S(1)} fusion(bf16[1152,1280]{1,0:T(8,128)(2,1)} %constant_dynamic-update-slice_fusion, f32[520,1152]{1,0:T(8,128)S(1)} %fusion.6, f32[1152]{0:T(1024)S(1)} %copy-done.11, f32[512]{0:T(512)S(1)} %get-tuple-element.5, f32[1152]{0:T(1024)S(1)} %copy-done.12, f32[512]{0:T(512)S(1)} %get-tuple-element.4, ...), kind=kOutput, calls=%fused_computation.30 | convolution fusion | flops 1515847680 | bytes 10319872 | tf_op jit(solution)/shard_map/dot_general | solution.py:43
  109.3 1.5 copy-done.9
  110.8 4.3 %fusion.9 = f32[512,1152]{1,0:T(8,128)} fusion(bf16[1152,1152]{1,0:T(8,128)(2,1)S(1)} %copy-done, f32[512,1280]{1,0:T(8,128)S(1)} %fusion.19, f32[512]{0:T(512)S(1)} %copy-done.16, f32[520,1152]{1,0:T(8,128)S(1)} %fusion.6, f32[1152]{0:T(1024)S(1)} %copy-done.11, f32[512]{0:T(512)S(1)} %get-tuple-element.5, f32[1152]{0:T(1024)S(1)} %copy-done.12, ...), kind=kOutput, calls=%fused_computation.15 | convolution fusion | flops 1374289920 | bytes 16873472 | tf_op jit(solution)/shard_map/dot_general | solution.py:46
  115.1 3.2 %copy.44 = f32[512,1152]{0,1:T(8,128)} copy(f32[512,1152]{1,0:T(8,128)} %fusion.9) | data formatting | bytes 4718592 | tf_op jit(solution)/shard_map/add | solution.py:127
  118.3 4.9 %all-to-all-start.1 = ((f32[512,16,72]{0,2,1:T(8,128)}), f32[512,16,72]{0,2,1:T(8,128)}, u32[]{:S(2)}, u32[]{:S(2)}) async-start(f32[512,16,72]{0,2,1:T(8,128)} %bitcast.25), calls=%async_computation.1 | async-start | bytes 4718592 | tf_op jit(solution)/shard_map/all_to_all | solution.py:151
  123.2 0.4 collective-permute-start.2
  123.6 1.2 convolution_divide_fusion
  124.8 1.7 collective-permute-start.3
  126.5 54.7 %collective-permute-done.2 = f32[33,128]{1,0:T(8,128)S(1)} collective-permute-done((f32[33,128]{1,0:T(8,128)S(1)}, f32[33,128]{1,0:T(8,128)S(1)}, u32[]{:S(2)}, u32[]{:S(2)}) %collective-permute-start.2) | collective-permute-done | bytes 16928 | tf_op jit(solution)/shard_map/ppermute | solution.py:18
  181.2 0.1 maximum_select_fusion
  181.3 0.1 reshape.111
  181.4 0.1 fusion.68
  181.6 0.3 fusion.29
  181.8 0.1 mul.257
  181.9 0.0 collective-permute-done.3
  181.9 0.6 fusion.50
  182.6 0.7 all-to-all-done.1
  183.3 3.4 %copy.48 = f32[16,9,8,512]{3,2,0,1:T(8,128)} copy(f32[16,9,8,512]{3,2,1,0:T(8,128)} %bitcast.14) | data formatting | bytes 4718592 | tf_op jit(solution)/shard_map/all_to_all | solution.py:151
  (47 shorter events, 0.1 us)
Async XLA Ops:
  0.6 95.9 %copy-start = (bf16[1152,1152]{1,0:T(8,128)(2,1)S(1)}, bf16[1152,1152]{1,0:T(8,128)(2,1)}, u32[]{:S(2)}) copy-start(bf16[1152,1152]{1,0:T(8,128)(2,1)} %param.11) | copy-start | bytes 7962628
  4.1 9.4 %copy-start.5 = (f32[64,128]{1,0:T(8,128)S(1)}, f32[64,128]{1,0:T(8,128)}, u32[]{:S(2)}) copy-start(f32[64,128]{1,0:T(8,128)} %param.9) | copy-start | bytes 98308
  4.1 17.2 %copy-start.3 = (s32[131072]{0:T(1024)S(1)}, s32[131072]{0:T(1024)}, u32[]{:S(2)}) copy-start(s32[131072]{0:T(1024)} %param.14) | copy-start | bytes 1572868
  4.1 69.2 %all-to-all-start = ((f32[16,512,72]{1,2,0:T(8,128)}), f32[16,512,72]{1,2,0:T(8,128)}, u32[]{:S(2)}, u32[]{:S(2)}) async-start(f32[16,512,72]{1,2,0:T(8,128)} %bitcast.24), calls=%async_computation | async-start | bytes 4718592 | tf_op jit(solution)/shard_map/all_to_all | solution.py:117
  14.1 52.2 %collective-permute-start.1 = (f32[33,128]{1,0:T(8,128)S(1)}, f32[33,128]{1,0:T(8,128)S(1)}, u32[]{:S(2)}, u32[]{:S(2)}) collective-permute-start(f32[33,128]{1,0:T(8,128)S(1)} %get-tuple-element.26), channel_id=1, source_target_pairs={{1,0},{2,1},{3,2},{4,3},{5,4},{6,5},{7,6},{8,7},{9,8},{10,9},{11,1... | collective-permute-start | bytes 50696 | tf_op jit(solution)/shard_map/ppermute | solution.py:18
  26.2 3.5 %copy-start.4 = (bf16[1152,128]{1,0:T(8,128)(2,1)S(1)}, bf16[1152,128]{1,0:T(8,128)(2,1)}, u32[]{:S(2)}) copy-start(bf16[1152,128]{1,0:T(8,128)(2,1)} %param.12) | copy-start | bytes 884740
  66.3 7.0 %copy-start.7 = (f32[33,128]{1,0:T(8,128)}, f32[33,128]{1,0:T(8,128)S(1)}, u32[]{:S(2)}) copy-start(f32[33,128]{1,0:T(8,128)S(1)} %collective-permute-done.1) | copy-start | bytes 50692
  75.4 10.6 %collective-permute-start = (f32[8,1152]{1,0:T(8,128)}, f32[8,1152]{1,0:T(8,128)S(1)}, u32[]{:S(2)}, u32[]{:S(2)}) collective-permute-start(f32[8,1152]{1,0:T(8,128)} %copy.46), channel_id=1, source_target_pairs={{0,1},{1,2},{2,3},{3,4},{4,5},{5,6},{6,7},{7,8},{8,9},{9,10},{10,1... | collective-permute-start | bytes 110600 | tf_op jit(solution)/shard_map/ppermute | solution.py:24
  81.9 6.0 %copy-start.1 = (f32[512,1152]{1,0:T(8,128)S(1)}, f32[512,1152]{1,0:T(8,128)}, u32[]{:S(2)}) copy-start(f32[512,1152]{1,0:T(8,128)} %copy.41) | copy-start | bytes 7077892
  81.9 6.0 %copy-start.11 = (f32[1152]{0:T(1024)S(1)}, f32[1152]{0:T(1024)}, u32[]{:S(2)}) copy-start(f32[1152]{0:T(1024)} %get-tuple-element.31) | copy-start | bytes 13828
  81.9 6.0 %copy-start.12 = (f32[1152]{0:T(1024)S(1)}, f32[1152]{0:T(1024)}, u32[]{:S(2)}) copy-start(f32[1152]{0:T(1024)} %get-tuple-element.32) | copy-start | bytes 13828
  81.9 6.0 %copy-start.20 = (f32[1152]{0:T(1024)S(1)}, f32[1152]{0:T(1024)}, u32[]{:S(2)}) copy-start(f32[1152]{0:T(1024)} %param.13) | copy-start | bytes 13828
  87.9 5.5 %copy-start.2 = (f32[519,1152]{1,0:T(8,128)}, f32[519,1152]{1,0:T(8,128)S(1)}, u32[]{:S(2)}) copy-start(f32[519,1152]{1,0:T(8,128)S(1)} %fusion.10) | copy-start | bytes 7174660
  87.9 5.5 %copy-start.13 = (f32[64]{0:T(128)S(1)}, f32[64]{0:T(128)}, u32[]{:S(2)}) copy-start(f32[64]{0:T(128)} %convert_reduce_fusion) | copy-start | bytes 772
  87.9 5.8 %copy-start.6 = (f32[33,128]{1,0:T(8,128)S(1)}, f32[33,128]{1,0:T(8,128)}, u32[]{:S(2)}) copy-start(f32[33,128]{1,0:T(8,128)} %get-tuple-element.25) | copy-start | bytes 50692
  87.9 5.7 %copy-start.8 = (f32[33,128]{1,0:T(8,128)S(1)}, f32[33,128]{1,0:T(8,128)}, u32[]{:S(2)}) copy-start(f32[33,128]{1,0:T(8,128)} %copy-done.7) | copy-start | bytes 50692
  87.9 5.7 %copy-start.18 = (pred[64]{0:T(512)(128)(4,1)S(1)}, pred[64]{0:T(512)(128)(4,1)}, u32[]{:S(2)}) copy-start(pred[64]{0:T(512)(128)(4,1)} %get-tuple-element.33) | copy-start | bytes 196
  88.0 5.7 %copy-start.19 = (pred[64]{0:T(512)(128)(4,1)S(1)}, pred[64]{0:T(512)(128)(4,1)}, u32[]{:S(2)}) copy-start(pred[64]{0:T(512)(128)(4,1)} %get-tuple-element.34) | copy-start | bytes 196
  88.0 8.1 %copy-start.15 = (pred[512]{0:T(512)(128)(4,1)S(1)}, pred[512]{0:T(512)(128)(4,1)}, u32[]{:S(2)}) copy-start(pred[512]{0:T(512)(128)(4,1)} %get-tuple-element.10) | copy-start | bytes 1540
  88.0 8.6 %copy-start.14 = (f32[520]{0:T(1024)S(1)}, f32[520]{0:T(1024)}, u32[]{:S(2)}) copy-start(f32[520]{0:T(1024)} %get-tuple-element.12) | copy-start | bytes 6244
  93.4 1.5 copy-start.10
  96.6 8.4 %copy-start.17 = (f32[512]{0:T(512)S(1)}, f32[512]{0:T(512)}, u32[]{:S(2)}) copy-start(f32[512]{0:T(512)} %get-tuple-element.28) | copy-start | bytes 6148
  105.0 5.8 %copy-start.16 = (f32[512]{0:T(512)S(1)}, f32[512]{0:T(512)}, u32[]{:S(2)}) copy-start(f32[512]{0:T(512)} %get-tuple-element.27) | copy-start | bytes 6148
  109.3 1.5 copy-start.9
  118.3 65.0 %all-to-all-start.1 = ((f32[512,16,72]{0,2,1:T(8,128)}), f32[512,16,72]{0,2,1:T(8,128)}, u32[]{:S(2)}, u32[]{:S(2)}) async-start(f32[512,16,72]{0,2,1:T(8,128)} %bitcast.25), calls=%async_computation.1 | async-start | bytes 4718592 | tf_op jit(solution)/shard_map/all_to_all | solution.py:151
  123.2 58.1 %collective-permute-start.2 = (f32[33,128]{1,0:T(8,128)S(1)}, f32[33,128]{1,0:T(8,128)S(1)}, u32[]{:S(2)}, u32[]{:S(2)}) collective-permute-start(f32[33,128]{1,0:T(8,128)S(1)} %get-tuple-element.23), channel_id=1, source_target_pairs={{255,0},{0,1},{1,2},{2,3},{3,4},{4,5},{5,6},{6,7},{7,8},{8,9},{9,1... | collective-permute-start | bytes 50696 | tf_op jit(solution)/shard_map/ppermute | solution.py:18
  124.8 57.1 %collective-permute-start.3 = (f32[32,128]{1,0:T(8,128)S(1)}, f32[32,128]{1,0:T(8,128)S(1)}, u32[]{:S(2)}, u32[]{:S(2)}) collective-permute-start(f32[32,128]{1,0:T(8,128)S(1)} %get-tuple-element.21), channel_id=1, source_target_pairs={{255,0},{0,1},{1,2},{2,3},{3,4},{4,5},{5,6},{6,7},{7,8},{8,9},{9,1... | collective-permute-start | bytes 49160 | tf_op jit(solution)/shard_map/ppermute | solution.py:18
